TPU v7x, 512 devices: a whole 4x4x16 slice. The times are simulated.
512 devices in a mesh: vox: 128 (over z, y, core), ch: 4 (over x).
Axes of the slice: x: 4, y: 4, z: 16, core: 2. Of those that a mesh axis runs over, the one named last changes fastest.
Arguments:
- features: bfloat16 [131072, 128], P('vox'), may hold values from -6 to 6
- kernel: bfloat16 [27, 256, 128], P(None, 'ch'), may hold values from -0.1875 to 0.1875
- coarse_grad: bfloat16 [256, 65536], P('ch', 'vox'), may hold values from -6 to 6
- pair_fine: int32 [524288], P('vox'), may hold values from 0 to 1023
- pair_target: int32 [524288], P('vox'), may hold values from 0 to 511
- block_offset: int32 [4096], P('vox'), may hold values from 0 to 26
- target_owner: int32 [65536, 1], P('vox'), may hold values from 0 to 127; in each aligned block of 512 rows (0 to 511, 512 to 1023, ...) at most 6 rows name the same one
- slot_coarse_row: int32 [98304], P('vox'), may hold values from 0 to 511
- fine_count: int32 [128], P('vox'), may hold values from 512 to 1024, as said below
Outputs:
- activation: bfloat16 [256, 65536], P('ch', 'vox')
- grad_features: bfloat16 [128, 131072], P('ch', 'vox')
- grad_kernel: bfloat16 [27, 256, 128], P(None, 'ch')
Inputs may be any that keep to these rules, and one draw needn't show every extreme that they name: `target_owner`: among the 512 targets of one block no owner appears more than 6 times, and in some block one owner appears exactly 6 times. `fine_count`: some block has all 1024 fine voxels live.
All inputs are finite; a program needn't handle non-finite values.
Results may differ from a plain program's by a relative error of at most 0.0053.
Values may be sent and summed in bfloat16 or wider, within the bound.
No kernel may reach another device: no remote copies, remote signals or barrier semaphores. Data moves between devices by JAX's collectives and lax.ppermute only.
A program may use at most 64 MiB of HBM per device.

v0:
```python
import math

import jax
import jax.numpy as jnp
from jax import lax
from jax.sharding import PartitionSpec as P


def owner_slots(owner_of, owners):
    labels = jnp.arange(owners, dtype=jnp.int32)
    onehot = (owner_of[:, None] == labels[None, :]).astype(jnp.int32)
    before = jnp.cumsum(onehot, axis=0) - onehot
    return jnp.sum(before * onehot, axis=1)


def body(
    features,
    kernel,
    coarse_grad,
    pair_fine,
    pair_target,
    block_offset,
    target_owner,
    slot_coarse_row,
    fine_count,
):
    owners = lax.axis_size("vox")
    fine_total, width_in = features.shape
    width_out, coarse_total = coarse_grad.shape
    offsets_all = kernel.shape[0]
    targets = target_owner.shape[0]
    capacity = slot_coarse_row.shape[0] // owners
    blocks = block_offset.shape[0]
    rows_each_turn = min(16, blocks)
    rounds = blocks // rows_each_turn
    live_mask = jnp.arange(fine_total, dtype=jnp.int32) < fine_count[0]
    masked = jnp.where(live_mask[:, None], features, jnp.zeros((), features.dtype))
    fine_ids = pair_fine.reshape(rounds, rows_each_turn, 128)
    target_ids = pair_target.reshape(rounds, rows_each_turn, 128)
    offset_ids = block_offset.reshape(rounds, rows_each_turn)

    def forward_step(totals, pieces):
        fine_at, target_at, offset_at = pieces
        gathered = masked[fine_at]
        partial_value = jnp.einsum(
            "gpc,goc->gpo", gathered, kernel[offset_at], preferred_element_type=jnp.float32
        )
        return (totals.at[target_at.reshape(-1)].add(partial_value.reshape(-1, width_out)), None)

    target_sum, leftover = lax.scan(
        forward_step,
        jnp.zeros((targets, width_out), jnp.float32),
        (fine_ids, target_ids, offset_ids),
    )
    target_part = target_sum.astype(jnp.bfloat16)
    owner_of = target_owner[:, 0]
    slot_index = owner_of * capacity + owner_slots(owner_of, owners)
    send_rows = (
        jnp.zeros((owners * capacity, width_out), jnp.bfloat16).at[slot_index].set(target_part)
    )
    as_lanes = capacity * width_out % 128 == 0
    lane_shape = (owners * capacity * width_out // 128, 128)
    received = lax.all_to_all(
        send_rows.reshape(lane_shape), "vox", split_axis=0, concat_axis=0, tiled=True
    )
    got_rows = received.reshape(owners * capacity, width_out).astype(jnp.float32)
    coarse = jax.ops.segment_sum(got_rows, slot_coarse_row, coarse_total)
    gate_output = jax.nn.sigmoid(coarse)
    activation = (coarse * gate_output).astype(jnp.bfloat16)
    grad_coarse = (
        coarse_grad.astype(jnp.float32).T * gate_output * (1.0 + coarse * (1.0 - gate_output))
    ).astype(jnp.bfloat16)
    back_rows = grad_coarse[slot_coarse_row]
    returned = lax.all_to_all(
        back_rows.reshape(lane_shape), "vox", split_axis=0, concat_axis=0, tiled=True
    )
    grad_target = returned.reshape(owners * capacity, width_out)[slot_index]
    weight_init = jnp.zeros((offsets_all, width_out, width_in), jnp.float32)

    def reverse_update(state_pair, pieces):
        fine_sum, weight_sum = state_pair
        fine_at, target_at, offset_at = pieces
        gathered = masked[fine_at]
        grad_rows = grad_target[target_at]
        grad_in = jnp.einsum(
            "gpo,goc->gpc", grad_rows, kernel[offset_at], preferred_element_type=jnp.float32
        )
        fine_sum = fine_sum.at[fine_at.reshape(-1)].add(grad_in.reshape(-1, width_in))
        grad_weight = jnp.einsum(
            "gpc,gpo->goc", gathered, grad_rows, preferred_element_type=jnp.float32
        )
        return ((fine_sum, weight_sum.at[offset_at].add(grad_weight)), None)

    (fine_sum, weight_sum), leftover = lax.scan(
        reverse_update,
        (jnp.zeros((fine_total, width_in), jnp.float32), weight_init),
        (fine_ids, target_ids, offset_ids),
    )
    fine_grad = lax.psum_scatter(fine_sum, "ch", scatter_dimension=1, tiled=True)
    grad_features = jnp.where(live_mask[:, None], fine_grad, jnp.zeros((), jnp.float32)).astype(
        jnp.bfloat16
    )
    weight_total = lax.psum(weight_sum, "vox")
    factor = math.sqrt(offsets_all / (blocks * 128 * owners))
    grad_kernel = (weight_total * factor).astype(jnp.bfloat16)
    return (activation.T, grad_features.T, grad_kernel)


def solution(mesh):
    in_specs = (
        P("vox", None),
        P(None, "ch", None),
        P("ch", "vox"),
        P("vox"),
        P("vox"),
        P("vox"),
        P("vox", None),
        P("vox"),
        P("vox"),
    )
    out_specs = (P("ch", "vox"), P("ch", "vox"), P(None, "ch", None))
    return jax.shard_map(body, mesh=mesh, in_specs=in_specs, out_specs=out_specs, check_vma=False)
```

profile of v0, /device:TPU:1, one launch (start us, length us, event | category | flops | bytes accessed | tf_op | source)
XLA Modules:
  0.0 524.8 jit_solution(3688180290305853097)
XLA Ops:
  8.7 0.6 copy-done.8
  9.4 1.1 broadcast_select_fusion
  10.6 0.7 copy-done.3
  11.3 39.6 %while.22 = (s32[]{:T(128)}, f32[512,64]{1,0:T(8,128)S(1)}, s32[2,16,128]{2,1,0:T(8,128)S(1)}, s32[2,16,128]{2,1,0:T(8,128)S(1)}, bf16[1024,128]{1,0:T(8,128)(2,...) while((s32[]{:T(128)}, f32[512,64]{1,0:T(8,128)S(1)}, ...), condition=%wide.region_5.6_spmd, body=%wide.region_3.5_spmd.sunk | while | flops 33700912 | bytes 4526433 | solution.py:50
  11.3 6.2 %gather_fusion = bf16[2048,128]{1,0:T(8,128)(2,1)S(1)} fusion(bf16[1024,128]{1,0:T(8,128)(2,1)S(1)} %get-tuple-element.268, s32[2048]{0:T(1024)S(1)} %fusion.48), kind=kCustom, calls=%fused_computation.clone.1 | custom fusion | bytes 1056768 | tf_op jit(solution)/shard_map/while/body/eval_jaxpr/gather | solution.py:44
  17.5 1.6 gather_fusion.1
  19.1 0.3 fusion.50
  19.5 11.6 %scatter_fusion = f32[512,64]{1,0:T(8,128)S(1)} fusion(f32[512,64]{1,0:T(8,128)S(1)} %get-tuple-element.257, s32[2048]{0:T(1024)S(1)} %bitcast.134, f32[2048,64]{1,0:T(8,128)S(1)} %bitcast.128), kind=kCustom, calls=%fused_computation.7.clone.1 | custom fusion | flops 131072 | bytes 1581056 | tf_op jit(solution)/shard_map/while/body/eval_jaxpr/scatter-add | solution.py:48
  31.1 6.2 %gather_fusion = bf16[2048,128]{1,0:T(8,128)(2,1)S(1)} fusion(bf16[1024,128]{1,0:T(8,128)(2,1)S(1)} %get-tuple-element.268, s32[2048]{0:T(1024)S(1)} %fusion.48), kind=kCustom, calls=%fused_computation.clone.1 | custom fusion | bytes 1056768 | tf_op jit(solution)/shard_map/while/body/eval_jaxpr/gather | solution.py:44
  37.3 1.6 gather_fusion.1
  38.9 0.3 fusion.50
  39.3 11.6 %scatter_fusion = f32[512,64]{1,0:T(8,128)S(1)} fusion(f32[512,64]{1,0:T(8,128)S(1)} %get-tuple-element.257, s32[2048]{0:T(1024)S(1)} %bitcast.134, f32[2048,64]{1,0:T(8,128)S(1)} %bitcast.128), kind=kCustom, calls=%fused_computation.7.clone.1 | custom fusion | flops 131072 | bytes 1581056 | tf_op jit(solution)/shard_map/while/body/eval_jaxpr/scatter-add | solution.py:48
  51.0 0.2 fusion.12
  51.3 0.2 fusion.11
  51.6 1.8 scatter_custom_fusion.3
  53.4 0.8 all_to_all.12
  54.2 20.7 %all-to-all-start = ((bf16[128,3,128]{2,1,0:T(4,128)(2,1)}), bf16[128,3,128]{2,1,0:T(4,128)(2,1)S(1)}, u32[]{:S(2)}, u32[]{:S(2)}) async-start(bf16[128,3,128]{2,1,0:T(4,128)(2,1)} %all_to_all.12), calls=%async_computation | async-start | bytes 262144 | tf_op jit(solution)/shard_map/all_to_all | solution.py:63
  74.9 16.0 %all-to-all-done = bf16[128,3,128]{2,1,0:T(4,128)(2,1)S(1)} async-done(((bf16[128,3,128]{2,1,0:T(4,128)(2,1)}), bf16[128,3,128]{2,1,0:T(4,128)(2,1)S(1)}, u32[]{:S(2)}, u32[]{:S(2)}) %all-to-all-start) | async-done | bytes 98336 | tf_op jit(solution)/shard_map/all_to_all | solution.py:63
  91.1 6.1 %scatter_custom_fusion.4 = f32[512,64]{1,0:T(8,128)S(1)} fusion(s32[768]{0:T(1024)S(1)} %copy-done.7, f32[768,64]{1,0:T(8,128)S(1)} %reshape.360, f32[]{:T(128)} %constant.32.clone.1), kind=kCustom, calls=%fused_computation.54 | custom fusion | flops 49152 | bytes 131076 | tf_op jit(solution)/shard_map/scatter-add | solution.py:67
  97.3 0.7 copy-done.5
  98.1 0.7 fusion.15
  98.9 1.9 gather_fusion.5
  100.8 0.8 all_to_all.14
  101.6 7.2 %all-to-all-start.1 = ((bf16[128,3,128]{2,1,0:T(4,128)(2,1)}), bf16[128,3,128]{2,1,0:T(4,128)(2,1)S(1)}, u32[]{:S(2)}, u32[]{:S(2)}) async-start(bf16[128,3,128]{2,1,0:T(4,128)(2,1)} %all_to_all.14), calls=%async_computation.1 | async-start | bytes 262144 | tf_op jit(solution)/shard_map/all_to_all | solution.py:74
  108.8 16.0 %all-to-all-done.1 = bf16[128,3,128]{2,1,0:T(4,128)(2,1)S(1)} async-done(((bf16[128,3,128]{2,1,0:T(4,128)(2,1)}), bf16[128,3,128]{2,1,0:T(4,128)(2,1)S(1)}, u32[]{:S(2)}, u32[]{:S(2)}) %all-to-all-start.1) | async-done | bytes 98336 | tf_op jit(solution)/shard_map/all_to_all | solution.py:74
  125.0 1.3 gather_fusion.6
  126.4 57.3 %while.23 = (s32[]{:T(128)}, f32[1024,128]{1,0:T(8,128)S(1)}, f32[27,64,128]{2,1,0:T(8,128)S(1)}, s32[2,16,128]{2,1,0:T(8,128)S(1)}, s32[2,16,128]{2,1,0:T(8,128...) while((s32[]{:T(128)}, f32[1024,128]{1,0:T(8,128)S(1)}, ...), condition=%wide.region_11.12_spmd, body=%wide.region_8.11_spmd.sunk | while | flops 67525680 | bytes 16863716 | solution.py:94
  126.5 6.2 %gather_fusion.2 = bf16[2048,64]{1,0:T(8,128)(2,1)S(1)} fusion(bf16[512,64]{1,0:T(8,128)(2,1)S(1)} %get-tuple-element.297, s32[2048]{0:T(1024)S(1)} %get-tuple-element.246), kind=kCustom, calls=%fused_computation.2.clone.1 | custom fusion | bytes 532480 | tf_op jit(solution)/shard_map/while/body/eval_jaxpr/gather | solution.py:84
  132.7 6.2 %gather_fusion.4 = bf16[2048,128]{1,0:T(8,128)(2,1)S(1)} fusion(bf16[1024,128]{1,0:T(8,128)(2,1)S(1)} %get-tuple-element.300, s32[2048]{0:T(1024)S(1)} %get-tuple-element.247), kind=kCustom, calls=%fused_computation.4.clone.1 | custom fusion | bytes 1056768 | tf_op jit(solution)/shard_map/while/body/eval_jaxpr/gather | solution.py:83
  138.9 0.3 fusion.58
  139.2 1.3 scatter_fusion.2
  140.6 0.9 copy-done
  141.5 1.6 gather_fusion.3
  143.1 0.3 fusion.57
  143.4 11.7 %scatter_fusion.1 = f32[1024,128]{1,0:T(8,128)S(1)} fusion(f32[1024,128]{1,0:T(8,128)S(1)} %get-tuple-element.283, s32[2048]{0:T(1024)S(1)} %bitcast.135, f32[2048,128]{1,0:T(8,128)S(1)} %bitcast.129), kind=kCustom, calls=%fused_computation.8.clone.1 | custom fusion | flops 262144 | bytes 3153920 | tf_op jit(solution)/shard_map/while/body/eval_jaxpr/scatter-add | solution.py:88
  155.1 6.2 %gather_fusion.2 = bf16[2048,64]{1,0:T(8,128)(2,1)S(1)} fusion(bf16[512,64]{1,0:T(8,128)(2,1)S(1)} %get-tuple-element.297, s32[2048]{0:T(1024)S(1)} %get-tuple-element.246), kind=kCustom, calls=%fused_computation.2.clone.1 | custom fusion | bytes 532480 | tf_op jit(solution)/shard_map/while/body/eval_jaxpr/gather | solution.py:84
  161.3 6.2 %gather_fusion.4 = bf16[2048,128]{1,0:T(8,128)(2,1)S(1)} fusion(bf16[1024,128]{1,0:T(8,128)(2,1)S(1)} %get-tuple-element.300, s32[2048]{0:T(1024)S(1)} %get-tuple-element.247), kind=kCustom, calls=%fused_computation.4.clone.1 | custom fusion | bytes 1056768 | tf_op jit(solution)/shard_map/while/body/eval_jaxpr/gather | solution.py:83
  167.5 0.3 fusion.58
  167.9 1.3 scatter_fusion.2
  169.2 0.9 copy-done
  170.1 1.6 gather_fusion.3
  171.7 0.3 fusion.57
  172.0 11.7 %scatter_fusion.1 = f32[1024,128]{1,0:T(8,128)S(1)} fusion(f32[1024,128]{1,0:T(8,128)S(1)} %get-tuple-element.283, s32[2048]{0:T(1024)S(1)} %bitcast.135, f32[2048,128]{1,0:T(8,128)S(1)} %bitcast.129), kind=kCustom, calls=%fused_computation.8.clone.1 | custom fusion | flops 262144 | bytes 3153920 | tf_op jit(solution)/shard_map/while/body/eval_jaxpr/scatter-add | solution.py:88
  183.8 0.9 copy-done.2
  184.8 1.0 copy.55
  185.8 328.0 %all-reduce.2.cloned.1.call-done = f32[27,64,128]{2,1,0:T(8,128)} async-done(((f32[27,64,128]{2,1,0:T(8,128)}), f32[27,64,128]{2,1,0:T(8,128)}) %all-reduce.2.cloned.1.call-update) | async-done | bytes 884752 | tf_op jit(solution)/shard_map/psum | solution.py:103
  513.8 2.1 multiply_convert_fusion
  515.8 1.5 fusion.22
  (59 shorter events, 1.3 us)
Async XLA Ops:
  8.7 0.7 copy-start.8
  10.6 0.7 copy-start.3
  10.6 0.7 copy-start.4
  11.3 39.6 %copy-start.6 = (s32[512,1]{0,1:T(1,128)S(1)}, s32[512,1]{0,1:T(1,128)}, u32[]{:S(2)}) copy-start(s32[512,1]{0,1:T(1,128)} %param.19) | copy-start | bytes 6148
  54.2 20.7 %copy-start.7 = (s32[768]{0:T(1024)S(1)}, s32[768]{0:T(1024)}, u32[]{:S(2)}) copy-start(s32[768]{0:T(1024)} %param.20) | copy-start | bytes 9220
  54.2 36.8 %all-to-all-start = ((bf16[128,3,128]{2,1,0:T(4,128)(2,1)}), bf16[128,3,128]{2,1,0:T(4,128)(2,1)S(1)}, u32[]{:S(2)}, u32[]{:S(2)}) async-start(bf16[128,3,128]{2,1,0:T(4,128)(2,1)} %all_to_all.12), calls=%async_computation | async-start | bytes 262144 | tf_op jit(solution)/shard_map/all_to_all | solution.py:63
  97.2 0.8 copy-start.5
  101.6 23.2 %all-to-all-start.1 = ((bf16[128,3,128]{2,1,0:T(4,128)(2,1)}), bf16[128,3,128]{2,1,0:T(4,128)(2,1)S(1)}, u32[]{:S(2)}, u32[]{:S(2)}) async-start(bf16[128,3,128]{2,1,0:T(4,128)(2,1)} %all_to_all.14), calls=%async_computation.1 | async-start | bytes 262144 | tf_op jit(solution)/shard_map/all_to_all | solution.py:74
  108.8 405.0 %all-reduce.2.cloned.1.call-start = ((), (), s32[]{:S(2)}) async-start(), calls=%async_computation.4 | async-start | bytes 1769472 | tf_op jit(solution)/shard_map/psum | solution.py:103
  140.5 0.9 copy-start
  143.4 11.7 %copy-start.1 = (f32[27,64,128]{2,1,0:T(8,128)S(1)}, f32[27,64,128]{2,1,0:T(8,128)}, u32[]{:S(2)}) copy-start(f32[27,64,128]{2,1,0:T(8,128)} %copy-done) | copy-start | bytes 2654212 | tf_op jit(solution)/shard_map/while
  169.2 0.9 copy-start
  172.0 11.7 %copy-start.1 = (f32[27,64,128]{2,1,0:T(8,128)S(1)}, f32[27,64,128]{2,1,0:T(8,128)}, u32[]{:S(2)}) copy-start(f32[27,64,128]{2,1,0:T(8,128)} %copy-done) | copy-start | bytes 2654212 | tf_op jit(solution)/shard_map/while
  183.8 0.9 copy-start.2
  184.7 331.1 %reduce-scatter.2.cloned.1.call-start = ((), (), s32[]{:S(2)}) async-start(), calls=%async_computation.3 | async-start | bytes 655360 | tf_op jit(solution)/shard_map/reduce_scatter | solution.py:99
Sparse Core Ops, SparseCore 0:
  184.8 328.8 all-reduce.1
Sparse Core Ops, SparseCore 1:
  188.0 18.9 reduce-scatter.1
where the time goes:
time: 525 us
  waiting for transfers between devices  360 us (69%)
  other arithmetic  63.2 us (12%)
  local copies, waits for them, and re-layouts  55.1 us (10%)
  starting transfers between devices  27.9 us (5%)
  between operations  16.4 us (3%)
    psum x1, waiting for transfers between devices, body(): weight_total = lax.psum(weight_sum, 'vox')  328 us
    scatter-add x2, other arithmetic, reverse_update(): fine_sum.at[fine_at.reshape(-1)].add(grad_in.reshape(-1, width_in))  23.4 us
    scatter-add x2, other arithmetic, forward_step(): totals.at[target_at.reshape(-1)].add(partial_value.reshape(-1, width_out))  23.2 us
    all_to_all x1, starting transfers between devices, body(): lax.all_to_all(send_rows.reshape(lane_shape), 'vox', split_axis=0, concat...  20.7 us
    all_to_all x1, waiting for transfers between devices, body(): lax.all_to_all(send_rows.reshape(lane_shape), 'vox', split_axis=0, concat...  16 us
    all_to_all x1, waiting for transfers between devices, body(): lax.all_to_all(back_rows.reshape(lane_shape), 'vox', split_axis=0, concat...  16 us
    gather x2, local copies, waits for them, and re-layouts, reverse_update(): gathered = masked[fine_at]  12.4 us
    gather x2, local copies, waits for them, and re-layouts, reverse_update(): grad_rows = grad_target[target_at]  12.4 us
  transfers between devices with their start and end apart: 4, of which 3 were waited for; matrix products, arithmetic and copies ran while one was open for 1% of the time, Pallas kernels for 0%

commit v1 on v0

--- a/solution.py
+++ b/solution.py
@@ -11,6 +11,18 @@
     onehot = (owner_of[:, None] == labels[None, :]).astype(jnp.int32)
     before = jnp.cumsum(onehot, axis=0) - onehot
     return jnp.sum(before * onehot, axis=1)
+
+
+def reduce_replicate(weight_sum, owners, factor):
+    shape = weight_sum.shape
+    rows = weight_sum.size // 128
+    chunk = -(-rows // owners)
+    flat = jnp.pad(weight_sum.reshape(rows, 128), ((0, chunk * owners - rows), (0, 0)))
+    got = lax.all_to_all(flat, "vox", 0, 0, tiled=True)
+    mine = (got.reshape(owners, chunk, 128).sum(axis=0) * factor).astype(jnp.bfloat16)
+    spread = jnp.broadcast_to(mine[None], (owners, chunk, 128)).reshape(owners * chunk, 128)
+    back = lax.all_to_all(spread, "vox", 0, 0, tiled=True)
+    return back[:rows].reshape(shape)
 
 
 def body(
@@ -100,9 +112,8 @@
     grad_features = jnp.where(live_mask[:, None], fine_grad, jnp.zeros((), jnp.float32)).astype(
         jnp.bfloat16
     )
-    weight_total = lax.psum(weight_sum, "vox")
     factor = math.sqrt(offsets_all / (blocks * 128 * owners))
-    grad_kernel = (weight_total * factor).astype(jnp.bfloat16)
+    grad_kernel = reduce_replicate(weight_sum, owners, factor)
     return (activation.T, grad_features.T, grad_kernel)
 
 

time: 525 us -> 298 us (0.57)
  waiting for transfers between devices: 360 us -> 63.1 us
  blocking collectives: 0 us -> 58.8 us
  starting transfers between devices: 27.9 us -> 38.1 us
    psum x1 -> x0, waiting for transfers between devices: 328 us -> none  [body(): weight_total = lax.psum(weight_sum, 'vox')]
    all_to_all x0 -> x1, blocking collectives: none -> 58.8 us  [reduce_replicate(): got = lax.all_to_all(flat, 'vox', 0, 0, tiled=True)]
    reduce_scatter x1, waiting for transfers between devices: 0.01 us -> 31 us  [body(): lax.psum_scatter(fine_sum, 'ch', scatter_dimension=1, tiled=True)]
    all_to_all x0 -> x1, starting transfers between devices: none -> 10.2 us  [reduce_replicate(): back = lax.all_to_all(spread, 'vox', 0, 0, tiled=True)]
where the time goes in v1:
time: 298 us; the launch traced here: 297 us
  waiting for transfers between devices  63.1 us (21%)
  other arithmetic  61.3 us (21%)
  blocking collectives  58.8 us (20%)
  local copies, waits for them, and re-layouts  58.3 us (20%)
  starting transfers between devices  38.1 us (13%)
  between operations  14.9 us (5%)
    all_to_all x1, blocking collectives, reduce_replicate(): got = lax.all_to_all(flat, 'vox', 0, 0, tiled=True)  58.8 us
    reduce_scatter x1, waiting for transfers between devices, body(): lax.psum_scatter(fine_sum, 'ch', scatter_dimension=1, tiled=True)  31 us
    scatter-add x2, other arithmetic, reverse_update(): fine_sum.at[fine_at.reshape(-1)].add(grad_in.reshape(-1, width_in))  23.4 us
    scatter-add x2, other arithmetic, forward_step(): totals.at[target_at.reshape(-1)].add(partial_value.reshape(-1, width_out))  23.2 us
    all_to_all x1, starting transfers between devices, body(): lax.all_to_all(send_rows.reshape(lane_shape), 'vox', split_axis=0, concat...  20.7 us
    all_to_all x1, waiting for transfers between devices, body(): lax.all_to_all(back_rows.reshape(lane_shape), 'vox', split_axis=0, concat...  16 us
    all_to_all x1, waiting for transfers between devices, body(): lax.all_to_all(send_rows.reshape(lane_shape), 'vox', split_axis=0, concat...  16 us
    gather x2, local copies, waits for them, and re-layouts, reverse_update(): gathered = masked[fine_at]  12.4 us
  transfers between devices with their start and end apart: 4, of which 3 were waited for; matrix products, arithmetic and copies ran while one was open for 1% of the time, Pallas kernels for 0%

profile of v1, /device:TPU:1, one launch (start us, length us, event | category | flops | bytes accessed | tf_op | source)
XLA Modules:
  0.0 296.6 jit_solution(4174528889327717299)
XLA Ops:
  7.8 0.6 copy-done.7
  8.6 1.1 broadcast_select_fusion
  9.8 0.7 copy-done.2
  10.5 39.6 %while.22 = (s32[]{:T(128)}, f32[512,64]{1,0:T(8,128)S(1)}, s32[2,16,128]{2,1,0:T(8,128)S(1)}, s32[2,16,128]{2,1,0:T(8,128)S(1)}, bf16[1024,128]{1,0:T(8,128)(2,...) while((s32[]{:T(128)}, f32[512,64]{1,0:T(8,128)S(1)}, ...), condition=%wide.region_5.6_spmd, body=%wide.region_3.5_spmd.sunk | while | flops 33700912 | bytes 4526433 | solution.py:62
  10.5 6.2 %gather_fusion = bf16[2048,128]{1,0:T(8,128)(2,1)S(1)} fusion(bf16[1024,128]{1,0:T(8,128)(2,1)S(1)} %get-tuple-element.268, s32[2048]{0:T(1024)S(1)} %fusion.48), kind=kCustom, calls=%fused_computation.clone.1 | custom fusion | bytes 1056768 | tf_op jit(solution)/shard_map/while/body/eval_jaxpr/gather | solution.py:56
  16.7 1.6 gather_fusion.1
  18.3 0.3 fusion.50
  18.6 11.6 %scatter_fusion = f32[512,64]{1,0:T(8,128)S(1)} fusion(f32[512,64]{1,0:T(8,128)S(1)} %get-tuple-element.257, s32[2048]{0:T(1024)S(1)} %bitcast.137, f32[2048,64]{1,0:T(8,128)S(1)} %bitcast.130), kind=kCustom, calls=%fused_computation.7.clone.1 | custom fusion | flops 131072 | bytes 1581056 | tf_op jit(solution)/shard_map/while/body/eval_jaxpr/scatter-add | solution.py:60
  30.3 6.2 %gather_fusion = bf16[2048,128]{1,0:T(8,128)(2,1)S(1)} fusion(bf16[1024,128]{1,0:T(8,128)(2,1)S(1)} %get-tuple-element.268, s32[2048]{0:T(1024)S(1)} %fusion.48), kind=kCustom, calls=%fused_computation.clone.1 | custom fusion | bytes 1056768 | tf_op jit(solution)/shard_map/while/body/eval_jaxpr/gather | solution.py:56
  36.5 1.6 gather_fusion.1
  38.1 0.3 fusion.50
  38.4 11.6 %scatter_fusion = f32[512,64]{1,0:T(8,128)S(1)} fusion(f32[512,64]{1,0:T(8,128)S(1)} %get-tuple-element.257, s32[2048]{0:T(1024)S(1)} %bitcast.137, f32[2048,64]{1,0:T(8,128)S(1)} %bitcast.130), kind=kCustom, calls=%fused_computation.7.clone.1 | custom fusion | flops 131072 | bytes 1581056 | tf_op jit(solution)/shard_map/while/body/eval_jaxpr/scatter-add | solution.py:60
  50.7 1.8 scatter_custom_fusion.3
  52.5 0.8 all_to_all.24
  53.4 20.7 %all-to-all-start = ((bf16[128,3,128]{2,1,0:T(4,128)(2,1)}), bf16[128,3,128]{2,1,0:T(4,128)(2,1)S(1)}, u32[]{:S(2)}, u32[]{:S(2)}) async-start(bf16[128,3,128]{2,1,0:T(4,128)(2,1)} %all_to_all.24), calls=%async_computation | async-start | bytes 262144 | tf_op jit(solution)/shard_map/all_to_all | solution.py:75
  74.1 16.0 %all-to-all-done = bf16[128,3,128]{2,1,0:T(4,128)(2,1)S(1)} async-done(((bf16[128,3,128]{2,1,0:T(4,128)(2,1)}), bf16[128,3,128]{2,1,0:T(4,128)(2,1)S(1)}, u32[]{:S(2)}, u32[]{:S(2)}) %all-to-all-start) | async-done | bytes 98336 | tf_op jit(solution)/shard_map/all_to_all | solution.py:75
  90.3 6.1 %scatter_custom_fusion.4 = f32[512,64]{1,0:T(8,128)S(1)} fusion(s32[768]{0:T(1024)S(1)} %copy-done.6, f32[768,64]{1,0:T(8,128)S(1)} %reshape.380, f32[]{:T(128)} %constant.32.clone.1), kind=kCustom, calls=%fused_computation.53 | custom fusion | flops 49152 | bytes 131076 | tf_op jit(solution)/shard_map/scatter-add | solution.py:79
  96.5 0.7 copy-done.4
  97.2 0.7 fusion.15
  98.0 1.9 gather_fusion.5
  99.9 0.8 all_to_all.26
  100.7 7.2 %all-to-all-start.1 = ((bf16[128,3,128]{2,1,0:T(4,128)(2,1)}), bf16[128,3,128]{2,1,0:T(4,128)(2,1)S(1)}, u32[]{:S(2)}, u32[]{:S(2)}) async-start(bf16[128,3,128]{2,1,0:T(4,128)(2,1)} %all_to_all.26), calls=%async_computation.1 | async-start | bytes 262144 | tf_op jit(solution)/shard_map/all_to_all | solution.py:86
  107.9 16.0 %all-to-all-done.1 = bf16[128,3,128]{2,1,0:T(4,128)(2,1)S(1)} async-done(((bf16[128,3,128]{2,1,0:T(4,128)(2,1)}), bf16[128,3,128]{2,1,0:T(4,128)(2,1)S(1)}, u32[]{:S(2)}, u32[]{:S(2)}) %all-to-all-start.1) | async-done | bytes 98336 | tf_op jit(solution)/shard_map/all_to_all | solution.py:86
  124.1 1.3 gather_fusion.6
  125.6 57.3 %while.23 = (s32[]{:T(128)}, f32[1024,128]{1,0:T(8,128)S(1)}, f32[27,64,128]{2,1,0:T(8,128)S(1)}, s32[2,16,128]{2,1,0:T(8,128)S(1)}, s32[2,16,128]{2,1,0:T(8,128...) while((s32[]{:T(128)}, f32[1024,128]{1,0:T(8,128)S(1)}, ...), condition=%wide.region_11.12_spmd, body=%wide.region_8.11_spmd.sunk | while | flops 67525680 | bytes 16863716 | solution.py:106
  125.6 6.2 %gather_fusion.2 = bf16[2048,64]{1,0:T(8,128)(2,1)S(1)} fusion(bf16[512,64]{1,0:T(8,128)(2,1)S(1)} %get-tuple-element.297, s32[2048]{0:T(1024)S(1)} %get-tuple-element.246), kind=kCustom, calls=%fused_computation.2.clone.1 | custom fusion | bytes 532480 | tf_op jit(solution)/shard_map/while/body/eval_jaxpr/gather | solution.py:96
  131.8 6.2 %gather_fusion.4 = bf16[2048,128]{1,0:T(8,128)(2,1)S(1)} fusion(bf16[1024,128]{1,0:T(8,128)(2,1)S(1)} %get-tuple-element.300, s32[2048]{0:T(1024)S(1)} %get-tuple-element.247), kind=kCustom, calls=%fused_computation.4.clone.1 | custom fusion | bytes 1056768 | tf_op jit(solution)/shard_map/while/body/eval_jaxpr/gather | solution.py:95
  138.0 0.3 fusion.58
  138.4 1.3 scatter_fusion.2
  139.7 0.9 copy-done
  140.6 1.6 gather_fusion.3
  142.5 11.7 %scatter_fusion.1 = f32[1024,128]{1,0:T(8,128)S(1)} fusion(f32[1024,128]{1,0:T(8,128)S(1)} %get-tuple-element.283, s32[2048]{0:T(1024)S(1)} %bitcast.138, f32[2048,128]{1,0:T(8,128)S(1)} %bitcast.131), kind=kCustom, calls=%fused_computation.8.clone.1 | custom fusion | flops 262144 | bytes 3153920 | tf_op jit(solution)/shard_map/while/body/eval_jaxpr/scatter-add | solution.py:100
  154.3 6.2 %gather_fusion.2 = bf16[2048,64]{1,0:T(8,128)(2,1)S(1)} fusion(bf16[512,64]{1,0:T(8,128)(2,1)S(1)} %get-tuple-element.297, s32[2048]{0:T(1024)S(1)} %get-tuple-element.246), kind=kCustom, calls=%fused_computation.2.clone.1 | custom fusion | bytes 532480 | tf_op jit(solution)/shard_map/while/body/eval_jaxpr/gather | solution.py:96
  160.5 6.2 %gather_fusion.4 = bf16[2048,128]{1,0:T(8,128)(2,1)S(1)} fusion(bf16[1024,128]{1,0:T(8,128)(2,1)S(1)} %get-tuple-element.300, s32[2048]{0:T(1024)S(1)} %get-tuple-element.247), kind=kCustom, calls=%fused_computation.4.clone.1 | custom fusion | bytes 1056768 | tf_op jit(solution)/shard_map/while/body/eval_jaxpr/gather | solution.py:95
  166.7 0.3 fusion.58
  167.0 1.3 scatter_fusion.2
  168.4 0.9 copy-done
  169.3 1.6 gather_fusion.3
  171.2 11.7 %scatter_fusion.1 = f32[1024,128]{1,0:T(8,128)S(1)} fusion(f32[1024,128]{1,0:T(8,128)S(1)} %get-tuple-element.283, s32[2048]{0:T(1024)S(1)} %bitcast.138, f32[2048,128]{1,0:T(8,128)S(1)} %bitcast.131), kind=kCustom, calls=%fused_computation.8.clone.1 | custom fusion | flops 262144 | bytes 3153920 | tf_op jit(solution)/shard_map/while/body/eval_jaxpr/scatter-add | solution.py:100
  182.9 1.0 pad.4
  183.9 1.3 all_to_all.28
  185.2 58.8 %all_to_all.36 = f32[128,14,128]{2,1,0:T(8,128)S(1)} all-to-all(f32[128,14,128]{2,1,0:T(8,128)S(1)} %all_to_all.28), channel_id=1, replica_groups=mesh['vox'=128,'ch'=4] {'vox'}, dimensions={0} | all-to-all | bytes 1835008 | tf_op jit(solution)/shard_map/all_to_all | solution.py:21
  244.1 0.9 broadcast_in_dim.67
  245.0 10.2 %all-to-all-start.3 = ((bf16[128,14,128]{2,1,0:T(8,128)(2,1)}), bf16[128,14,128]{2,1,0:T(8,128)(2,1)S(1)}, u32[]{:S(2)}, u32[]{:S(2)}) async-start(bf16[128,14,128]{2,1,0:T(8,128)(2,1)} %broadcast_in_dim.67), calls=%async_computation.4 | async-start | bytes 1048576 | tf_op jit(solution)/shard_map/all_to_all | solution.py:24
  255.2 1.0 copy.55
  256.3 31.0 %reduce-scatter.2.cloned.1.call-done = f32[1024,32]{0,1:T(8,128)} async-done(((f32[1024,128]{0,1:T(8,128)}), f32[1024,32]{0,1:T(8,128)}) %reduce-scatter.2.cloned.1.call-update) | async-done | bytes 131088 | tf_op jit(solution)/shard_map/reduce_scatter | solution.py:111
  287.3 1.5 fusion.22
  289.0 0.8 slice.27
  (63 shorter events, 2.5 us)
Async XLA Ops:
  7.8 0.7 copy-start.7
  9.7 0.7 copy-start.2
  9.7 0.7 copy-start.3
  10.5 39.6 %copy-start.5 = (s32[512,1]{0,1:T(1,128)S(1)}, s32[512,1]{0,1:T(1,128)}, u32[]{:S(2)}) copy-start(s32[512,1]{0,1:T(1,128)} %param.19) | copy-start | bytes 6148
  53.4 20.7 %copy-start.6 = (s32[768]{0:T(1024)S(1)}, s32[768]{0:T(1024)}, u32[]{:S(2)}) copy-start(s32[768]{0:T(1024)} %param.20) | copy-start | bytes 9220
  53.4 36.8 %all-to-all-start = ((bf16[128,3,128]{2,1,0:T(4,128)(2,1)}), bf16[128,3,128]{2,1,0:T(4,128)(2,1)S(1)}, u32[]{:S(2)}, u32[]{:S(2)}) async-start(bf16[128,3,128]{2,1,0:T(4,128)(2,1)} %all_to_all.24), calls=%async_computation | async-start | bytes 262144 | tf_op jit(solution)/shard_map/all_to_all | solution.py:75
  96.4 0.8 copy-start.4
  100.7 23.2 %all-to-all-start.1 = ((bf16[128,3,128]{2,1,0:T(4,128)(2,1)}), bf16[128,3,128]{2,1,0:T(4,128)(2,1)S(1)}, u32[]{:S(2)}, u32[]{:S(2)}) async-start(bf16[128,3,128]{2,1,0:T(4,128)(2,1)} %all_to_all.26), calls=%async_computation.1 | async-start | bytes 262144 | tf_op jit(solution)/shard_map/all_to_all | solution.py:86
  139.7 0.9 copy-start
  142.5 11.7 %copy-start.1 = (f32[27,64,128]{2,1,0:T(8,128)S(1)}, f32[27,64,128]{2,1,0:T(8,128)}, u32[]{:S(2)}) copy-start(f32[27,64,128]{2,1,0:T(8,128)} %copy-done) | copy-start | bytes 2654212 | tf_op jit(solution)/shard_map/while
  168.3 0.9 copy-start
  171.2 11.7 %copy-start.1 = (f32[27,64,128]{2,1,0:T(8,128)S(1)}, f32[27,64,128]{2,1,0:T(8,128)}, u32[]{:S(2)}) copy-start(f32[27,64,128]{2,1,0:T(8,128)} %copy-done) | copy-start | bytes 2654212 | tf_op jit(solution)/shard_map/while
  245.0 43.9 %all-to-all-start.3 = ((bf16[128,14,128]{2,1,0:T(8,128)(2,1)}), bf16[128,14,128]{2,1,0:T(8,128)(2,1)S(1)}, u32[]{:S(2)}, u32[]{:S(2)}) async-start(bf16[128,14,128]{2,1,0:T(8,128)(2,1)} %broadcast_in_dim.67), calls=%async_computation.4 | async-start | bytes 1048576 | tf_op jit(solution)/shard_map/all_to_all | solution.py:24
  255.2 32.1 %reduce-scatter.2.cloned.1.call-start = ((), (), s32[]{:S(2)}) async-start(), calls=%async_computation.5 | async-start | bytes 655360 | tf_op jit(solution)/shard_map/reduce_scatter | solution.py:111
Sparse Core Ops, SparseCore 0:
  258.8 28.4 reduce-scatter.1

commit v2 on v1

v2 whole, which is shorter than its diff:
```python
import math

import jax
import jax.numpy as jnp
from jax import lax
from jax.sharding import PartitionSpec as P


def owner_slots(owner_of, owners):
    labels = jnp.arange(owners, dtype=jnp.int32)
    onehot = (owner_of[:, None] == labels[None, :]).astype(jnp.int32)
    before = jnp.cumsum(onehot, axis=0) - onehot
    return jnp.sum(before * onehot, axis=1)


def one_hot(index, size):
    return (index[:, None] == jnp.arange(size, dtype=jnp.int32)[None, :]).astype(jnp.bfloat16)


def exact_sum(onehot, values):
    high = values.astype(jnp.bfloat16)
    low = (values - high.astype(jnp.float32)).astype(jnp.bfloat16)
    both = jnp.concatenate([high, low], axis=1)
    total = jnp.einsum("pt,pc->tc", onehot, both, preferred_element_type=jnp.float32)
    width = values.shape[1]
    return total[:, :width] + total[:, width:]


def reduce_replicate(weight_sum, owners, factor):
    shape = weight_sum.shape
    rows = weight_sum.size // 128
    chunk = -(-rows // owners)
    flat = jnp.pad(weight_sum.reshape(rows, 128), ((0, chunk * owners - rows), (0, 0)))
    got = lax.all_to_all(flat, "vox", 0, 0, tiled=True)
    mine = (got.reshape(owners, chunk, 128).sum(axis=0) * factor).astype(jnp.bfloat16)
    spread = jnp.broadcast_to(mine[None], (owners, chunk, 128)).reshape(owners * chunk, 128)
    back = lax.all_to_all(spread, "vox", 0, 0, tiled=True)
    return back[:rows].reshape(shape)


def body(
    features,
    kernel,
    coarse_grad,
    pair_fine,
    pair_target,
    block_offset,
    target_owner,
    slot_coarse_row,
    fine_count,
):
    owners = lax.axis_size("vox")
    fine_total, width_in = features.shape
    width_out, coarse_total = coarse_grad.shape
    offsets_all = kernel.shape[0]
    targets = target_owner.shape[0]
    capacity = slot_coarse_row.shape[0] // owners
    slots = owners * capacity
    blocks = block_offset.shape[0]
    pairs = pair_fine.shape[0]
    group = pairs // blocks
    live_mask = jnp.arange(fine_total, dtype=jnp.int32) < fine_count[0]
    masked = jnp.where(live_mask[:, None], features, jnp.zeros((), features.dtype))
    fine_hot = one_hot(pair_fine, fine_total)
    target_hot = one_hot(pair_target, targets)
    gathered = jnp.dot(fine_hot, masked, preferred_element_type=jnp.float32).astype(jnp.bfloat16)
    gathered = gathered.reshape(blocks, group, width_in)
    weights = kernel[block_offset]
    partial_value = jnp.einsum(
        "bpc,boc->bpo", gathered, weights, preferred_element_type=jnp.float32
    ).reshape(pairs, width_out)
    target_part = exact_sum(target_hot, partial_value).astype(jnp.bfloat16)

    owner_of = target_owner[:, 0]
    slot_index = owner_of * capacity + owner_slots(owner_of, owners)
    slot_hot = one_hot(slot_index, slots)
    send_rows = jnp.einsum(
        "ts,to->so", slot_hot, target_part, preferred_element_type=jnp.float32
    ).astype(jnp.bfloat16)
    lane_shape = (slots * width_out // 128, 128)
    received = lax.all_to_all(
        send_rows.reshape(lane_shape), "vox", split_axis=0, concat_axis=0, tiled=True
    )
    got_rows = received.reshape(slots, width_out)
    row_hot = one_hot(slot_coarse_row, coarse_total)
    coarse = jnp.einsum("sc,so->co", row_hot, got_rows, preferred_element_type=jnp.float32)
    gate_output = jax.nn.sigmoid(coarse)
    activation = (coarse * gate_output).astype(jnp.bfloat16)
    grad_coarse = (
        coarse_grad.astype(jnp.float32).T * gate_output * (1.0 + coarse * (1.0 - gate_output))
    ).astype(jnp.bfloat16)
    back_rows = jnp.einsum(
        "sc,co->so", row_hot, grad_coarse, preferred_element_type=jnp.float32
    ).astype(jnp.bfloat16)
    returned = lax.all_to_all(
        back_rows.reshape(lane_shape), "vox", split_axis=0, concat_axis=0, tiled=True
    )
    grad_target = jnp.einsum(
        "ts,so->to", slot_hot, returned.reshape(slots, width_out), preferred_element_type=jnp.float32
    ).astype(jnp.bfloat16)
    grad_rows = jnp.einsum(
        "pt,to->po", target_hot, grad_target, preferred_element_type=jnp.float32
    ).astype(jnp.bfloat16)
    grad_rows = grad_rows.reshape(blocks, group, width_out)
    grad_in = jnp.einsum(
        "bpo,boc->bpc", grad_rows, weights, preferred_element_type=jnp.float32
    ).reshape(pairs, width_in)
    fine_sum = exact_sum(fine_hot, grad_in)
    fine_grad = lax.psum_scatter(fine_sum, "ch", scatter_dimension=1, tiled=True)
    grad_features = jnp.where(live_mask[:, None], fine_grad, jnp.zeros((), jnp.float32)).astype(
        jnp.bfloat16
    )
    grad_weight = jnp.einsum(
        "bpc,bpo->boc", gathered, grad_rows, preferred_element_type=jnp.float32
    )
    weight_sum = (
        jnp.zeros((offsets_all, width_out, width_in), jnp.float32).at[block_offset].add(grad_weight)
    )
    factor = math.sqrt(offsets_all / (blocks * group * owners))
    grad_kernel = reduce_replicate(weight_sum, owners, factor)
    return (activation.T, grad_features.T, grad_kernel)


def solution(mesh):
    in_specs = (
        P("vox", None),
        P(None, "ch", None),
        P("ch", "vox"),
        P("vox"),
        P("vox"),
        P("vox"),
        P("vox", None),
        P("vox"),
        P("vox"),
    )
    out_specs = (P("ch", "vox"), P("ch", "vox"), P(None, "ch", None))
    return jax.shard_map(body, mesh=mesh, in_specs=in_specs, out_specs=out_specs, check_vma=False)
```

time: 298 us -> 205 us (0.69)
  other arithmetic: 61.3 us -> 5.03 us
  local copies, waits for them, and re-layouts: 58.3 us -> 8.29 us
  starting transfers between devices: 38.1 us -> 17.3 us
  matrix products: 1.74 us -> 19.7 us
  waiting for transfers between devices: 63.1 us -> 78.5 us
    scatter-add x7 -> x1, other arithmetic: 55.3 us -> 2.13 us  [body(): jnp.zeros((offsets_all, width_out, width_in), jnp.float32).at[block_offset]]
    gather x12 -> x1, local copies, waits for them, and re-layouts: 46.8 us -> 0.65 us  [body(): weights = kernel[block_offset]]
    reduce_scatter x1 -> x0, waiting for transfers between devices: 31 us -> none  [body(): lax.psum_scatter(fine_sum, 'ch', scatter_dimension=1, tiled=True)]
    unnamed x1 -> x2, waiting for transfers between devices: 0.02 us -> 28.4 us
    all_to_all x2 -> x1, starting transfers between devices: 27.8 us -> 6.84 us  [reduce_replicate(): got = lax.all_to_all(flat, 'vox', 0, 0, tiled=True)]
    dot_general x4 -> x10, matrix products: 1.18 us -> 19.7 us  [the longest x2 7.85 us: exact_sum(): jnp.einsum('pt,pc->tc', onehot, both, preferred_element_type=jnp.float32)]
    all_to_all x2 -> x1, waiting for transfers between devices: 32.1 us -> 50.1 us  [reduce_replicate(): got = lax.all_to_all(flat, 'vox', 0, 0, tiled=True)]
    all_to_all x1 -> x2, blocking collectives: 58.8 us -> 59.8 us  [the longest x1 36.8 us: body(): lax.all_to_all(send_rows.reshape(lane_shape), 'vox', split_axis=0, concat...]
  transfers between devices with their start and end apart: 4 -> 3, of which waited for: 3 -> 2; matrix products, arithmetic and copies ran while one was open for 1% -> 5% of each run, Pallas kernels for 0% -> 0%
where the time goes in v2:
time: 205 us; the launch traced here: 204 us
  waiting for transfers between devices  78.5 us (38%)
  blocking collectives  59.8 us (29%)
  matrix products  19.7 us (10%)
  starting transfers between devices  17.3 us (8%)
  between operations  15 us (7%)
  local copies, waits for them, and re-layouts  8.29 us (4%)
  other arithmetic  5.03 us (2%)
    all_to_all x1, waiting for transfers between devices, reduce_replicate(): got = lax.all_to_all(flat, 'vox', 0, 0, tiled=True)  50.1 us
    all_to_all x1, blocking collectives, body(): lax.all_to_all(send_rows.reshape(lane_shape), 'vox', split_axis=0, concat...  36.8 us
    unnamed x2, waiting for transfers between devices  28.4 us
    all_to_all x1, blocking collectives, body(): lax.all_to_all(back_rows.reshape(lane_shape), 'vox', split_axis=0, concat...  23.1 us
    all_to_all x1, starting transfers between devices, reduce_replicate(): back = lax.all_to_all(spread, 'vox', 0, 0, tiled=True)  10.2 us
    dot_general x2, matrix products, exact_sum(): jnp.einsum('pt,pc->tc', onehot, both, preferred_element_type=jnp.float32)  7.85 us
    all_to_all x1, starting transfers between devices, reduce_replicate(): got = lax.all_to_all(flat, 'vox', 0, 0, tiled=True)  6.84 us
  transfers between devices with their start and end apart: 3, of which 2 were waited for; matrix products, arithmetic and copies ran while one was open for 5% of the time, Pallas kernels for 0%

profile of v2, /device:TPU:1, one launch (start us, length us, event | category | flops | bytes accessed | tf_op | source)
XLA Modules:
  0.0 203.7 jit_solution(12631588119628834391)
XLA Ops:
  7.2 0.0 copy-start
  7.9 0.7 compare_select_fusion
  8.6 0.6 gather_fusion
  9.2 4.1 %fusion.6 = bf16[4096,128]{1,0:T(8,128)(2,1)S(1)} fusion(s32[4096]{0:T(1024)} %param.12, bf16[1024,128]{1,0:T(8,128)(2,1)} %param.9, pred[1024]{0:T(1024)(128)(4,1)S(1)} %iota_compare_fusion.29), kind=kOutput, calls=%fused_computation.10 | convolution fusion | flops 1078591488 | bytes 1328128 | tf_op jit(solution)/shard_map/dot_general | solution.py:66
  13.3 0.8 convolution_bitcast_fusion
  14.1 0.0 copy-start.4
  14.1 0.1 fusion.22
  14.2 0.1 copy.48
  14.3 0.5 copy-done.2
  14.8 0.1 copy.24
  14.9 0.2 fusion.41
  15.2 0.2 fusion.39
  15.5 1.5 fusion.5
  17.0 0.5 fusion.20
  17.5 0.2 copy.27
  17.6 0.2 all_to_all.24
  17.8 36.8 %all_to_all.36 = bf16[128,3,128]{2,1,0:T(4,128)(2,1)S(1)} all-to-all(bf16[128,3,128]{2,1,0:T(4,128)(2,1)S(1)} %all_to_all.24), channel_id=1, replica_groups=mesh['vox'=128,'ch'=4] {'vox'}, dimensions={0} | all-to-all | bytes 196608 | tf_op jit(solution)/shard_map/all_to_all | solution.py:81
  54.6 0.1 reshape.79
  54.7 1.2 fusion.52
  55.9 0.5 fusion.19
  56.4 0.2 copy.28
  56.6 0.2 all_to_all.26
  56.8 23.1 %all_to_all.37 = bf16[128,3,128]{2,1,0:T(4,128)(2,1)S(1)} all-to-all(bf16[128,3,128]{2,1,0:T(4,128)(2,1)S(1)} %all_to_all.26), channel_id=1, replica_groups=mesh['vox'=128,'ch'=4] {'vox'}, dimensions={0} | all-to-all | bytes 196608 | tf_op jit(solution)/shard_map/all_to_all | solution.py:95
  79.8 0.1 reshape.80
  80.0 2.9 %fusion.18 = bf16[8,32,8,128]{3,2,1,0:T(8,128)(2,1)} fusion(s32[4096]{0:T(1024)S(1)} %copy-done.4, bf16[768,64]{1,0:T(8,128)(2,1)S(1)} %reshape.80, s32[512]{0:T(512)S(1)} %bitcast.89), kind=kOutput, calls=%fused_computation.27 | convolution fusion | flops 321552384 | bytes 641024 | tf_op jit(solution)/shard_map/pt,to->po/dot_general | solution.py:101
  82.9 1.4 fusion.31
  84.3 0.1 broadcast_in_dim.53
  84.4 2.1 %scatter_fusion = f32[27,64,128]{2,1,0:T(8,128)S(1)} fusion(f32[27,64,128]{2,1,0:T(8,128)S(1)} %broadcast_in_dim.53, s32[32]{0:T(128)S(1)} %compare_select_fusion, f32[32,64,128]{2,1,0:T(8,128)S(1)} %fusion.31), kind=kCustom, calls=%fused_computation.1 | custom fusion | flops 262144 | bytes 3145856 | tf_op jit(solution)/shard_map/scatter-add | solution.py:117
  86.6 0.1 pad.4
  86.7 1.1 all_to_all.28
  87.8 6.8 %all-to-all-start.2 = ((f32[128,14,128]{2,1,0:T(8,128)}), f32[128,14,128]{2,1,0:T(8,128)S(1)}, u32[]{:S(2)}, u32[]{:S(2)}) async-start(f32[128,14,128]{2,1,0:T(8,128)} %all_to_all.28), calls=%async_computation.2 | async-start | bytes 2097152 | tf_op jit(solution)/shard_map/all_to_all | solution.py:34
  94.6 0.5 fusion.33
  95.1 1.3 fusion.13
  96.4 50.1 %all-to-all-done.2 = f32[128,14,128]{2,1,0:T(8,128)S(1)} async-done(((f32[128,14,128]{2,1,0:T(8,128)}), f32[128,14,128]{2,1,0:T(8,128)S(1)}, u32[]{:S(2)}, u32[]{:S(2)}) %all-to-all-start.2) | async-done | bytes 917536 | tf_op jit(solution)/shard_map/all_to_all | solution.py:34
  146.5 0.1 reduce_sum.22
  146.6 0.9 broadcast_in_dim.54
  147.5 10.2 %all-to-all-start.3 = ((bf16[128,14,128]{2,1,0:T(8,128)(2,1)}), bf16[128,14,128]{2,1,0:T(8,128)(2,1)S(1)}, u32[]{:S(2)}, u32[]{:S(2)}) async-start(bf16[128,14,128]{2,1,0:T(8,128)(2,1)} %broadcast_in_dim.54), calls=%async_computation.3 | async-start | bytes 1048576 | tf_op jit(solution)/shard_map/all_to_all | solution.py:37
  157.7 0.3 reduce-scatter.4.cloned.1.call-start
  158.0 6.3 %fusion = f32[1024,256]{1,0:T(8,128)S(1)} fusion(s32[4096]{0:T(1024)S(1)} %copy-done.5, bf16[4096,128]{1,0:T(8,128)(2,1)S(1)} %get-tuple-element.12, bf16[4096,128]{1,0:T(8,128)(2,1)} %get-tuple-element.13), kind=kOutput, calls=%fused_computation.3 | convolution fusion | flops 2155872256 | bytes 3162112 | tf_op jit(solution)/shard_map/pt,pc->tc/dot_general | solution.py:24
  164.4 0.1 slice_add_fusion
  164.4 1.0 copy.32
  165.4 0.0 reduce-scatter.4.cloned.1.call-update
  165.4 28.4 %reduce-scatter.4.cloned.1.call-done = f32[32,1024]{1,0:T(8,128)} async-done(((f32[128,1024]{1,0:T(8,128)}), f32[32,1024]{1,0:T(8,128)}) %reduce-scatter.4.cloned.1.call-update) | async-done | bytes 131088
  193.8 1.1 copy.33
  194.9 0.2 fusion.37
  195.1 0.8 copy.31
  195.9 0.1 all_to_all.31
  196.0 0.8 slice.35
  (22 shorter events, 0.1 us)
Async XLA Ops:
  7.2 1.4 copy-start
  14.1 0.7 copy-start.2
  14.1 1.4 copy-start.4
  15.5 39.3 %copy-start.6 = (s32[768]{0:T(1024)S(1)}, s32[768]{0:T(1024)}, u32[]{:S(2)}) copy-start(s32[768]{0:T(1024)} %param.16) | copy-start | bytes 9220
  17.0 38.9 %copy-start.3 = (bf16[64,512]{1,0:T(8,128)(2,1)S(1)}, bf16[64,512]{1,0:T(8,128)(2,1)}, u32[]{:S(2)}) copy-start(bf16[64,512]{1,0:T(8,128)(2,1)} %param.11) | copy-start | bytes 196612
  86.7 8.0 %copy-start.1 = (bf16[8,32,8,128]{3,2,1,0:T(8,128)(2,1)S(1)}, bf16[8,32,8,128]{3,2,1,0:T(8,128)(2,1)}, u32[]{:S(2)}) copy-start(bf16[8,32,8,128]{3,2,1,0:T(8,128)(2,1)} %fusion.18) | copy-start | bytes 1572868
  87.8 58.7 %all-to-all-start.2 = ((f32[128,14,128]{2,1,0:T(8,128)}), f32[128,14,128]{2,1,0:T(8,128)S(1)}, u32[]{:S(2)}, u32[]{:S(2)}) async-start(f32[128,14,128]{2,1,0:T(8,128)} %all_to_all.28), calls=%async_computation.2 | async-start | bytes 2097152 | tf_op jit(solution)/shard_map/all_to_all | solution.py:34
  96.4 61.6 %copy-start.5 = (s32[4096]{0:T(1024)S(1)}, s32[4096]{0:T(1024)}, u32[]{:S(2)}) copy-start(s32[4096]{0:T(1024)} %param.12) | copy-start | bytes 49156
  147.5 48.4 %all-to-all-start.3 = ((bf16[128,14,128]{2,1,0:T(8,128)(2,1)}), bf16[128,14,128]{2,1,0:T(8,128)(2,1)S(1)}, u32[]{:S(2)}, u32[]{:S(2)}) async-start(bf16[128,14,128]{2,1,0:T(8,128)(2,1)} %broadcast_in_dim.54), calls=%async_computation.3 | async-start | bytes 1048576 | tf_op jit(solution)/shard_map/all_to_all | solution.py:37
  157.7 36.1 %reduce-scatter.4.cloned.1.call-start = ((), (), s32[]{:S(2)}) async-start(), calls=%async_computation.5 | async-start | bytes 655360
Sparse Core Ops, SparseCore 0:
  165.6 28.2 reduce-scatter.3

commit v3 on v2

--- a/solution.py
+++ b/solution.py
@@ -18,9 +18,9 @@
 
 
 def exact_sum(onehot, values):
-    high = values.astype(jnp.bfloat16)
-    low = (values - high.astype(jnp.float32)).astype(jnp.bfloat16)
-    both = jnp.concatenate([high, low], axis=1)
+    high = lax.reduce_precision(values, exponent_bits=8, mantissa_bits=7)
+    low = values - high
+    both = jnp.concatenate([high.astype(jnp.bfloat16), low.astype(jnp.bfloat16)], axis=1)
     total = jnp.einsum("pt,pc->tc", onehot, both, preferred_element_type=jnp.float32)
     width = values.shape[1]
     return total[:, :width] + total[:, width:]

time: 205 us -> 205 us (level)
  no operation moved by 1% of the time
where the time goes in v3:
time: 205 us; the launch traced here: 204 us
  waiting for transfers between devices  78.5 us (38%)
  blocking collectives  59.8 us (29%)
  matrix products  18.7 us (9%)
  starting transfers between devices  17.3 us (8%)
  between operations  15 us (7%)
  local copies, waits for them, and re-layouts  8.37 us (4%)
  other arithmetic  6.55 us (3%)
    all_to_all x1, waiting for transfers between devices, reduce_replicate(): got = lax.all_to_all(flat, 'vox', 0, 0, tiled=True)  50 us
    all_to_all x1, blocking collectives, body(): lax.all_to_all(send_rows.reshape(lane_shape), 'vox', split_axis=0, concat...  36.8 us
    unnamed x2, waiting for transfers between devices  28.4 us
    all_to_all x1, blocking collectives, body(): lax.all_to_all(back_rows.reshape(lane_shape), 'vox', split_axis=0, concat...  23.1 us
    all_to_all x1, starting transfers between devices, reduce_replicate(): back = lax.all_to_all(spread, 'vox', 0, 0, tiled=True)  10.2 us
    dot_general x2, matrix products, exact_sum(): jnp.einsum('pt,pc->tc', onehot, both, preferred_element_type=jnp.float32)  7.85 us
    all_to_all x1, starting transfers between devices, reduce_replicate(): got = lax.all_to_all(flat, 'vox', 0, 0, tiled=True)  6.83 us
  transfers between devices with their start and end apart: 3, of which 2 were waited for; matrix products, arithmetic and copies ran while one was open for 5% of the time, Pallas kernels for 0%

profile of v3, /device:TPU:1, one launch (start us, length us, event | category | flops | bytes accessed | tf_op | source)
XLA Modules:
  0.0 204.2 jit_solution(16556421932449508191)
XLA Ops:
  7.2 0.0 copy-start
  7.9 0.7 compare_select_fusion
  8.6 0.8 copy.24
  9.4 0.2 fusion.41
  9.7 0.9 fusion.39
  10.6 0.7 multiply_add_fusion
  11.3 0.6 gather_fusion
  12.0 3.1 %fusion.6 = bf16[4096,128]{1,0:T(8,128)(2,1)S(1)} fusion(s32[4096]{0:T(1024)S(1)} %copy-done.5, bf16[1024,128]{1,0:T(8,128)(2,1)S(1)} %copy-done.2, pred[1024]{0:T(1024)(128)(4,1)S(1)} %iota_compare_fusion.29), kind=kOutput, calls=%fused_computation.10 | convolution fusion | flops 1078591488 | bytes 1328128 | tf_op jit(solution)/shard_map/dot_general | solution.py:66
  15.1 0.8 convolution_bitcast_fusion
  15.9 0.2 reduce-precision_convert_fusion.1
  16.1 0.0 copy-start.6
  16.1 1.5 fusion.5
  17.6 0.0 copy-start.3
  17.6 0.5 fusion.20
  18.1 0.2 copy.27
  18.2 0.2 all_to_all.24
  18.4 36.8 %all_to_all.36 = bf16[128,3,128]{2,1,0:T(4,128)(2,1)S(1)} all-to-all(bf16[128,3,128]{2,1,0:T(4,128)(2,1)S(1)} %all_to_all.24), channel_id=1, replica_groups=mesh['vox'=128,'ch'=4] {'vox'}, dimensions={0} | all-to-all | bytes 196608 | tf_op jit(solution)/shard_map/all_to_all | solution.py:81
  55.2 0.1 reshape.79
  55.3 1.2 fusion.52
  56.5 0.5 fusion.19
  57.0 0.2 copy.28
  57.2 0.2 all_to_all.26
  57.4 23.1 %all_to_all.37 = bf16[128,3,128]{2,1,0:T(4,128)(2,1)S(1)} all-to-all(bf16[128,3,128]{2,1,0:T(4,128)(2,1)S(1)} %all_to_all.26), channel_id=1, replica_groups=mesh['vox'=128,'ch'=4] {'vox'}, dimensions={0} | all-to-all | bytes 196608 | tf_op jit(solution)/shard_map/all_to_all | solution.py:95
  80.4 0.1 reshape.80
  80.6 2.9 %fusion.18 = bf16[8,32,8,128]{3,2,1,0:T(8,128)(2,1)} fusion(s32[4096]{0:T(1024)S(1)} %copy-done.4, bf16[768,64]{1,0:T(8,128)(2,1)S(1)} %reshape.80, s32[512]{0:T(512)S(1)} %bitcast.80), kind=kOutput, calls=%fused_computation.29 | convolution fusion | flops 321552384 | bytes 641024 | tf_op jit(solution)/shard_map/pt,to->po/dot_general | solution.py:101
  83.5 1.4 fusion.31
  84.9 0.1 broadcast_in_dim.53
  85.0 2.1 %scatter_fusion = f32[27,64,128]{2,1,0:T(8,128)S(1)} fusion(f32[27,64,128]{2,1,0:T(8,128)S(1)} %broadcast_in_dim.53, s32[32]{0:T(128)S(1)} %compare_select_fusion, f32[32,64,128]{2,1,0:T(8,128)S(1)} %fusion.31), kind=kCustom, calls=%fused_computation.1 | custom fusion | flops 262144 | bytes 3145856 | tf_op jit(solution)/shard_map/scatter-add | solution.py:117
  87.2 0.1 pad.4
  87.3 1.1 all_to_all.28
  88.4 6.8 %all-to-all-start.2 = ((f32[128,14,128]{2,1,0:T(8,128)}), f32[128,14,128]{2,1,0:T(8,128)S(1)}, u32[]{:S(2)}, u32[]{:S(2)}) async-start(f32[128,14,128]{2,1,0:T(8,128)} %all_to_all.28), calls=%async_computation.2 | async-start | bytes 2097152 | tf_op jit(solution)/shard_map/all_to_all | solution.py:34
  95.2 0.5 fusion.33
  95.7 1.3 reduce-precision_convert_fusion
  97.0 50.0 %all-to-all-done.2 = f32[128,14,128]{2,1,0:T(8,128)S(1)} async-done(((f32[128,14,128]{2,1,0:T(8,128)}), f32[128,14,128]{2,1,0:T(8,128)S(1)}, u32[]{:S(2)}, u32[]{:S(2)}) %all-to-all-start.2) | async-done | bytes 917536 | tf_op jit(solution)/shard_map/all_to_all | solution.py:34
  147.1 0.1 reduce_sum.22
  147.2 0.9 broadcast_in_dim.54
  148.1 10.2 %all-to-all-start.3 = ((bf16[128,14,128]{2,1,0:T(8,128)(2,1)}), bf16[128,14,128]{2,1,0:T(8,128)(2,1)S(1)}, u32[]{:S(2)}, u32[]{:S(2)}) async-start(bf16[128,14,128]{2,1,0:T(8,128)(2,1)} %broadcast_in_dim.54), calls=%async_computation.3 | async-start | bytes 1048576 | tf_op jit(solution)/shard_map/all_to_all | solution.py:37
  158.3 0.3 reduce-scatter.4.cloned.1.call-start
  158.6 6.3 %fusion = f32[1024,256]{1,0:T(8,128)S(1)} fusion(s32[4096]{0:T(1024)S(1)} %copy-done.5, bf16[4096,128]{1,0:T(8,128)(2,1)} %get-tuple-element.13, bf16[4096,128]{1,0:T(8,128)(2,1)S(1)} %get-tuple-element.12), kind=kOutput, calls=%fused_computation.3 | convolution fusion | flops 2155872256 | bytes 3162112 | tf_op jit(solution)/shard_map/pt,pc->tc/dot_general | solution.py:24
  164.9 0.1 slice_add_fusion
  165.0 1.0 copy.32
  166.0 0.0 reduce-scatter.4.cloned.1.call-update
  166.0 28.4 %reduce-scatter.4.cloned.1.call-done = f32[32,1024]{1,0:T(8,128)} async-done(((f32[128,1024]{1,0:T(8,128)}), f32[32,1024]{1,0:T(8,128)}) %reduce-scatter.4.cloned.1.call-update) | async-done | bytes 131088
  194.4 1.1 copy.33
  195.5 0.2 fusion.37
  195.7 0.8 copy.31
  196.5 0.1 all_to_all.31
  196.6 0.8 slice.35
  (21 shorter events, 0.1 us)
Async XLA Ops:
  7.2 4.1 %copy-start = (bf16[27,64,128]{2,1,0:T(8,128)(2,1)S(1)}, bf16[27,64,128]{2,1,0:T(8,128)(2,1)}, u32[]{:S(2)}) copy-start(bf16[27,64,128]{2,1,0:T(8,128)(2,1)} %param.10) | copy-start | bytes 1327108
  7.2 4.8 %copy-start.5 = (s32[4096]{0:T(1024)S(1)}, s32[4096]{0:T(1024)}, u32[]{:S(2)}) copy-start(s32[4096]{0:T(1024)} %param.12) | copy-start | bytes 49156
  7.2 4.8 %copy-start.2 = (bf16[1024,128]{1,0:T(8,128)(2,1)S(1)}, bf16[1024,128]{1,0:T(8,128)(2,1)}, u32[]{:S(2)}) copy-start(bf16[1024,128]{1,0:T(8,128)(2,1)} %param.9) | copy-start | bytes 786436
  15.1 1.0 copy-start.4
  16.1 39.3 %copy-start.6 = (s32[768]{0:T(1024)S(1)}, s32[768]{0:T(1024)}, u32[]{:S(2)}) copy-start(s32[768]{0:T(1024)} %param.16) | copy-start | bytes 9220
  17.6 38.9 %copy-start.3 = (bf16[64,512]{1,0:T(8,128)(2,1)S(1)}, bf16[64,512]{1,0:T(8,128)(2,1)}, u32[]{:S(2)}) copy-start(bf16[64,512]{1,0:T(8,128)(2,1)} %param.11) | copy-start | bytes 196612
  87.2 8.0 %copy-start.1 = (bf16[8,32,8,128]{3,2,1,0:T(8,128)(2,1)S(1)}, bf16[8,32,8,128]{3,2,1,0:T(8,128)(2,1)}, u32[]{:S(2)}) copy-start(bf16[8,32,8,128]{3,2,1,0:T(8,128)(2,1)} %fusion.18) | copy-start | bytes 1572868
  88.4 58.7 %all-to-all-start.2 = ((f32[128,14,128]{2,1,0:T(8,128)}), f32[128,14,128]{2,1,0:T(8,128)S(1)}, u32[]{:S(2)}, u32[]{:S(2)}) async-start(f32[128,14,128]{2,1,0:T(8,128)} %all_to_all.28), calls=%async_computation.2 | async-start | bytes 2097152 | tf_op jit(solution)/shard_map/all_to_all | solution.py:34
  148.1 48.4 %all-to-all-start.3 = ((bf16[128,14,128]{2,1,0:T(8,128)(2,1)}), bf16[128,14,128]{2,1,0:T(8,128)(2,1)S(1)}, u32[]{:S(2)}, u32[]{:S(2)}) async-start(bf16[128,14,128]{2,1,0:T(8,128)(2,1)} %broadcast_in_dim.54), calls=%async_computation.3 | async-start | bytes 1048576 | tf_op jit(solution)/shard_map/all_to_all | solution.py:37
  158.3 36.1 %reduce-scatter.4.cloned.1.call-start = ((), (), s32[]{:S(2)}) async-start(), calls=%async_computation.5 | async-start | bytes 655360
Sparse Core Ops, SparseCore 0:
  166.1 28.2 reduce-scatter.3

commit v4 on v3

--- a/solution.py
+++ b/solution.py
@@ -26,15 +26,29 @@
     return total[:, :width] + total[:, width:]
 
 
-def reduce_replicate(weight_sum, owners, factor):
+VOX = ("z", "y", "core")
+
+
+def staged_all_to_all(x):
+    for axis, name in ((2, "core"), (1, "y"), (0, "z")):
+        x = lax.all_to_all(x, name, axis, axis, tiled=True)
+    return x
+
+
+def reduce_replicate(weight_sum, sizes, factor):
     shape = weight_sum.shape
+    owners = math.prod(sizes)
     rows = weight_sum.size // 128
     chunk = -(-rows // owners)
     flat = jnp.pad(weight_sum.reshape(rows, 128), ((0, chunk * owners - rows), (0, 0)))
-    got = lax.all_to_all(flat, "vox", 0, 0, tiled=True)
-    mine = (got.reshape(owners, chunk, 128).sum(axis=0) * factor).astype(jnp.bfloat16)
-    spread = jnp.broadcast_to(mine[None], (owners, chunk, 128)).reshape(owners * chunk, 128)
-    back = lax.all_to_all(spread, "vox", 0, 0, tiled=True)
+    part = flat.reshape(*sizes, chunk, 128)
+    for axis, name in ((2, "core"), (1, "y"), (0, "z")):
+        part = lax.all_to_all(part, name, axis, axis, tiled=True).sum(axis=axis)
+    mine = (part * factor).astype(jnp.bfloat16)
+    for axis, name in ((0, "z"), (1, "y"), (2, "core")):
+        mine = jnp.broadcast_to(mine[None], (sizes[axis],) + mine.shape)
+        mine = lax.all_to_all(mine, name, 0, 0, tiled=True)
+    back = jnp.transpose(mine, (2, 1, 0, 3, 4)).reshape(owners * chunk, 128)
     return back[:rows].reshape(shape)
 
 
@@ -49,7 +63,8 @@
     slot_coarse_row,
     fine_count,
 ):
-    owners = lax.axis_size("vox")
+    sizes = tuple(lax.axis_size(name) for name in VOX)
+    owners = math.prod(sizes)
     fine_total, width_in = features.shape
     width_out, coarse_total = coarse_grad.shape
     offsets_all = kernel.shape[0]
@@ -77,10 +92,8 @@
     send_rows = jnp.einsum(
         "ts,to->so", slot_hot, target_part, preferred_element_type=jnp.float32
     ).astype(jnp.bfloat16)
-    lane_shape = (slots * width_out // 128, 128)
-    received = lax.all_to_all(
-        send_rows.reshape(lane_shape), "vox", split_axis=0, concat_axis=0, tiled=True
-    )
+    lane_shape = (*sizes, capacity * width_out // 128, 128)
+    received = staged_all_to_all(send_rows.reshape(lane_shape))
     got_rows = received.reshape(slots, width_out)
     row_hot = one_hot(slot_coarse_row, coarse_total)
     coarse = jnp.einsum("sc,so->co", row_hot, got_rows, preferred_element_type=jnp.float32)
@@ -92,9 +105,7 @@
     back_rows = jnp.einsum(
         "sc,co->so", row_hot, grad_coarse, preferred_element_type=jnp.float32
     ).astype(jnp.bfloat16)
-    returned = lax.all_to_all(
-        back_rows.reshape(lane_shape), "vox", split_axis=0, concat_axis=0, tiled=True
-    )
+    returned = staged_all_to_all(back_rows.reshape(lane_shape))
     grad_target = jnp.einsum(
         "ts,so->to", slot_hot, returned.reshape(slots, width_out), preferred_element_type=jnp.float32
     ).astype(jnp.bfloat16)
@@ -106,32 +117,40 @@
         "bpo,boc->bpc", grad_rows, weights, preferred_element_type=jnp.float32
     ).reshape(pairs, width_in)
     fine_sum = exact_sum(fine_hot, grad_in)
-    fine_grad = lax.psum_scatter(fine_sum, "ch", scatter_dimension=1, tiled=True)
-    grad_features = jnp.where(live_mask[:, None], fine_grad, jnp.zeros((), jnp.float32)).astype(
-        jnp.bfloat16
-    )
     grad_weight = jnp.einsum(
         "bpc,bpo->boc", gathered, grad_rows, preferred_element_type=jnp.float32
     )
     weight_sum = (
         jnp.zeros((offsets_all, width_out, width_in), jnp.float32).at[block_offset].add(grad_weight)
     )
+    fine_sum, weight_sum = lax.optimization_barrier((fine_sum, weight_sum))
+    fine_grad = lax.psum_scatter(fine_sum, "ch", scatter_dimension=1, tiled=True)
+    grad_features = jnp.where(live_mask[:, None], fine_grad, jnp.zeros((), jnp.float32)).astype(
+        jnp.bfloat16
+    )
     factor = math.sqrt(offsets_all / (blocks * group * owners))
-    grad_kernel = reduce_replicate(weight_sum, owners, factor)
+    grad_kernel = reduce_replicate(weight_sum, sizes, factor)
     return (activation.T, grad_features.T, grad_kernel)
 
 
 def solution(mesh):
+    vox = mesh.shape["vox"]
+    cores = 2
+    across = 4
+    split = jax.sharding.Mesh(
+        mesh.devices.reshape(vox // (cores * across), across, cores, mesh.shape["ch"]),
+        VOX + ("ch",),
+    )
     in_specs = (
-        P("vox", None),
+        P(VOX, None),
         P(None, "ch", None),
-        P("ch", "vox"),
-        P("vox"),
-        P("vox"),
-        P("vox"),
-        P("vox", None),
-        P("vox"),
-        P("vox"),
+        P("ch", VOX),
+        P(VOX),
+        P(VOX),
+        P(VOX),
+        P(VOX, None),
+        P(VOX),
+        P(VOX),
     )
-    out_specs = (P("ch", "vox"), P("ch", "vox"), P(None, "ch", None))
-    return jax.shard_map(body, mesh=mesh, in_specs=in_specs, out_specs=out_specs, check_vma=False)
+    out_specs = (P("ch", VOX), P("ch", VOX), P(None, "ch", None))
+    return jax.shard_map(body, mesh=split, in_specs=in_specs, out_specs=out_specs, check_vma=False)

time: 205 us -> 182 us (0.89)
  waiting for transfers between devices: 78.5 us -> 10.7 us
  blocking collectives: 59.8 us -> 116 us
  starting transfers between devices: 17.3 us -> 6.89 us
    all_to_all x2 -> x10, blocking collectives: 59.8 us -> 116 us  [the longest x6 68.6 us: staged_all_to_all(): x = lax.all_to_all(x, name, axis, axis, tiled=True)]
    all_to_all x2, waiting for transfers between devices: 50 us -> 10.7 us  [the longest x1 7.42 us: reduce_replicate(): part = lax.all_to_all(part, name, axis, axis, tiled=True).sum(axis=axis)]
    unnamed x2, waiting for transfers between devices: 28.4 us -> 0.04 us
    all_to_all x2, starting transfers between devices: 17 us -> 6.85 us  [the longest x1 3.46 us: reduce_replicate(): part = lax.all_to_all(part, name, axis, axis, tiled=True).sum(axis=axis)]
  transfers between devices with their start and end apart: 3 -> 3, of which waited for: 2 -> 2; matrix products, arithmetic and copies ran while one was open for 5% -> 2% of each run, Pallas kernels for 0% -> 0%
where the time goes in v4:
time: 182 us; the launch traced here: 181 us
  blocking collectives  116 us (64%)
  matrix products  17.6 us (10%)
  between operations  15.1 us (8%)
  waiting for transfers between devices  10.7 us (6%)
  local copies, waits for them, and re-layouts  8.29 us (5%)
  other arithmetic  7.1 us (4%)
  starting transfers between devices  6.89 us (4%)
    all_to_all x6, blocking collectives, staged_all_to_all(): x = lax.all_to_all(x, name, axis, axis, tiled=True)  68.6 us
    all_to_all x2, blocking collectives, reduce_replicate(): mine = lax.all_to_all(mine, name, 0, 0, tiled=True)  25 us
    all_to_all x2, blocking collectives, reduce_replicate(): part = lax.all_to_all(part, name, axis, axis, tiled=True).sum(axis=axis)  22.1 us
    all_to_all x1, waiting for transfers between devices, reduce_replicate(): part = lax.all_to_all(part, name, axis, axis, tiled=True).sum(axis=axis)  7.42 us
    dot_general x2, matrix products, exact_sum(): jnp.einsum('pt,pc->tc', onehot, both, preferred_element_type=jnp.float32)  6.63 us
  transfers between devices with their start and end apart: 3, of which 2 were waited for; matrix products, arithmetic and copies ran while one was open for 2% of the time, Pallas kernels for 0%

profile of v4, /device:TPU:1, one launch (start us, length us, event | category | flops | bytes accessed | tf_op | source)
XLA Modules:
  0.0 181.4 jit_solution(13474200455317499685)
XLA Ops:
  7.9 0.7 compare_select_fusion
  8.6 0.8 copy.61
  9.4 0.2 fusion.41
  9.7 0.9 fusion.39
  10.6 0.7 multiply_add_fusion
  11.3 0.6 gather_fusion
  12.0 3.1 %fusion.6 = bf16[4096,128]{1,0:T(8,128)(2,1)S(1)} fusion(s32[4096]{0:T(1024)S(1)} %copy-done.6, bf16[1024,128]{1,0:T(8,128)(2,1)S(1)} %copy-done.3, pred[1024]{0:T(1024)(128)(4,1)S(1)} %iota_compare_fusion.29), kind=kOutput, calls=%fused_computation.10 | convolution fusion | flops 1078591488 | bytes 1328128 | tf_op jit(solution)/shard_map/dot_general | solution.py:81
  15.1 0.8 convolution_bitcast_fusion
  15.9 0.2 reduce-precision_convert_fusion.1
  16.1 1.5 fusion.5
  17.6 0.5 fusion.20
  18.1 0.2 copy.64
  18.2 0.2 reshape.75
  18.5 10.3 %all_to_all.60 = bf16[16,4,2,3,128]{4,0,3,1,2:T(8,128)(2,1)S(1)} all-to-all(bf16[16,4,2,3,128]{4,0,3,1,2:T(8,128)(2,1)S(1)} %copy.65), channel_id=1, replica_groups=mesh['z'=16,'y'=4,'core'=2,'ch'=4] {'core'}, dimensions={2} | all-to-all | bytes 196608 | tf_op jit(solution)/shard_map/all_to_all | solution.py:34
  28.8 7.0 %all_to_all.61 = bf16[16,4,2,3,128]{4,0,3,2,1:T(8,128)(2,1)S(1)} all-to-all(bf16[16,4,2,3,128]{4,0,3,2,1:T(8,128)(2,1)S(1)} %copy.66), channel_id=1, replica_groups=mesh['z'=16,'y'=4,'core'=2,'ch'=4] {'y'}, dimensions={1} | all-to-all | bytes 196608 | tf_op jit(solution)/shard_map/all_to_all | solution.py:34
  35.9 22.8 %all_to_all.62 = bf16[16,4,2,3,128]{4,1,3,2,0:T(4,128)(2,1)S(1)} all-to-all(bf16[16,4,2,3,128]{4,1,3,2,0:T(4,128)(2,1)S(1)} %copy.67), channel_id=1, replica_groups=mesh['z'=16,'y'=4,'core'=2,'ch'=4] {'z'}, dimensions={0} | all-to-all | bytes 196608 | tf_op jit(solution)/shard_map/all_to_all | solution.py:34
  58.7 0.1 reshape.76
  58.9 1.2 fusion.52
  60.0 0.5 fusion.19
  60.5 0.2 copy.69
  60.7 0.2 reshape.77
  61.0 6.7 %all_to_all.63 = bf16[16,4,2,3,128]{4,0,3,1,2:T(8,128)(2,1)S(1)} all-to-all(bf16[16,4,2,3,128]{4,0,3,1,2:T(8,128)(2,1)S(1)} %copy.70), channel_id=1, replica_groups=mesh['z'=16,'y'=4,'core'=2,'ch'=4] {'core'}, dimensions={2} | all-to-all | bytes 196608 | tf_op jit(solution)/shard_map/all_to_all | solution.py:34
  67.7 7.0 %all_to_all.64 = bf16[16,4,2,3,128]{4,0,3,2,1:T(8,128)(2,1)S(1)} all-to-all(bf16[16,4,2,3,128]{4,0,3,2,1:T(8,128)(2,1)S(1)} %copy.71), channel_id=1, replica_groups=mesh['z'=16,'y'=4,'core'=2,'ch'=4] {'y'}, dimensions={1} | all-to-all | bytes 196608 | tf_op jit(solution)/shard_map/all_to_all | solution.py:34
  74.7 14.8 %all_to_all.65 = bf16[16,4,2,3,128]{4,1,3,2,0:T(4,128)(2,1)S(1)} all-to-all(bf16[16,4,2,3,128]{4,1,3,2,0:T(4,128)(2,1)S(1)} %copy.72), channel_id=1, replica_groups=mesh['z'=16,'y'=4,'core'=2,'ch'=4] {'z'}, dimensions={0} | all-to-all | bytes 196608 | tf_op jit(solution)/shard_map/all_to_all | solution.py:34
  89.6 0.1 reshape.78
  89.7 2.9 %fusion.18 = bf16[8,32,8,128]{3,2,1,0:T(8,128)(2,1)} fusion(s32[4096]{0:T(1024)S(1)} %copy-done.5, bf16[768,64]{1,0:T(8,128)(2,1)S(1)} %reshape.78, s32[512]{0:T(512)S(1)} %bitcast.82), kind=kOutput, calls=%fused_computation.29 | convolution fusion | flops 321552384 | bytes 641024 | tf_op jit(solution)/shard_map/pt,to->po/dot_general | solution.py:112
  92.6 1.5 fusion.31
  94.2 0.5 fusion.33
  94.7 0.3 reduce-precision_convert_fusion
  95.0 5.1 %fusion = f32[1024,256]{1,0:T(8,128)S(1)} fusion(s32[4096]{0:T(1024)S(1)} %copy-done.6, bf16[4096,128]{1,0:T(8,128)(2,1)S(1)} %get-tuple-element.23, bf16[4096,128]{1,0:T(8,128)(2,1)S(1)} %get-tuple-element.22), kind=kOutput, calls=%fused_computation.3 | convolution fusion | flops 2155872256 | bytes 3162112 | tf_op jit(solution)/shard_map/pt,pc->tc/dot_general | solution.py:24
  100.1 0.8 slice_add_fusion
  101.1 2.1 %scatter_fusion = f32[27,64,128]{2,1,0:T(8,128)S(1)} fusion(f32[27,64,128]{2,1,0:T(8,128)S(1)} %broadcast_in_dim.38, s32[32]{0:T(128)S(1)} %compare_select_fusion, f32[32,64,128]{2,1,0:T(8,128)S(1)} %fusion.31), kind=kCustom, calls=%fused_computation.1 | custom fusion | flops 262144 | bytes 3145856 | tf_op jit(solution)/shard_map/scatter-add | solution.py:124
  103.4 0.5 copy.76
  103.9 7.3 %all_to_all.66 = f32[16,4,2,14,128]{4,0,3,1,2:T(8,128)S(1)} all-to-all(f32[16,4,2,14,128]{4,0,3,1,2:T(8,128)S(1)} %copy.76), channel_id=1, replica_groups=mesh['z'=16,'y'=4,'core'=2,'ch'=4] {'core'}, dimensions={2} | all-to-all | bytes 1835008 | tf_op jit(solution)/shard_map/all_to_all | solution.py:46
  111.2 0.8 reduce_sum.40
  112.1 3.5 %all-to-all-start.7 = ((f32[16,4,14,128]{3,0,2,1:T(8,128)}), f32[16,4,14,128]{3,0,2,1:T(8,128)S(1)}, u32[]{:S(2)}, u32[]{:S(2)}) async-start(f32[16,4,14,128]{3,0,2,1:T(8,128)} %reduce_sum.40), calls=%async_computation.7 | async-start | bytes 917504 | tf_op jit(solution)/shard_map/all_to_all | solution.py:46
  115.6 1.0 copy.81
  116.6 7.4 %all-to-all-done.7 = f32[16,4,14,128]{3,0,2,1:T(8,128)S(1)} async-done(((f32[16,4,14,128]{3,0,2,1:T(8,128)}), f32[16,4,14,128]{3,0,2,1:T(8,128)S(1)}, u32[]{:S(2)}, u32[]{:S(2)}) %all-to-all-start.7) | async-done | bytes 458784 | tf_op jit(solution)/shard_map/all_to_all | solution.py:46
  124.1 14.8 %all_to_all.67 = f32[16,14,128]{2,1,0:T(8,128)S(1)} all-to-all(f32[16,14,128]{2,1,0:T(8,128)S(1)} %copy.77), channel_id=1, replica_groups=mesh['z'=16,'y'=4,'core'=2,'ch'=4] {'z'}, dimensions={0} | all-to-all | bytes 229376 | tf_op jit(solution)/shard_map/all_to_all | solution.py:46
  139.0 16.8 %all_to_all.68 = bf16[16,14,128]{2,1,0:T(8,128)(2,1)S(1)} all-to-all(bf16[16,14,128]{2,1,0:T(8,128)(2,1)S(1)} %broadcast_in_dim.40), channel_id=1, replica_groups=mesh['z'=16,'y'=4,'core'=2,'ch'=4] {'z'}, dimensions={0} | all-to-all | bytes 114688 | tf_op jit(solution)/shard_map/all_to_all | solution.py:50
  155.8 0.7 broadcast_in_dim.41
  156.5 3.4 %all-to-all-start.10 = ((bf16[4,16,14,128]{3,1,2,0:T(8,128)(2,1)}), bf16[4,16,14,128]{3,1,2,0:T(8,128)(2,1)S(1)}, u32[]{:S(2)}, u32[]{:S(2)}) async-start(bf16[4,16,14,128]{3,1,2,0:T(8,128)(2,1)} %broadcast_in_dim.41), calls=%async_computation.10 | async-start | bytes 458752 | tf_op jit(solution)/shard_map/all_to_all | solution.py:50
  159.9 1.1 copy.82
  161.0 0.2 fusion.37
  161.2 0.8 copy.80
  162.0 3.2 %all-to-all-done.10 = bf16[4,16,14,128]{3,1,2,0:T(8,128)(2,1)S(1)} async-done(((bf16[4,16,14,128]{3,1,2,0:T(8,128)(2,1)}), bf16[4,16,14,128]{3,1,2,0:T(8,128)(2,1)S(1)}, u32[]{:S(2)}, u32[]{:S(2)}) %all-to-all-start.10) | async-done | bytes 229408 | tf_op jit(solution)/shard_map/all_to_all | solution.py:50
  165.3 8.2 %all_to_all.69 = bf16[2,4,16,14,128]{4,2,3,1,0:T(8,128)(2,1)S(1)} all-to-all(bf16[2,4,16,14,128]{4,2,3,1,0:T(8,128)(2,1)S(1)} %broadcast_in_dim.68), channel_id=1, replica_groups=mesh['z'=16,'y'=4,'core'=2,'ch'=4] {'core'}, dimensions={0} | all-to-all | bytes 917504 | tf_op jit(solution)/shard_map/all_to_all | solution.py:50
  173.8 0.8 slice.35
  (47 shorter events, 1.2 us)
Async XLA Ops:
  7.2 4.1 %copy-start = (bf16[27,64,128]{2,1,0:T(8,128)(2,1)S(1)}, bf16[27,64,128]{2,1,0:T(8,128)(2,1)}, u32[]{:S(2)}) copy-start(bf16[27,64,128]{2,1,0:T(8,128)(2,1)} %param.10) | copy-start | bytes 1327108
  7.2 4.8 %copy-start.6 = (s32[4096]{0:T(1024)S(1)}, s32[4096]{0:T(1024)}, u32[]{:S(2)}) copy-start(s32[4096]{0:T(1024)} %param.12) | copy-start | bytes 49156
  7.2 4.8 %copy-start.3 = (bf16[1024,128]{1,0:T(8,128)(2,1)S(1)}, bf16[1024,128]{1,0:T(8,128)(2,1)}, u32[]{:S(2)}) copy-start(bf16[1024,128]{1,0:T(8,128)(2,1)} %param.9) | copy-start | bytes 786436
  15.1 1.0 copy-start.5
  17.6 41.3 %copy-start.7 = (s32[768]{0:T(1024)S(1)}, s32[768]{0:T(1024)}, u32[]{:S(2)}) copy-start(s32[768]{0:T(1024)} %param.16) | copy-start | bytes 9220
  17.6 42.4 %copy-start.4 = (bf16[64,512]{1,0:T(8,128)(2,1)S(1)}, bf16[64,512]{1,0:T(8,128)(2,1)}, u32[]{:S(2)}) copy-start(bf16[64,512]{1,0:T(8,128)(2,1)} %param.11) | copy-start | bytes 196612
  92.6 1.5 copy-start.2
  103.9 11.7 %copy-start.1 = (f32[1024,128]{1,0:T(8,128)S(1)}, f32[1024,128]{1,0:T(8,128)}, u32[]{:S(2)}) copy-start(f32[1024,128]{1,0:T(8,128)} %slice_add_fusion) | copy-start | bytes 1572868
  112.1 12.0 %all-to-all-start.7 = ((f32[16,4,14,128]{3,0,2,1:T(8,128)}), f32[16,4,14,128]{3,0,2,1:T(8,128)S(1)}, u32[]{:S(2)}, u32[]{:S(2)}) async-start(f32[16,4,14,128]{3,0,2,1:T(8,128)} %reduce_sum.40), calls=%async_computation.7 | async-start | bytes 917504 | tf_op jit(solution)/shard_map/all_to_all | solution.py:46
  115.5 44.4 %reduce-scatter.4.cloned.1.call-start = ((), (), s32[]{:S(2)}) async-start(), calls=%async_computation.13 | async-start | bytes 655360
  156.5 8.7 %all-to-all-start.10 = ((bf16[4,16,14,128]{3,1,2,0:T(8,128)(2,1)}), bf16[4,16,14,128]{3,1,2,0:T(8,128)(2,1)S(1)}, u32[]{:S(2)}, u32[]{:S(2)}) async-start(bf16[4,16,14,128]{3,1,2,0:T(8,128)(2,1)} %broadcast_in_dim.41), calls=%async_computation.10 | async-start | bytes 458752 | tf_op jit(solution)/shard_map/all_to_all | solution.py:50
Sparse Core Ops, SparseCore 0:
  119.2 20.1 reduce-scatter.3

commit v5 on v4

--- a/solution.py
+++ b/solution.py
@@ -29,10 +29,8 @@
 VOX = ("z", "y", "core")
 
 
-def staged_all_to_all(x):
-    for axis, name in ((2, "core"), (1, "y"), (0, "z")):
-        x = lax.all_to_all(x, name, axis, axis, tiled=True)
-    return x
+def flat_all_to_all(x):
+    return lax.all_to_all(x, VOX, 0, 0, tiled=True)
 
 
 def reduce_replicate(weight_sum, sizes, factor):
@@ -92,8 +90,8 @@
     send_rows = jnp.einsum(
         "ts,to->so", slot_hot, target_part, preferred_element_type=jnp.float32
     ).astype(jnp.bfloat16)
-    lane_shape = (*sizes, capacity * width_out // 128, 128)
-    received = staged_all_to_all(send_rows.reshape(lane_shape))
+    lane_shape = (slots * width_out // 128, 128)
+    received = flat_all_to_all(send_rows.reshape(lane_shape))
     got_rows = received.reshape(slots, width_out)
     row_hot = one_hot(slot_coarse_row, coarse_total)
     coarse = jnp.einsum("sc,so->co", row_hot, got_rows, preferred_element_type=jnp.float32)
@@ -105,7 +103,7 @@
     back_rows = jnp.einsum(
         "sc,co->so", row_hot, grad_coarse, preferred_element_type=jnp.float32
     ).astype(jnp.bfloat16)
-    returned = staged_all_to_all(back_rows.reshape(lane_shape))
+    returned = flat_all_to_all(back_rows.reshape(lane_shape))
     grad_target = jnp.einsum(
         "ts,so->to", slot_hot, returned.reshape(slots, width_out), preferred_element_type=jnp.float32
     ).astype(jnp.bfloat16)

time: 182 us -> 171 us (0.940)
  blocking collectives: 116 us -> 106 us
    all_to_all x6 -> x2, blocking collectives: 68.6 us -> 59.8 us  [flat_all_to_all(): return lax.all_to_all(x, VOX, 0, 0, tiled=True)]
where the time goes in v5:
time: 171 us
  blocking collectives  106 us (62%)
  matrix products  17.6 us (10%)
  between operations  15 us (9%)
  waiting for transfers between devices  10.5 us (6%)
  local copies, waits for them, and re-layouts  7.96 us (5%)
  starting transfers between devices  7.11 us (4%)
  other arithmetic  7.1 us (4%)
    all_to_all x2, blocking collectives, flat_all_to_all(): return lax.all_to_all(x, VOX, 0, 0, tiled=True)  59.8 us
    all_to_all x2, blocking collectives, reduce_replicate(): mine = lax.all_to_all(mine, name, 0, 0, tiled=True)  25 us
    all_to_all x2, blocking collectives, reduce_replicate(): part = lax.all_to_all(part, name, axis, axis, tiled=True).sum(axis=axis)  20.8 us
    all_to_all x1, waiting for transfers between devices, reduce_replicate(): part = lax.all_to_all(part, name, axis, axis, tiled=True).sum(axis=axis)  7.18 us
    dot_general x2, matrix products, exact_sum(): jnp.einsum('pt,pc->tc', onehot, both, preferred_element_type=jnp.float32)  6.64 us
    all_to_all x1, starting transfers between devices, reduce_replicate(): part = lax.all_to_all(part, name, axis, axis, tiled=True).sum(axis=axis)  3.72 us
  transfers between devices with their start and end apart: 3, of which 2 were waited for; matrix products, arithmetic and copies ran while one was open for 2% of the time, Pallas kernels for 0%

profile of v5, /device:TPU:1, one launch (start us, length us, event | category | flops | bytes accessed | tf_op | source)
XLA Modules:
  0.0 170.9 jit_solution(6817582062667711956)
XLA Ops:
  7.9 0.7 compare_select_fusion
  8.6 0.8 copy.45
  9.4 0.2 fusion.41
  9.7 0.9 fusion.39
  10.6 0.7 multiply_add_fusion
  11.3 0.6 gather_fusion
  12.0 3.1 %fusion.6 = bf16[4096,128]{1,0:T(8,128)(2,1)S(1)} fusion(s32[4096]{0:T(1024)S(1)} %copy-done.6, bf16[1024,128]{1,0:T(8,128)(2,1)S(1)} %copy-done.3, pred[1024]{0:T(1024)(128)(4,1)S(1)} %iota_compare_fusion.29), kind=kOutput, calls=%fused_computation.10 | convolution fusion | flops 1078591488 | bytes 1328128 | tf_op jit(solution)/shard_map/dot_general | solution.py:79
  15.1 0.8 convolution_bitcast_fusion
  15.9 0.2 reduce-precision_convert_fusion.1
  16.1 1.5 fusion.5
  17.6 0.5 fusion.20
  18.1 0.2 copy.48
  18.2 0.2 all_to_all.30
  18.4 36.8 %all_to_all.48 = bf16[128,3,128]{2,1,0:T(4,128)(2,1)S(1)} all-to-all(bf16[128,3,128]{2,1,0:T(4,128)(2,1)S(1)} %all_to_all.30), channel_id=1, replica_groups=mesh['z'=16,'y'=4,'core'=2,'ch'=4] {'z','y','core'}, dimensions={0} | all-to-all | bytes 196608 | tf_op jit(solution)/shard_map/all_to_all | solution.py:33
  55.2 0.1 reshape.79
  55.3 1.2 fusion.52
  56.5 0.5 fusion.19
  57.0 0.2 copy.49
  57.2 0.2 all_to_all.32
  57.4 23.1 %all_to_all.49 = bf16[128,3,128]{2,1,0:T(4,128)(2,1)S(1)} all-to-all(bf16[128,3,128]{2,1,0:T(4,128)(2,1)S(1)} %all_to_all.32), channel_id=1, replica_groups=mesh['z'=16,'y'=4,'core'=2,'ch'=4] {'z','y','core'}, dimensions={0} | all-to-all | bytes 196608 | tf_op jit(solution)/shard_map/all_to_all | solution.py:33
  80.4 0.1 reshape.80
  80.6 2.9 %fusion.18 = bf16[8,32,8,128]{3,2,1,0:T(8,128)(2,1)} fusion(s32[4096]{0:T(1024)S(1)} %copy-done.5, bf16[768,64]{1,0:T(8,128)(2,1)S(1)} %reshape.80, s32[512]{0:T(512)S(1)} %bitcast.82), kind=kOutput, calls=%fused_computation.29 | convolution fusion | flops 321552384 | bytes 641024 | tf_op jit(solution)/shard_map/pt,to->po/dot_general | solution.py:110
  83.5 1.5 fusion.31
  85.0 0.5 fusion.33
  85.5 0.3 reduce-precision_convert_fusion
  85.8 5.1 %fusion = f32[1024,256]{1,0:T(8,128)S(1)} fusion(s32[4096]{0:T(1024)S(1)} %copy-done.6, bf16[4096,128]{1,0:T(8,128)(2,1)S(1)} %get-tuple-element.23, bf16[4096,128]{1,0:T(8,128)(2,1)S(1)} %get-tuple-element.22), kind=kOutput, calls=%fused_computation.3 | convolution fusion | flops 2155872256 | bytes 3162112 | tf_op jit(solution)/shard_map/pt,pc->tc/dot_general | solution.py:24
  91.0 0.8 slice_add_fusion
  91.8 0.1 broadcast_in_dim.38
  91.9 2.1 %scatter_fusion = f32[27,64,128]{2,1,0:T(8,128)S(1)} fusion(f32[27,64,128]{2,1,0:T(8,128)S(1)} %broadcast_in_dim.38, s32[32]{0:T(128)S(1)} %compare_select_fusion, f32[32,64,128]{2,1,0:T(8,128)S(1)} %fusion.31), kind=kCustom, calls=%fused_computation.1 | custom fusion | flops 262144 | bytes 3145856 | tf_op jit(solution)/shard_map/scatter-add | solution.py:122
  94.1 0.1 reshape.84
  94.2 0.5 copy.52
  94.8 4.6 %all_to_all.50 = f32[16,4,2,14,128]{4,0,3,1,2:T(8,128)S(1)} all-to-all(f32[16,4,2,14,128]{4,0,3,1,2:T(8,128)S(1)} %copy.52), channel_id=1, replica_groups=mesh['z'=16,'y'=4,'core'=2,'ch'=4] {'core'}, dimensions={2} | all-to-all | bytes 1835008 | tf_op jit(solution)/shard_map/all_to_all | solution.py:44
  99.4 0.8 reduce_sum.40
  100.3 3.7 %all-to-all-start.3 = ((f32[16,4,14,128]{3,0,2,1:T(8,128)}), f32[16,4,14,128]{3,0,2,1:T(8,128)S(1)}, u32[]{:S(2)}, u32[]{:S(2)}) async-start(f32[16,4,14,128]{3,0,2,1:T(8,128)} %reduce_sum.40), calls=%async_computation.3 | async-start | bytes 917504 | tf_op jit(solution)/shard_map/all_to_all | solution.py:44
  104.0 1.0 copy.57
  105.0 7.2 %all-to-all-done.3 = f32[16,4,14,128]{3,0,2,1:T(8,128)S(1)} async-done(((f32[16,4,14,128]{3,0,2,1:T(8,128)}), f32[16,4,14,128]{3,0,2,1:T(8,128)S(1)}, u32[]{:S(2)}, u32[]{:S(2)}) %all-to-all-start.3) | async-done | bytes 458784 | tf_op jit(solution)/shard_map/all_to_all | solution.py:44
  112.3 16.2 %all_to_all.51 = f32[16,14,128]{2,1,0:T(8,128)S(1)} all-to-all(f32[16,14,128]{2,1,0:T(8,128)S(1)} %copy.53), channel_id=1, replica_groups=mesh['z'=16,'y'=4,'core'=2,'ch'=4] {'z'}, dimensions={0} | all-to-all | bytes 229376 | tf_op jit(solution)/shard_map/all_to_all | solution.py:44
  128.5 16.8 %all_to_all.52 = bf16[16,14,128]{2,1,0:T(8,128)(2,1)S(1)} all-to-all(bf16[16,14,128]{2,1,0:T(8,128)(2,1)S(1)} %broadcast_in_dim.40), channel_id=1, replica_groups=mesh['z'=16,'y'=4,'core'=2,'ch'=4] {'z'}, dimensions={0} | all-to-all | bytes 114688 | tf_op jit(solution)/shard_map/all_to_all | solution.py:48
  145.3 0.7 broadcast_in_dim.41
  146.0 3.4 %all-to-all-start.6 = ((bf16[4,16,14,128]{3,1,2,0:T(8,128)(2,1)}), bf16[4,16,14,128]{3,1,2,0:T(8,128)(2,1)S(1)}, u32[]{:S(2)}, u32[]{:S(2)}) async-start(bf16[4,16,14,128]{3,1,2,0:T(8,128)(2,1)} %broadcast_in_dim.41), calls=%async_computation.6 | async-start | bytes 458752 | tf_op jit(solution)/shard_map/all_to_all | solution.py:48
  149.4 1.1 copy.58
  150.5 0.2 fusion.37
  150.7 0.8 copy.56
  151.5 3.2 %all-to-all-done.6 = bf16[4,16,14,128]{3,1,2,0:T(8,128)(2,1)S(1)} async-done(((bf16[4,16,14,128]{3,1,2,0:T(8,128)(2,1)}), bf16[4,16,14,128]{3,1,2,0:T(8,128)(2,1)S(1)}, u32[]{:S(2)}, u32[]{:S(2)}) %all-to-all-start.6) | async-done | bytes 229408 | tf_op jit(solution)/shard_map/all_to_all | solution.py:48
  154.8 8.2 %all_to_all.53 = bf16[2,4,16,14,128]{4,2,3,1,0:T(8,128)(2,1)S(1)} all-to-all(bf16[2,4,16,14,128]{4,2,3,1,0:T(8,128)(2,1)S(1)} %broadcast_in_dim.68), channel_id=1, replica_groups=mesh['z'=16,'y'=4,'core'=2,'ch'=4] {'core'}, dimensions={0} | all-to-all | bytes 917504 | tf_op jit(solution)/shard_map/all_to_all | solution.py:48
  163.0 0.1 copy.55
  163.1 0.1 reshape.85
  163.2 0.8 slice.35
  (35 shorter events, 0.4 us)
Async XLA Ops:
  7.2 4.1 %copy-start = (bf16[27,64,128]{2,1,0:T(8,128)(2,1)S(1)}, bf16[27,64,128]{2,1,0:T(8,128)(2,1)}, u32[]{:S(2)}) copy-start(bf16[27,64,128]{2,1,0:T(8,128)(2,1)} %param.10) | copy-start | bytes 1327108
  7.2 4.8 %copy-start.6 = (s32[4096]{0:T(1024)S(1)}, s32[4096]{0:T(1024)}, u32[]{:S(2)}) copy-start(s32[4096]{0:T(1024)} %param.12) | copy-start | bytes 49156
  7.2 4.8 %copy-start.3 = (bf16[1024,128]{1,0:T(8,128)(2,1)S(1)}, bf16[1024,128]{1,0:T(8,128)(2,1)}, u32[]{:S(2)}) copy-start(bf16[1024,128]{1,0:T(8,128)(2,1)} %param.9) | copy-start | bytes 786436
  15.1 1.0 copy-start.5
  16.1 39.3 %copy-start.7 = (s32[768]{0:T(1024)S(1)}, s32[768]{0:T(1024)}, u32[]{:S(2)}) copy-start(s32[768]{0:T(1024)} %param.16) | copy-start | bytes 9220
  17.6 38.9 %copy-start.4 = (bf16[64,512]{1,0:T(8,128)(2,1)S(1)}, bf16[64,512]{1,0:T(8,128)(2,1)}, u32[]{:S(2)}) copy-start(bf16[64,512]{1,0:T(8,128)(2,1)} %param.11) | copy-start | bytes 196612
  83.5 1.5 copy-start.2
  94.8 9.2 %copy-start.1 = (f32[1024,128]{1,0:T(8,128)S(1)}, f32[1024,128]{1,0:T(8,128)}, u32[]{:S(2)}) copy-start(f32[1024,128]{1,0:T(8,128)} %slice_add_fusion) | copy-start | bytes 1572868
  100.3 11.9 %all-to-all-start.3 = ((f32[16,4,14,128]{3,0,2,1:T(8,128)}), f32[16,4,14,128]{3,0,2,1:T(8,128)S(1)}, u32[]{:S(2)}, u32[]{:S(2)}) async-start(f32[16,4,14,128]{3,0,2,1:T(8,128)} %reduce_sum.40), calls=%async_computation.3 | async-start | bytes 917504 | tf_op jit(solution)/shard_map/all_to_all | solution.py:44
  104.0 45.4 %reduce-scatter.4.cloned.1.call-start = ((), (), s32[]{:S(2)}) async-start(), calls=%async_computation.9 | async-start | bytes 655360
  146.0 8.7 %all-to-all-start.6 = ((bf16[4,16,14,128]{3,1,2,0:T(8,128)(2,1)}), bf16[4,16,14,128]{3,1,2,0:T(8,128)(2,1)S(1)}, u32[]{:S(2)}, u32[]{:S(2)}) async-start(bf16[4,16,14,128]{3,1,2,0:T(8,128)(2,1)} %broadcast_in_dim.41), calls=%async_computation.6 | async-start | bytes 458752 | tf_op jit(solution)/shard_map/all_to_all | solution.py:48
Sparse Core Ops, SparseCore 0:
  107.6 21.2 reduce-scatter.3

commit v6 on v5

--- a/solution.py
+++ b/solution.py
@@ -36,17 +36,19 @@
 def reduce_replicate(weight_sum, sizes, factor):
     shape = weight_sum.shape
     owners = math.prod(sizes)
+    near = owners // sizes[0]
     rows = weight_sum.size // 128
     chunk = -(-rows // owners)
     flat = jnp.pad(weight_sum.reshape(rows, 128), ((0, chunk * owners - rows), (0, 0)))
-    part = flat.reshape(*sizes, chunk, 128)
-    for axis, name in ((2, "core"), (1, "y"), (0, "z")):
-        part = lax.all_to_all(part, name, axis, axis, tiled=True).sum(axis=axis)
+    part = flat.reshape(sizes[0], near, chunk, 128)
+    part = lax.all_to_all(part, VOX[1:], 1, 1, tiled=True).sum(axis=1)
+    part = lax.all_to_all(part, VOX[0], 0, 0, tiled=True).sum(axis=0)
     mine = (part * factor).astype(jnp.bfloat16)
-    for axis, name in ((0, "z"), (1, "y"), (2, "core")):
-        mine = jnp.broadcast_to(mine[None], (sizes[axis],) + mine.shape)
-        mine = lax.all_to_all(mine, name, 0, 0, tiled=True)
-    back = jnp.transpose(mine, (2, 1, 0, 3, 4)).reshape(owners * chunk, 128)
+    mine = jnp.broadcast_to(mine[None], (sizes[0], chunk, 128))
+    mine = lax.all_to_all(mine, VOX[0], 0, 0, tiled=True)
+    mine = jnp.broadcast_to(mine[None], (near, sizes[0], chunk, 128))
+    mine = lax.all_to_all(mine, VOX[1:], 0, 0, tiled=True)
+    back = jnp.transpose(mine, (1, 0, 2, 3)).reshape(owners * chunk, 128)
     return back[:rows].reshape(shape)
 
 

time: 171 us -> 171 us (level)
  blocking collectives: 106 us -> 92.4 us
  waiting for transfers between devices: 10.5 us -> 19.4 us
  starting transfers between devices: 7.11 us -> 10.9 us
    all_to_all x4 -> x2, blocking collectives: 45.8 us -> 32.5 us  [the longest x1 16.9 us: reduce_replicate(): mine = lax.all_to_all(mine, VOX[0], 0, 0, tiled=True)]
    all_to_all x2, waiting for transfers between devices: 10.4 us -> 19.4 us  [the longest x1 12.7 us: reduce_replicate(): part = lax.all_to_all(part, VOX[1:], 1, 1, tiled=True).sum(axis=1)]
    all_to_all x2, starting transfers between devices: 7.1 us -> 10.9 us  [the longest x1 6.55 us: reduce_replicate(): mine = lax.all_to_all(mine, VOX[1:], 0, 0, tiled=True)]
where the time goes in v6:
time: 171 us
  blocking collectives  92.4 us (54%)
  waiting for transfers between devices  19.4 us (11%)
  matrix products  17.6 us (10%)
  between operations  15 us (9%)
  starting transfers between devices  10.9 us (6%)
  local copies, waits for them, and re-layouts  8.95 us (5%)
  other arithmetic  6.3 us (4%)
    all_to_all x2, blocking collectives, flat_all_to_all(): return lax.all_to_all(x, VOX, 0, 0, tiled=True)  59.8 us
    all_to_all x1, blocking collectives, reduce_replicate(): mine = lax.all_to_all(mine, VOX[0], 0, 0, tiled=True)  16.9 us
    all_to_all x1, blocking collectives, reduce_replicate(): part = lax.all_to_all(part, VOX[0], 0, 0, tiled=True).sum(axis=0)  15.6 us
    all_to_all x1, waiting for transfers between devices, reduce_replicate(): part = lax.all_to_all(part, VOX[1:], 1, 1, tiled=True).sum(axis=1)  12.7 us
    all_to_all x1, waiting for transfers between devices, reduce_replicate(): mine = lax.all_to_all(mine, VOX[1:], 0, 0, tiled=True)  6.75 us
    dot_general x2, matrix products, exact_sum(): jnp.einsum('pt,pc->tc', onehot, both, preferred_element_type=jnp.float32)  6.64 us
    all_to_all x1, starting transfers between devices, reduce_replicate(): mine = lax.all_to_all(mine, VOX[1:], 0, 0, tiled=True)  6.55 us
    all_to_all x1, starting transfers between devices, reduce_replicate(): part = lax.all_to_all(part, VOX[1:], 1, 1, tiled=True).sum(axis=1)  4.39 us
  transfers between devices with their start and end apart: 3, of which 2 were waited for; matrix products, arithmetic and copies ran while one was open for 2% of the time, Pallas kernels for 0%

profile of v6, /device:TPU:1, one launch (start us, length us, event | category | flops | bytes accessed | tf_op | source)
XLA Modules:
  0.0 170.6 jit_solution(8972849100382588491)
XLA Ops:
  7.9 0.7 compare_select_fusion
  8.6 0.8 copy.45
  9.4 0.2 fusion.41
  9.7 0.9 fusion.39
  10.6 0.7 multiply_add_fusion
  11.3 0.6 gather_fusion
  12.0 3.1 %fusion.6 = bf16[4096,128]{1,0:T(8,128)(2,1)S(1)} fusion(s32[4096]{0:T(1024)S(1)} %copy-done.6, bf16[1024,128]{1,0:T(8,128)(2,1)S(1)} %copy-done.3, pred[1024]{0:T(1024)(128)(4,1)S(1)} %iota_compare_fusion.29), kind=kOutput, calls=%fused_computation.10 | convolution fusion | flops 1078591488 | bytes 1328128 | tf_op jit(solution)/shard_map/dot_general | solution.py:81
  15.1 0.8 convolution_bitcast_fusion
  15.9 0.2 reduce-precision_convert_fusion.1
  16.1 1.5 fusion.5
  17.6 0.5 fusion.20
  18.1 0.2 copy.48
  18.2 0.2 all_to_all.24
  18.4 36.8 %all_to_all.38 = bf16[128,3,128]{2,1,0:T(4,128)(2,1)S(1)} all-to-all(bf16[128,3,128]{2,1,0:T(4,128)(2,1)S(1)} %all_to_all.24), channel_id=1, replica_groups=mesh['z'=16,'y'=4,'core'=2,'ch'=4] {'z','y','core'}, dimensions={0} | all-to-all | bytes 196608 | tf_op jit(solution)/shard_map/all_to_all | solution.py:33
  55.2 0.1 reshape.78
  55.3 1.2 fusion.52
  56.5 0.5 fusion.19
  57.0 0.2 copy.49
  57.2 0.2 all_to_all.26
  57.4 23.1 %all_to_all.39 = bf16[128,3,128]{2,1,0:T(4,128)(2,1)S(1)} all-to-all(bf16[128,3,128]{2,1,0:T(4,128)(2,1)S(1)} %all_to_all.26), channel_id=1, replica_groups=mesh['z'=16,'y'=4,'core'=2,'ch'=4] {'z','y','core'}, dimensions={0} | all-to-all | bytes 196608 | tf_op jit(solution)/shard_map/all_to_all | solution.py:33
  80.4 0.1 reshape.79
  80.6 2.9 %fusion.18 = bf16[8,32,8,128]{3,2,1,0:T(8,128)(2,1)} fusion(s32[4096]{0:T(1024)S(1)} %copy-done.5, bf16[768,64]{1,0:T(8,128)(2,1)S(1)} %reshape.79, s32[512]{0:T(512)S(1)} %bitcast.82), kind=kOutput, calls=%fused_computation.29 | convolution fusion | flops 321552384 | bytes 641024 | tf_op jit(solution)/shard_map/pt,to->po/dot_general | solution.py:112
  83.5 1.5 fusion.31
  85.0 0.5 fusion.33
  85.5 0.3 reduce-precision_convert_fusion
  85.8 5.1 %fusion = f32[1024,256]{1,0:T(8,128)S(1)} fusion(s32[4096]{0:T(1024)S(1)} %copy-done.6, bf16[4096,128]{1,0:T(8,128)(2,1)S(1)} %get-tuple-element.23, bf16[4096,128]{1,0:T(8,128)(2,1)S(1)} %get-tuple-element.22), kind=kOutput, calls=%fused_computation.3 | convolution fusion | flops 2155872256 | bytes 3162112 | tf_op jit(solution)/shard_map/pt,pc->tc/dot_general | solution.py:24
  91.0 0.8 slice_add_fusion
  91.8 0.1 broadcast_in_dim.36
  91.9 2.1 %scatter_fusion = f32[27,64,128]{2,1,0:T(8,128)S(1)} fusion(f32[27,64,128]{2,1,0:T(8,128)S(1)} %broadcast_in_dim.36, s32[32]{0:T(128)S(1)} %compare_select_fusion, f32[32,64,128]{2,1,0:T(8,128)S(1)} %fusion.31), kind=kCustom, calls=%fused_computation.1 | custom fusion | flops 262144 | bytes 3145856 | tf_op jit(solution)/shard_map/scatter-add | solution.py:124
  94.1 0.1 pad.4
  94.1 0.1 reshape.83
  94.3 1.5 copy.52
  95.7 4.4 %all-to-all-start.2 = ((f32[16,8,14,128]{3,0,2,1:T(8,128)}), f32[16,8,14,128]{3,0,2,1:T(8,128)S(1)}, u32[]{:S(2)}, u32[]{:S(2)}) async-start(f32[16,8,14,128]{3,0,2,1:T(8,128)} %copy.52), calls=%async_computation.2 | async-start | bytes 1835008 | tf_op jit(solution)/shard_map/all_to_all | solution.py:44
  100.1 1.0 copy.57
  101.1 0.0 reduce-scatter.4.cloned.1.call-update
  101.1 12.7 %all-to-all-done.2 = f32[16,8,14,128]{3,0,2,1:T(8,128)S(1)} async-done(((f32[16,8,14,128]{3,0,2,1:T(8,128)}), f32[16,8,14,128]{3,0,2,1:T(8,128)S(1)}, u32[]{:S(2)}, u32[]{:S(2)}) %all-to-all-start.2) | async-done | bytes 917536 | tf_op jit(solution)/shard_map/all_to_all | solution.py:44
  113.8 0.1 reduce_sum.31
  113.9 15.6 %all_to_all.40 = f32[16,14,128]{2,1,0:T(8,128)S(1)} all-to-all(f32[16,14,128]{2,1,0:T(8,128)S(1)} %copy.53), channel_id=1, replica_groups=mesh['z'=16,'y'=4,'core'=2,'ch'=4] {'z'}, dimensions={0} | all-to-all | bytes 229376 | tf_op jit(solution)/shard_map/all_to_all | solution.py:45
  129.5 16.9 %all_to_all.41 = bf16[16,14,128]{2,1,0:T(8,128)(2,1)S(1)} all-to-all(bf16[16,14,128]{2,1,0:T(8,128)(2,1)S(1)} %broadcast_in_dim.60), channel_id=1, replica_groups=mesh['z'=16,'y'=4,'core'=2,'ch'=4] {'z'}, dimensions={0} | all-to-all | bytes 114688 | tf_op jit(solution)/shard_map/all_to_all | solution.py:48
  146.5 0.8 broadcast_in_dim.61
  147.3 6.6 %all-to-all-start.5 = ((bf16[8,16,14,128]{3,1,2,0:T(8,128)(2,1)}), bf16[8,16,14,128]{3,1,2,0:T(8,128)(2,1)S(1)}, u32[]{:S(2)}, u32[]{:S(2)}) async-start(bf16[8,16,14,128]{3,1,2,0:T(8,128)(2,1)} %broadcast_in_dim.61), calls=%async_computation.5 | async-start | bytes 917504 | tf_op jit(solution)/shard_map/all_to_all | solution.py:50
  153.9 1.1 copy.58
  155.0 0.2 fusion.37
  155.2 0.8 copy.56
  155.9 6.8 %all-to-all-done.5 = bf16[8,16,14,128]{3,1,2,0:T(8,128)(2,1)S(1)} async-done(((bf16[8,16,14,128]{3,1,2,0:T(8,128)(2,1)}), bf16[8,16,14,128]{3,1,2,0:T(8,128)(2,1)S(1)}, u32[]{:S(2)}, u32[]{:S(2)}) %all-to-all-start.5) | async-done | bytes 458784 | tf_op jit(solution)/shard_map/all_to_all | solution.py:50
  162.7 0.1 copy.55
  162.8 0.1 reshape.84
  163.0 0.8 slice.35
  (31 shorter events, 0.2 us)
Async XLA Ops:
  7.2 4.1 %copy-start = (bf16[27,64,128]{2,1,0:T(8,128)(2,1)S(1)}, bf16[27,64,128]{2,1,0:T(8,128)(2,1)}, u32[]{:S(2)}) copy-start(bf16[27,64,128]{2,1,0:T(8,128)(2,1)} %param.10) | copy-start | bytes 1327108
  7.2 4.8 %copy-start.6 = (s32[4096]{0:T(1024)S(1)}, s32[4096]{0:T(1024)}, u32[]{:S(2)}) copy-start(s32[4096]{0:T(1024)} %param.12) | copy-start | bytes 49156
  7.2 4.8 %copy-start.3 = (bf16[1024,128]{1,0:T(8,128)(2,1)S(1)}, bf16[1024,128]{1,0:T(8,128)(2,1)}, u32[]{:S(2)}) copy-start(bf16[1024,128]{1,0:T(8,128)(2,1)} %param.9) | copy-start | bytes 786436
  15.1 1.0 copy-start.5
  16.1 39.3 %copy-start.7 = (s32[768]{0:T(1024)S(1)}, s32[768]{0:T(1024)}, u32[]{:S(2)}) copy-start(s32[768]{0:T(1024)} %param.16) | copy-start | bytes 9220
  17.6 38.9 %copy-start.4 = (bf16[64,512]{1,0:T(8,128)(2,1)S(1)}, bf16[64,512]{1,0:T(8,128)(2,1)}, u32[]{:S(2)}) copy-start(bf16[64,512]{1,0:T(8,128)(2,1)} %param.11) | copy-start | bytes 196612
  83.5 1.5 copy-start.2
  94.2 5.9 %copy-start.1 = (f32[1024,128]{1,0:T(8,128)S(1)}, f32[1024,128]{1,0:T(8,128)}, u32[]{:S(2)}) copy-start(f32[1024,128]{1,0:T(8,128)} %slice_add_fusion) | copy-start | bytes 1572868
  95.7 18.1 %all-to-all-start.2 = ((f32[16,8,14,128]{3,0,2,1:T(8,128)}), f32[16,8,14,128]{3,0,2,1:T(8,128)S(1)}, u32[]{:S(2)}, u32[]{:S(2)}) async-start(f32[16,8,14,128]{3,0,2,1:T(8,128)} %copy.52), calls=%async_computation.2 | async-start | bytes 1835008 | tf_op jit(solution)/shard_map/all_to_all | solution.py:44
  100.1 53.8 %reduce-scatter.4.cloned.1.call-start = ((), (), s32[]{:S(2)}) async-start(), calls=%async_computation.7 | async-start | bytes 655360
  147.3 15.3 %all-to-all-start.5 = ((bf16[8,16,14,128]{3,1,2,0:T(8,128)(2,1)}), bf16[8,16,14,128]{3,1,2,0:T(8,128)(2,1)S(1)}, u32[]{:S(2)}, u32[]{:S(2)}) async-start(bf16[8,16,14,128]{3,1,2,0:T(8,128)(2,1)} %broadcast_in_dim.61), calls=%async_computation.5 | async-start | bytes 917504 | tf_op jit(solution)/shard_map/all_to_all | solution.py:50
Sparse Core Ops, SparseCore 0:
  103.8 20.4 reduce-scatter.3

commit v7 on v6

--- a/solution.py
+++ b/solution.py
@@ -120,10 +120,10 @@
     grad_weight = jnp.einsum(
         "bpc,bpo->boc", gathered, grad_rows, preferred_element_type=jnp.float32
     )
-    weight_sum = (
-        jnp.zeros((offsets_all, width_out, width_in), jnp.float32).at[block_offset].add(grad_weight)
+    offset_hot = one_hot(block_offset, offsets_all).astype(jnp.float32)
+    weight_sum = jnp.einsum(
+        "bk,boc->koc", offset_hot, grad_weight, precision=lax.Precision.HIGHEST
     )
-    fine_sum, weight_sum = lax.optimization_barrier((fine_sum, weight_sum))
     fine_grad = lax.psum_scatter(fine_sum, "ch", scatter_dimension=1, tiled=True)
     grad_features = jnp.where(live_mask[:, None], fine_grad, jnp.zeros((), jnp.float32)).astype(
         jnp.bfloat16

time: 171 us -> 171 us (level)
  local copies, waits for them, and re-layouts: 8.95 us -> 14.5 us
  waiting for transfers between devices: 19.4 us -> 14 us
  other arithmetic: 6.3 us -> 4.55 us
    all_to_all x1, waiting for transfers between devices: 12.7 us -> 7.24 us  [reduce_replicate(): part = lax.all_to_all(part, VOX[1:], 1, 1, tiled=True).sum(axis=1)]
    reshape x2, local copies, waits for them, and re-layouts: 1.55 us -> 4.96 us  [reduce_replicate(): part = flat.reshape(sizes[0], near, chunk, 128)]
    scatter-add x1 -> x0, other arithmetic: 2.14 us -> none  [body(): jnp.zeros((offsets_all, width_out, width_in), jnp.float32).at[block_offset]]
  transfers between devices with their start and end apart: 3 -> 3, of which waited for: 2 -> 2; matrix products, arithmetic and copies ran while one was open for 2% -> 6% of each run, Pallas kernels for 0% -> 0%
where the time goes in v7:
time: 171 us; the launch traced here: 170 us
  blocking collectives  92.9 us (54%)
  matrix products  18 us (11%)
  between operations  15 us (9%)
  local copies, waits for them, and re-layouts  14.5 us (8%)
  waiting for transfers between devices  14 us (8%)
  starting transfers between devices  11 us (6%)
  other arithmetic  4.55 us (3%)
    all_to_all x2, blocking collectives, flat_all_to_all(): return lax.all_to_all(x, VOX, 0, 0, tiled=True)  59.8 us
    all_to_all x1, blocking collectives, reduce_replicate(): mine = lax.all_to_all(mine, VOX[0], 0, 0, tiled=True)  16.9 us
    all_to_all x1, blocking collectives, reduce_replicate(): part = lax.all_to_all(part, VOX[0], 0, 0, tiled=True).sum(axis=0)  16.1 us
    all_to_all x1, waiting for transfers between devices, reduce_replicate(): part = lax.all_to_all(part, VOX[1:], 1, 1, tiled=True).sum(axis=1)  7.24 us
    all_to_all x1, waiting for transfers between devices, reduce_replicate(): mine = lax.all_to_all(mine, VOX[1:], 0, 0, tiled=True)  6.75 us
    dot_general x2, matrix products, exact_sum(): jnp.einsum('pt,pc->tc', onehot, both, preferred_element_type=jnp.float32)  6.64 us
    all_to_all x1, starting transfers between devices, reduce_replicate(): mine = lax.all_to_all(mine, VOX[1:], 0, 0, tiled=True)  6.55 us
    reshape x2, local copies, waits for them, and re-layouts, reduce_replicate(): part = flat.reshape(sizes[0], near, chunk, 128)  4.96 us
  transfers between devices with their start and end apart: 3, of which 2 were waited for; matrix products, arithmetic and copies ran while one was open for 6% of the time, Pallas kernels for 0%

profile of v7, /device:TPU:1, one launch (start us, length us, event | category | flops | bytes accessed | tf_op | source)
XLA Modules:
  0.0 170.1 jit_solution(10276937871392798223)
XLA Ops:
  7.9 0.7 compare_select_fusion
  8.6 0.8 copy.48
  9.4 0.2 fusion.43
  9.7 0.9 fusion.41
  10.6 0.7 multiply_add_fusion
  11.3 0.6 gather_fusion
  12.0 3.1 %fusion.6 = bf16[4096,128]{1,0:T(8,128)(2,1)S(1)} fusion(s32[4096]{0:T(1024)S(1)} %copy-done.6, bf16[1024,128]{1,0:T(8,128)(2,1)S(1)} %copy-done.3, pred[1024]{0:T(1024)(128)(4,1)S(1)} %iota_compare_fusion.30), kind=kOutput, calls=%fused_computation.9 | convolution fusion | flops 1078591488 | bytes 1328128 | tf_op jit(solution)/shard_map/dot_general | solution.py:81
  15.1 0.8 convolution_bitcast_fusion
  15.9 0.2 reduce-precision_convert_fusion.1
  16.1 1.5 fusion.5
  17.6 0.5 fusion.20
  18.1 0.2 copy.51
  18.2 0.2 all_to_all.24
  18.4 36.8 %all_to_all.38 = bf16[128,3,128]{2,1,0:T(4,128)(2,1)S(1)} all-to-all(bf16[128,3,128]{2,1,0:T(4,128)(2,1)S(1)} %all_to_all.24), channel_id=1, replica_groups=mesh['z'=16,'y'=4,'core'=2,'ch'=4] {'z','y','core'}, dimensions={0} | all-to-all | bytes 196608 | tf_op jit(solution)/shard_map/all_to_all | solution.py:33
  55.2 0.1 reshape.79
  55.3 1.2 fusion.54
  56.5 0.5 fusion.19
  57.0 0.2 copy.52
  57.2 0.2 all_to_all.26
  57.4 23.1 %all_to_all.39 = bf16[128,3,128]{2,1,0:T(4,128)(2,1)S(1)} all-to-all(bf16[128,3,128]{2,1,0:T(4,128)(2,1)S(1)} %all_to_all.26), channel_id=1, replica_groups=mesh['z'=16,'y'=4,'core'=2,'ch'=4] {'z','y','core'}, dimensions={0} | all-to-all | bytes 196608 | tf_op jit(solution)/shard_map/all_to_all | solution.py:33
  80.4 0.1 reshape.80
  80.6 2.1 %fusion.18 = bf16[8,32,8,128]{3,2,1,0:T(8,128)(2,1)S(1)} fusion(s32[4096]{0:T(1024)S(1)} %copy-done.5, bf16[768,64]{1,0:T(8,128)(2,1)S(1)} %reshape.80, s32[512]{0:T(512)S(1)} %bitcast.85), kind=kOutput, calls=%fused_computation.28 | convolution fusion | flops 321552384 | bytes 641024 | tf_op jit(solution)/shard_map/pt,to->po/dot_general | solution.py:112
  82.7 0.8 copy-done.1
  83.5 0.4 fusion.33
  83.9 1.5 fusion.35
  85.5 1.3 fusion.26
  86.7 0.5 copy.56
  87.3 1.0 pad.4
  88.3 2.2 %reshape.84 = f32[16,8,14,128]{3,2,1,0:T(8,128)} reshape(f32[1792,128]{1,0:T(8,128)} %pad.4) | data formatting | bytes 1835008 | tf_op jit(solution)/shard_map/reshape | solution.py:43
  90.5 2.7 %copy.57 = f32[16,8,14,128]{3,0,2,1:T(8,128)} copy(f32[16,8,14,128]{3,2,1,0:T(8,128)} %reshape.84) | data formatting | bytes 1835008 | tf_op jit(solution)/shard_map/reshape | solution.py:43
  93.3 4.5 %all-to-all-start.2 = ((f32[16,8,14,128]{3,0,2,1:T(8,128)}), f32[16,8,14,128]{3,0,2,1:T(8,128)}, u32[]{:S(2)}, u32[]{:S(2)}) async-start(f32[16,8,14,128]{3,0,2,1:T(8,128)} %copy.57), calls=%async_computation.2 | async-start | bytes 1835008 | tf_op jit(solution)/shard_map/all_to_all | solution.py:44
  97.7 0.3 reduce-precision_convert_fusion
  98.1 5.1 %fusion = f32[1024,256]{1,0:T(8,128)S(1)} fusion(s32[4096]{0:T(1024)S(1)} %copy-done.6, bf16[4096,128]{1,0:T(8,128)(2,1)S(1)} %get-tuple-element.19, bf16[4096,128]{1,0:T(8,128)(2,1)S(1)} %get-tuple-element.18), kind=kOutput, calls=%fused_computation.2 | convolution fusion | flops 2155872256 | bytes 3162112 | tf_op jit(solution)/shard_map/pt,pc->tc/dot_general | solution.py:24
  103.2 0.1 slice_add_fusion
  103.3 1.0 copy.62
  104.3 7.2 %all-to-all-done.2 = f32[16,8,14,128]{3,0,2,1:T(8,128)} async-done(((f32[16,8,14,128]{3,0,2,1:T(8,128)}), f32[16,8,14,128]{3,0,2,1:T(8,128)}, u32[]{:S(2)}, u32[]{:S(2)}) %all-to-all-start.2) | async-done | bytes 917536 | tf_op jit(solution)/shard_map/all_to_all | solution.py:44
  111.6 1.2 reduce_sum.31
  112.9 16.1 %all_to_all.40 = f32[16,14,128]{2,1,0:T(8,128)S(1)} all-to-all(f32[16,14,128]{2,1,0:T(8,128)S(1)} %copy.58), channel_id=1, replica_groups=mesh['z'=16,'y'=4,'core'=2,'ch'=4] {'z'}, dimensions={0} | all-to-all | bytes 229376 | tf_op jit(solution)/shard_map/all_to_all | solution.py:45
  129.0 16.9 %all_to_all.41 = bf16[16,14,128]{2,1,0:T(8,128)(2,1)S(1)} all-to-all(bf16[16,14,128]{2,1,0:T(8,128)(2,1)S(1)} %broadcast_in_dim.35), channel_id=1, replica_groups=mesh['z'=16,'y'=4,'core'=2,'ch'=4] {'z'}, dimensions={0} | all-to-all | bytes 114688 | tf_op jit(solution)/shard_map/all_to_all | solution.py:48
  146.0 0.8 broadcast_in_dim.36
  146.8 6.6 %all-to-all-start.5 = ((bf16[8,16,14,128]{3,1,2,0:T(8,128)(2,1)}), bf16[8,16,14,128]{3,1,2,0:T(8,128)(2,1)S(1)}, u32[]{:S(2)}, u32[]{:S(2)}) async-start(bf16[8,16,14,128]{3,1,2,0:T(8,128)(2,1)} %broadcast_in_dim.36), calls=%async_computation.5 | async-start | bytes 917504 | tf_op jit(solution)/shard_map/all_to_all | solution.py:50
  153.3 1.1 copy.63
  154.4 0.2 fusion.39
  154.6 0.8 copy.61
  155.4 6.8 %all-to-all-done.5 = bf16[8,16,14,128]{3,1,2,0:T(8,128)(2,1)S(1)} async-done(((bf16[8,16,14,128]{3,1,2,0:T(8,128)(2,1)}), bf16[8,16,14,128]{3,1,2,0:T(8,128)(2,1)S(1)}, u32[]{:S(2)}, u32[]{:S(2)}) %all-to-all-start.5) | async-done | bytes 458784 | tf_op jit(solution)/shard_map/all_to_all | solution.py:50
  162.1 0.1 copy.60
  162.3 0.1 reshape.85
  162.4 0.8 slice.35
  (31 shorter events, 0.3 us)
Async XLA Ops:
  7.2 4.1 %copy-start = (bf16[27,64,128]{2,1,0:T(8,128)(2,1)S(1)}, bf16[27,64,128]{2,1,0:T(8,128)(2,1)}, u32[]{:S(2)}) copy-start(bf16[27,64,128]{2,1,0:T(8,128)(2,1)} %param.10) | copy-start | bytes 1327108
  7.2 4.8 %copy-start.6 = (s32[4096]{0:T(1024)S(1)}, s32[4096]{0:T(1024)}, u32[]{:S(2)}) copy-start(s32[4096]{0:T(1024)} %param.12) | copy-start | bytes 49156
  7.2 4.8 %copy-start.3 = (bf16[1024,128]{1,0:T(8,128)(2,1)S(1)}, bf16[1024,128]{1,0:T(8,128)(2,1)}, u32[]{:S(2)}) copy-start(bf16[1024,128]{1,0:T(8,128)(2,1)} %param.9) | copy-start | bytes 786436
  15.1 1.0 copy-start.5
  16.1 39.3 %copy-start.7 = (s32[768]{0:T(1024)S(1)}, s32[768]{0:T(1024)}, u32[]{:S(2)}) copy-start(s32[768]{0:T(1024)} %param.16) | copy-start | bytes 9220
  17.6 38.9 %copy-start.4 = (bf16[64,512]{1,0:T(8,128)(2,1)S(1)}, bf16[64,512]{1,0:T(8,128)(2,1)}, u32[]{:S(2)}) copy-start(bf16[64,512]{1,0:T(8,128)(2,1)} %param.11) | copy-start | bytes 196612
  82.7 0.8 copy-start.1
  83.9 1.6 copy-start.2
  93.3 18.3 %all-to-all-start.2 = ((f32[16,8,14,128]{3,0,2,1:T(8,128)}), f32[16,8,14,128]{3,0,2,1:T(8,128)}, u32[]{:S(2)}, u32[]{:S(2)}) async-start(f32[16,8,14,128]{3,0,2,1:T(8,128)} %copy.57), calls=%async_computation.2 | async-start | bytes 1835008 | tf_op jit(solution)/shard_map/all_to_all | solution.py:44
  97.7 55.6 %reduce-scatter.4.cloned.1.call-start = ((), (), s32[]{:S(2)}) async-start(), calls=%async_computation.7 | async-start | bytes 655360
  146.8 15.3 %all-to-all-start.5 = ((bf16[8,16,14,128]{3,1,2,0:T(8,128)(2,1)}), bf16[8,16,14,128]{3,1,2,0:T(8,128)(2,1)S(1)}, u32[]{:S(2)}, u32[]{:S(2)}) async-start(bf16[8,16,14,128]{3,1,2,0:T(8,128)(2,1)} %broadcast_in_dim.36), calls=%async_computation.5 | async-start | bytes 917504 | tf_op jit(solution)/shard_map/all_to_all | solution.py:50
Sparse Core Ops, SparseCore 0:
  104.4 21.1 reduce-scatter.3

commit v8 on v7

--- a/solution.py
+++ b/solution.py
@@ -33,23 +33,21 @@
     return lax.all_to_all(x, VOX, 0, 0, tiled=True)
 
 
-def reduce_replicate(weight_sum, sizes, factor):
-    shape = weight_sum.shape
+def reduce_replicate(weight_sum, sizes, factor, rows):
     owners = math.prod(sizes)
     near = owners // sizes[0]
-    rows = weight_sum.size // 128
-    chunk = -(-rows // owners)
-    flat = jnp.pad(weight_sum.reshape(rows, 128), ((0, chunk * owners - rows), (0, 0)))
-    part = flat.reshape(sizes[0], near, chunk, 128)
-    part = lax.all_to_all(part, VOX[1:], 1, 1, tiled=True).sum(axis=1)
+    width = weight_sum.shape[-1]
+    chunk = weight_sum.size // (width * owners)
+    part = weight_sum.reshape(near, sizes[0], chunk, width)
+    part = lax.all_to_all(part, VOX[1:], 0, 0, tiled=True).sum(axis=0)
     part = lax.all_to_all(part, VOX[0], 0, 0, tiled=True).sum(axis=0)
     mine = (part * factor).astype(jnp.bfloat16)
-    mine = jnp.broadcast_to(mine[None], (sizes[0], chunk, 128))
+    mine = jnp.broadcast_to(mine[None], (sizes[0], chunk, width))
     mine = lax.all_to_all(mine, VOX[0], 0, 0, tiled=True)
-    mine = jnp.broadcast_to(mine[None], (near, sizes[0], chunk, 128))
+    mine = jnp.broadcast_to(mine[None], (near, sizes[0], chunk, width))
     mine = lax.all_to_all(mine, VOX[1:], 0, 0, tiled=True)
-    back = jnp.transpose(mine, (1, 0, 2, 3)).reshape(owners * chunk, 128)
-    return back[:rows].reshape(shape)
+    back = mine.reshape(owners * chunk, width)
+    return back[:rows].reshape((-1,) + weight_sum.shape[1:])
 
 
 def body(
@@ -120,7 +118,10 @@
     grad_weight = jnp.einsum(
         "bpc,bpo->boc", gathered, grad_rows, preferred_element_type=jnp.float32
     )
-    offset_hot = one_hot(block_offset, offsets_all).astype(jnp.float32)
+    rows_all = offsets_all * width_out
+    step = owners * 8
+    padded = -(-rows_all // step) * step // width_out
+    offset_hot = one_hot(block_offset, padded).astype(jnp.float32)
     weight_sum = jnp.einsum(
         "bk,boc->koc", offset_hot, grad_weight, precision=lax.Precision.HIGHEST
     )
@@ -129,7 +130,7 @@
         jnp.bfloat16
     )
     factor = math.sqrt(offsets_all / (blocks * group * owners))
-    grad_kernel = reduce_replicate(weight_sum, sizes, factor)
+    grad_kernel = reduce_replicate(weight_sum, sizes, factor, rows_all)
     return (activation.T, grad_features.T, grad_kernel)
 
 

time: 171 us -> 169 us (0.988)
  blocking collectives: 92.9 us -> 76.8 us
  waiting for transfers between devices: 14 us -> 28.1 us
  local copies, waits for them, and re-layouts: 14.5 us -> 9.36 us
  starting transfers between devices: 11 us -> 15.5 us
    all_to_all x1 -> x0, blocking collectives: 16.1 us -> none  [reduce_replicate(): part = lax.all_to_all(part, VOX[0], 0, 0, tiled=True).sum(axis=0)]
    all_to_all x1 -> x2, waiting for transfers between devices: 7.24 us -> 20.6 us  [the longest x1 10.8 us: reduce_replicate(): part = lax.all_to_all(part, VOX[0], 0, 0, tiled=True).sum(axis=0)]
    reshape x3 -> x0, local copies, waits for them, and re-layouts: 5.1 us -> none  [the longest x2 4.96 us: reduce_replicate(): part = flat.reshape(sizes[0], near, chunk, 128)]
    all_to_all x1 -> x2, starting transfers between devices: 4.49 us -> 8.83 us  [the longest x1 4.51 us: reduce_replicate(): part = lax.all_to_all(part, VOX[1:], 0, 0, tiled=True).sum(axis=0)]
  transfers between devices with their start and end apart: 3 -> 4, of which waited for: 2 -> 3; matrix products, arithmetic and copies ran while one was open for 6% -> 6% of each run, Pallas kernels for 0% -> 0%
where the time goes in v8:
time: 169 us; the launch traced here: 168 us
  blocking collectives  76.8 us (45%)
  waiting for transfers between devices  28.1 us (17%)
  matrix products  18 us (11%)
  starting transfers between devices  15.5 us (9%)
  between operations  15 us (9%)
  local copies, waits for them, and re-layouts  9.36 us (6%)
  other arithmetic  5.26 us (3%)
    all_to_all x2, blocking collectives, flat_all_to_all(): return lax.all_to_all(x, VOX, 0, 0, tiled=True)  59.8 us
    all_to_all x1, blocking collectives, reduce_replicate(): mine = lax.all_to_all(mine, VOX[0], 0, 0, tiled=True)  16.9 us
    all_to_all x1, waiting for transfers between devices, reduce_replicate(): part = lax.all_to_all(part, VOX[0], 0, 0, tiled=True).sum(axis=0)  10.8 us
    all_to_all x1, waiting for transfers between devices, reduce_replicate(): part = lax.all_to_all(part, VOX[1:], 0, 0, tiled=True).sum(axis=0)  9.75 us
    all_to_all x1, waiting for transfers between devices, reduce_replicate(): mine = lax.all_to_all(mine, VOX[1:], 0, 0, tiled=True)  7.45 us
    dot_general x2, matrix products, exact_sum(): jnp.einsum('pt,pc->tc', onehot, both, preferred_element_type=jnp.float32)  6.64 us
    all_to_all x1, starting transfers between devices, reduce_replicate(): mine = lax.all_to_all(mine, VOX[1:], 0, 0, tiled=True)  6.6 us
    all_to_all x1, starting transfers between devices, reduce_replicate(): part = lax.all_to_all(part, VOX[1:], 0, 0, tiled=True).sum(axis=0)  4.51 us
  transfers between devices with their start and end apart: 4, of which 3 were waited for; matrix products, arithmetic and copies ran while one was open for 6% of the time, Pallas kernels for 0%

profile of v8, /device:TPU:1, one launch (start us, length us, event | category | flops | bytes accessed | tf_op | source)
XLA Modules:
  0.0 168.0 jit_solution(6083458316305477349)
XLA Ops:
  7.2 0.0 copy-start
  7.9 0.7 compare_select_fusion
  8.6 0.8 copy.33
  9.4 0.2 fusion.43
  9.7 0.9 fusion.41
  10.6 0.7 multiply_add_fusion
  11.3 0.6 gather_fusion
  12.0 3.1 %fusion.6 = bf16[4096,128]{1,0:T(8,128)(2,1)S(1)} fusion(s32[4096]{0:T(1024)S(1)} %copy-done.6, bf16[1024,128]{1,0:T(8,128)(2,1)S(1)} %copy-done.3, pred[1024]{0:T(1024)(128)(4,1)S(1)} %iota_compare_fusion.30), kind=kOutput, calls=%fused_computation.9 | convolution fusion | flops 1078591488 | bytes 1328128 | tf_op jit(solution)/shard_map/dot_general | solution.py:79
  15.1 0.0 copy-start.5
  15.1 0.8 convolution_bitcast_fusion
  15.9 0.2 reduce-precision_convert_fusion.1
  16.1 1.5 fusion.5
  17.6 0.5 fusion.20
  18.1 0.2 copy.36
  18.2 0.2 all_to_all.24
  18.4 36.8 %all_to_all.38 = bf16[128,3,128]{2,1,0:T(4,128)(2,1)S(1)} all-to-all(bf16[128,3,128]{2,1,0:T(4,128)(2,1)S(1)} %all_to_all.24), channel_id=1, replica_groups=mesh['z'=16,'y'=4,'core'=2,'ch'=4] {'z','y','core'}, dimensions={0} | all-to-all | bytes 196608 | tf_op jit(solution)/shard_map/all_to_all | solution.py:33
  55.2 0.1 reshape.76
  55.3 1.2 fusion.54
  56.5 0.5 fusion.19
  57.0 0.2 copy.37
  57.2 0.2 all_to_all.26
  57.4 23.1 %all_to_all.39 = bf16[128,3,128]{2,1,0:T(4,128)(2,1)S(1)} all-to-all(bf16[128,3,128]{2,1,0:T(4,128)(2,1)S(1)} %all_to_all.26), channel_id=1, replica_groups=mesh['z'=16,'y'=4,'core'=2,'ch'=4] {'z','y','core'}, dimensions={0} | all-to-all | bytes 196608 | tf_op jit(solution)/shard_map/all_to_all | solution.py:33
  80.4 0.1 reshape.77
  80.6 2.1 %fusion.18 = bf16[8,32,8,128]{3,2,1,0:T(8,128)(2,1)S(1)} fusion(s32[4096]{0:T(1024)S(1)} %copy-done.5, bf16[768,64]{1,0:T(8,128)(2,1)S(1)} %reshape.77, s32[512]{0:T(512)S(1)} %bitcast.85), kind=kOutput, calls=%fused_computation.28 | convolution fusion | flops 321552384 | bytes 641024 | tf_op jit(solution)/shard_map/pt,to->po/dot_general | solution.py:110
  82.7 0.8 copy-done.1
  83.5 0.4 fusion.33
  83.9 1.5 fusion.35
  85.5 1.3 fusion.26
  86.8 1.6 copy.41
  88.4 4.5 %all-to-all-start.2 = ((f32[8,16,16,128]{3,2,1,0:T(8,128)}), f32[8,16,16,128]{3,2,1,0:T(8,128)}, u32[]{:S(2)}, u32[]{:S(2)}) async-start(f32[8,16,16,128]{3,2,1,0:T(8,128)} %bitcast.73), calls=%async_computation.2 | async-start | bytes 2097152 | tf_op jit(solution)/shard_map/all_to_all | solution.py:42
  92.9 0.3 reduce-precision_convert_fusion
  93.2 5.1 %fusion = f32[1024,256]{1,0:T(8,128)S(1)} fusion(s32[4096]{0:T(1024)S(1)} %copy-done.6, bf16[4096,128]{1,0:T(8,128)(2,1)S(1)} %get-tuple-element.16, bf16[4096,128]{1,0:T(8,128)(2,1)S(1)} %get-tuple-element.15), kind=kOutput, calls=%fused_computation.2 | convolution fusion | flops 2155872256 | bytes 3162112 | tf_op jit(solution)/shard_map/pt,pc->tc/dot_general | solution.py:24
  98.4 9.7 %all-to-all-done.2 = f32[8,16,16,128]{3,2,1,0:T(8,128)} async-done(((f32[8,16,16,128]{3,2,1,0:T(8,128)}), f32[8,16,16,128]{3,2,1,0:T(8,128)}, u32[]{:S(2)}, u32[]{:S(2)}) %all-to-all-start.2) | async-done | bytes 1048608 | tf_op jit(solution)/shard_map/all_to_all | solution.py:42
  108.1 2.0 %reduce_sum.31 = f32[16,16,128]{2,1,0:T(8,128)} reduce(f32[8,16,16,128]{3,2,1,0:T(8,128)} %all-to-all-done.2, f32[]{:T(128)} %constant.6.clone.1), dimensions={0}, to_apply=%region_4.5 | reduce | flops 229376 | bytes 1179652 | tf_op jit(solution)/shard_map/reduce_sum | solution.py:42
  110.1 4.3 %all-to-all-start.3 = ((f32[16,16,128]{2,1,0:T(8,128)}), f32[16,16,128]{2,1,0:T(8,128)S(1)}, u32[]{:S(2)}, u32[]{:S(2)}) async-start(f32[16,16,128]{2,1,0:T(8,128)} %reduce_sum.31), calls=%async_computation.3 | async-start | bytes 262144 | tf_op jit(solution)/shard_map/all_to_all | solution.py:43
  114.4 0.0 reduce-scatter.4.cloned.1.call-start
  114.5 0.1 slice_add_fusion
  114.5 1.0 copy.43
  115.5 0.0 reduce-scatter.4.cloned.1.call-update
  115.5 10.8 %all-to-all-done.3 = f32[16,16,128]{2,1,0:T(8,128)S(1)} async-done(((f32[16,16,128]{2,1,0:T(8,128)}), f32[16,16,128]{2,1,0:T(8,128)S(1)}, u32[]{:S(2)}, u32[]{:S(2)}) %all-to-all-start.3) | async-done | bytes 131104 | tf_op jit(solution)/shard_map/all_to_all | solution.py:43
  126.4 16.9 %all_to_all.40 = bf16[16,16,128]{2,1,0:T(8,128)(2,1)S(1)} all-to-all(bf16[16,16,128]{2,1,0:T(8,128)(2,1)S(1)} %broadcast_in_dim.35), channel_id=1, replica_groups=mesh['z'=16,'y'=4,'core'=2,'ch'=4] {'z'}, dimensions={0} | all-to-all | bytes 131072 | tf_op jit(solution)/shard_map/all_to_all | solution.py:46
  143.4 0.9 broadcast_in_dim.36
  144.2 6.6 %all-to-all-start.5 = ((bf16[8,16,16,128]{3,2,1,0:T(8,128)(2,1)}), bf16[8,16,16,128]{3,2,1,0:T(8,128)(2,1)S(1)}, u32[]{:S(2)}, u32[]{:S(2)}) async-start(bf16[8,16,16,128]{3,2,1,0:T(8,128)(2,1)} %broadcast_in_dim.36), calls=%async_computation.5 | async-start | bytes 1048576 | tf_op jit(solution)/shard_map/all_to_all | solution.py:48
  150.8 1.1 copy.44
  151.9 0.2 fusion.39
  152.1 0.8 copy.42
  152.9 7.5 %all-to-all-done.5 = bf16[8,16,16,128]{3,2,1,0:T(8,128)(2,1)S(1)} async-done(((bf16[8,16,16,128]{3,2,1,0:T(8,128)(2,1)}), bf16[8,16,16,128]{3,2,1,0:T(8,128)(2,1)S(1)}, u32[]{:S(2)}, u32[]{:S(2)}) %all-to-all-start.5) | async-done | bytes 524320 | tf_op jit(solution)/shard_map/all_to_all | solution.py:48
  160.3 0.8 slice.35
  (25 shorter events, 0.2 us)
Async XLA Ops:
  7.2 4.1 %copy-start = (bf16[27,64,128]{2,1,0:T(8,128)(2,1)S(1)}, bf16[27,64,128]{2,1,0:T(8,128)(2,1)}, u32[]{:S(2)}) copy-start(bf16[27,64,128]{2,1,0:T(8,128)(2,1)} %param.10) | copy-start | bytes 1327108
  7.2 4.8 %copy-start.6 = (s32[4096]{0:T(1024)S(1)}, s32[4096]{0:T(1024)}, u32[]{:S(2)}) copy-start(s32[4096]{0:T(1024)} %param.12) | copy-start | bytes 49156
  7.2 4.8 %copy-start.3 = (bf16[1024,128]{1,0:T(8,128)(2,1)S(1)}, bf16[1024,128]{1,0:T(8,128)(2,1)}, u32[]{:S(2)}) copy-start(bf16[1024,128]{1,0:T(8,128)(2,1)} %param.9) | copy-start | bytes 786436
  15.1 1.0 copy-start.5
  16.1 39.3 %copy-start.7 = (s32[768]{0:T(1024)S(1)}, s32[768]{0:T(1024)}, u32[]{:S(2)}) copy-start(s32[768]{0:T(1024)} %param.16) | copy-start | bytes 9220
  17.6 38.9 %copy-start.4 = (bf16[64,512]{1,0:T(8,128)(2,1)S(1)}, bf16[64,512]{1,0:T(8,128)(2,1)}, u32[]{:S(2)}) copy-start(bf16[64,512]{1,0:T(8,128)(2,1)} %param.11) | copy-start | bytes 196612
  82.7 0.8 copy-start.1
  83.9 1.6 copy-start.2
  88.4 19.7 %all-to-all-start.2 = ((f32[8,16,16,128]{3,2,1,0:T(8,128)}), f32[8,16,16,128]{3,2,1,0:T(8,128)}, u32[]{:S(2)}, u32[]{:S(2)}) async-start(f32[8,16,16,128]{3,2,1,0:T(8,128)} %bitcast.73), calls=%async_computation.2 | async-start | bytes 2097152 | tf_op jit(solution)/shard_map/all_to_all | solution.py:42
  110.1 16.3 %all-to-all-start.3 = ((f32[16,16,128]{2,1,0:T(8,128)}), f32[16,16,128]{2,1,0:T(8,128)S(1)}, u32[]{:S(2)}, u32[]{:S(2)}) async-start(f32[16,16,128]{2,1,0:T(8,128)} %reduce_sum.31), calls=%async_computation.3 | async-start | bytes 262144 | tf_op jit(solution)/shard_map/all_to_all | solution.py:43
  114.4 36.4 %reduce-scatter.4.cloned.1.call-start = ((), (), s32[]{:S(2)}) async-start(), calls=%async_computation.7 | async-start | bytes 655360
  144.2 16.1 %all-to-all-start.5 = ((bf16[8,16,16,128]{3,2,1,0:T(8,128)(2,1)}), bf16[8,16,16,128]{3,2,1,0:T(8,128)(2,1)S(1)}, u32[]{:S(2)}, u32[]{:S(2)}) async-start(bf16[8,16,16,128]{3,2,1,0:T(8,128)(2,1)} %broadcast_in_dim.36), calls=%async_computation.5 | async-start | bytes 1048576 | tf_op jit(solution)/shard_map/all_to_all | solution.py:48
Sparse Core Ops, SparseCore 0:
  118.1 27.3 reduce-scatter.3

commit v9 on v8

--- a/solution.py
+++ b/solution.py
@@ -31,6 +31,15 @@
 
 def flat_all_to_all(x):
     return lax.all_to_all(x, VOX, 0, 0, tiled=True)
+
+
+def exact_sum_t(onehot, values):
+    high = lax.reduce_precision(values, exponent_bits=8, mantissa_bits=7)
+    low = values - high
+    both = jnp.concatenate([high.astype(jnp.bfloat16), low.astype(jnp.bfloat16)], axis=1)
+    total = jnp.einsum("pc,pt->ct", both, onehot, preferred_element_type=jnp.float32)
+    width = values.shape[1]
+    return total[:width] + total[width:]
 
 
 def reduce_replicate(weight_sum, sizes, factor, rows):
@@ -114,7 +123,7 @@
     grad_in = jnp.einsum(
         "bpo,boc->bpc", grad_rows, weights, preferred_element_type=jnp.float32
     ).reshape(pairs, width_in)
-    fine_sum = exact_sum(fine_hot, grad_in)
+    fine_sum = exact_sum_t(fine_hot, grad_in)
     grad_weight = jnp.einsum(
         "bpc,bpo->boc", gathered, grad_rows, preferred_element_type=jnp.float32
     )
@@ -125,13 +134,15 @@
     weight_sum = jnp.einsum(
         "bk,boc->koc", offset_hot, grad_weight, precision=lax.Precision.HIGHEST
     )
-    fine_grad = lax.psum_scatter(fine_sum, "ch", scatter_dimension=1, tiled=True)
-    grad_features = jnp.where(live_mask[:, None], fine_grad, jnp.zeros((), jnp.float32)).astype(
+    groups = lax.axis_size("ch")
+    fine_parts = fine_sum.reshape(groups, width_in // groups, fine_total)
+    fine_grad = lax.all_to_all(fine_parts, "ch", 0, 0, tiled=True).sum(axis=0)
+    grad_features = jnp.where(live_mask[None, :], fine_grad, jnp.zeros((), jnp.float32)).astype(
         jnp.bfloat16
     )
     factor = math.sqrt(offsets_all / (blocks * group * owners))
     grad_kernel = reduce_replicate(weight_sum, sizes, factor, rows_all)
-    return (activation.T, grad_features.T, grad_kernel)
+    return (activation.T, grad_features, grad_kernel)
 
 
 def solution(mesh):

time: 169 us -> 168 us (level)
  between operations: 15 us -> 1.6 us
  waiting for transfers between devices: 28.1 us -> 36.2 us
  starting transfers between devices: 15.5 us -> 20.6 us
  local copies, waits for them, and re-layouts: 9.36 us -> 6.47 us
  other arithmetic: 5.26 us -> 7.85 us
    all_to_all x0 -> x1, waiting for transfers between devices: none -> 6.9 us  [body(): fine_grad = lax.all_to_all(fine_parts, 'ch', 0, 0, tiled=True).sum(axis=0)]
    dot_general x2 -> x1, matrix products: 6.64 us -> 1.5 us  [exact_sum(): jnp.einsum('pt,pc->tc', onehot, both, preferred_element_type=jnp.float32)]
    dot_general x0 -> x1, matrix products: none -> 4.24 us  [exact_sum_t(): jnp.einsum('pc,pt->ct', both, onehot, preferred_element_type=jnp.float32)]
    all_to_all x0 -> x1, starting transfers between devices: none -> 4.01 us  [body(): fine_grad = lax.all_to_all(fine_parts, 'ch', 0, 0, tiled=True).sum(axis=0)]
    all_to_all x1, waiting for transfers between devices: 10.8 us -> 6.89 us  [reduce_replicate(): part = lax.all_to_all(part, VOX[0], 0, 0, tiled=True).sum(axis=0)]
    all_to_all x1, waiting for transfers between devices: 9.75 us -> 13.6 us  [reduce_replicate(): part = lax.all_to_all(part, VOX[1:], 0, 0, tiled=True).sum(axis=0)]
    unnamed x20 -> x17, local copies, waits for them, and re-layouts: 3.65 us -> 0.82 us
    convert_element_type x0 -> x2, other arithmetic: none -> 2.31 us  [the longest x1 1.67 us: exact_sum_t(): high.astype(jnp.bfloat16)]
  transfers between devices with their start and end apart: 4 -> 4, of which waited for: 3 -> 4; matrix products, arithmetic and copies ran while one was open for 6% -> 4% of each run, Pallas kernels for 0% -> 0%
where the time goes in v9:
time: 168 us; the launch traced here: 167 us
  blocking collectives  77.4 us (46%)
  waiting for transfers between devices  36.2 us (22%)
  starting transfers between devices  20.6 us (12%)
  matrix products  17.1 us (10%)
  other arithmetic  7.85 us (5%)
  local copies, waits for them, and re-layouts  6.47 us (4%)
    all_to_all x2, blocking collectives, flat_all_to_all(): return lax.all_to_all(x, VOX, 0, 0, tiled=True)  59.8 us
    all_to_all x1, blocking collectives, reduce_replicate(): mine = lax.all_to_all(mine, VOX[0], 0, 0, tiled=True)  17.6 us
    all_to_all x1, waiting for transfers between devices, reduce_replicate(): part = lax.all_to_all(part, VOX[1:], 0, 0, tiled=True).sum(axis=0)  13.6 us
    all_to_all x1, waiting for transfers between devices, reduce_replicate(): mine = lax.all_to_all(mine, VOX[1:], 0, 0, tiled=True)  8.82 us
    all_to_all x1, starting transfers between devices, reduce_replicate(): mine = lax.all_to_all(mine, VOX[1:], 0, 0, tiled=True)  7.79 us
    all_to_all x1, waiting for transfers between devices, body(): fine_grad = lax.all_to_all(fine_parts, 'ch', 0, 0, tiled=True).sum(axis=0)  6.9 us
    all_to_all x1, waiting for transfers between devices, reduce_replicate(): part = lax.all_to_all(part, VOX[0], 0, 0, tiled=True).sum(axis=0)  6.89 us
    all_to_all x1, starting transfers between devices, reduce_replicate(): part = lax.all_to_all(part, VOX[1:], 0, 0, tiled=True).sum(axis=0)  4.5 us
  transfers between devices with their start and end apart: 4, of which 4 were waited for; matrix products, arithmetic and copies ran while one was open for 4% of the time, Pallas kernels for 0%

profile of v9, /device:TPU:1, one launch (start us, length us, event | category | flops | bytes accessed | tf_op | source)
XLA Modules:
  0.0 167.2 jit_solution(8322509712314720821)
XLA Ops:
  0.6 0.0 copy-start
  1.4 0.7 compare_select_fusion
  2.1 0.8 copy.21
  2.8 0.2 fusion.42
  3.2 0.9 fusion.40
  4.1 0.7 multiply_add_fusion
  4.8 0.6 gather_fusion
  5.4 3.1 %fusion.6 = bf16[4096,128]{1,0:T(8,128)(2,1)S(1)} fusion(s32[4096]{0:T(1024)S(1)} %copy-done.6, bf16[1024,128]{1,0:T(8,128)(2,1)S(1)} %copy-done.3, pred[1024]{0:T(1024)(128)(4,1)S(1)} %iota_compare_fusion.30), kind=kOutput, calls=%fused_computation.9 | convolution fusion | flops 1078591488 | bytes 1328128 | tf_op jit(solution)/shard_map/dot_general | solution.py:88
  8.5 0.0 copy-start.5
  8.5 0.8 convolution_bitcast_fusion
  9.4 0.2 reduce-precision_convert_fusion.1
  9.5 0.0 copy-start.7
  9.5 1.5 fusion.5
  11.1 0.0 copy-start.4
  11.1 0.5 fusion.20
  11.5 0.2 copy.24
  11.7 0.2 all_to_all.27
  11.9 36.8 %all_to_all.43 = bf16[128,3,128]{2,1,0:T(4,128)(2,1)S(1)} all-to-all(bf16[128,3,128]{2,1,0:T(4,128)(2,1)S(1)} %all_to_all.27), channel_id=1, replica_groups=mesh['z'=16,'y'=4,'core'=2,'ch'=4] {'z','y','core'}, dimensions={0} | all-to-all | bytes 196608 | tf_op jit(solution)/shard_map/all_to_all | solution.py:33
  48.7 0.1 reshape.83
  48.8 1.2 fusion.53
  50.0 0.5 fusion.19
  50.5 0.2 copy.25
  50.7 0.2 all_to_all.29
  50.8 23.1 %all_to_all.44 = bf16[128,3,128]{2,1,0:T(4,128)(2,1)S(1)} all-to-all(bf16[128,3,128]{2,1,0:T(4,128)(2,1)S(1)} %all_to_all.29), channel_id=1, replica_groups=mesh['z'=16,'y'=4,'core'=2,'ch'=4] {'z','y','core'}, dimensions={0} | all-to-all | bytes 196608 | tf_op jit(solution)/shard_map/all_to_all | solution.py:33
  73.9 0.1 reshape.84
  74.0 2.1 %fusion.18 = bf16[8,32,8,128]{3,2,1,0:T(8,128)(2,1)S(1)} fusion(s32[4096]{0:T(1024)S(1)} %copy-done.5, bf16[768,64]{1,0:T(8,128)(2,1)S(1)} %reshape.84, s32[512]{0:T(512)S(1)} %bitcast.80), kind=kOutput, calls=%fused_computation.28 | convolution fusion | flops 321552384 | bytes 641024 | tf_op jit(solution)/shard_map/pt,to->po/dot_general | solution.py:119
  76.2 0.8 copy-done.1
  77.0 0.4 fusion.33
  77.4 0.0 copy-start.2
  77.4 1.5 fusion.35
  78.9 1.3 fusion.26
  80.2 1.6 copy.29
  81.8 4.5 %all-to-all-start.3 = ((f32[8,16,16,128]{3,2,1,0:T(8,128)}), f32[8,16,16,128]{3,2,1,0:T(8,128)}, u32[]{:S(2)}, u32[]{:S(2)}) async-start(f32[8,16,16,128]{3,2,1,0:T(8,128)} %bitcast.70), calls=%async_computation.3 | async-start | bytes 2097152 | tf_op jit(solution)/shard_map/all_to_all | solution.py:51
  86.3 1.7 reduce-precision_convert_fusion
  88.0 13.6 %all-to-all-done.3 = f32[8,16,16,128]{3,2,1,0:T(8,128)} async-done(((f32[8,16,16,128]{3,2,1,0:T(8,128)}), f32[8,16,16,128]{3,2,1,0:T(8,128)}, u32[]{:S(2)}, u32[]{:S(2)}) %all-to-all-start.3) | async-done | bytes 1048608 | tf_op jit(solution)/shard_map/all_to_all | solution.py:51
  101.5 2.0 %reduce_sum.41 = f32[16,16,128]{2,1,0:T(8,128)} reduce(f32[8,16,16,128]{3,2,1,0:T(8,128)} %all-to-all-done.3, f32[]{:T(128)} %constant.6.clone.1), dimensions={0}, to_apply=%region_4.5 | reduce | flops 229376 | bytes 1179652 | tf_op jit(solution)/shard_map/reduce_sum | solution.py:51
  103.5 4.3 %all-to-all-start.4 = ((f32[16,16,128]{2,1,0:T(8,128)}), f32[16,16,128]{2,1,0:T(8,128)S(1)}, u32[]{:S(2)}, u32[]{:S(2)}) async-start(f32[16,16,128]{2,1,0:T(8,128)} %reduce_sum.41), calls=%async_computation.4 | async-start | bytes 262144 | tf_op jit(solution)/shard_map/all_to_all | solution.py:52
  107.8 4.2 %fusion = f32[256,1024]{1,0:T(8,128)S(1)} fusion(s32[4096]{0:T(1024)S(1)} %copy-done.6, bf16[4096,128]{1,0:T(8,128)(2,1)} %get-tuple-element.4, bf16[4096,128]{1,0:T(8,128)(2,1)} %get-tuple-element.3), kind=kOutput, calls=%fused_computation.2 | convolution fusion | flops 2155872256 | bytes 3162112 | tf_op jit(solution)/shard_map/pc,pt->ct/dot_general | solution.py:40
  112.0 0.8 slice_add_fusion
  112.9 6.9 %all-to-all-done.4 = f32[16,16,128]{2,1,0:T(8,128)S(1)} async-done(((f32[16,16,128]{2,1,0:T(8,128)}), f32[16,16,128]{2,1,0:T(8,128)S(1)}, u32[]{:S(2)}, u32[]{:S(2)}) %all-to-all-start.4) | async-done | bytes 131104 | tf_op jit(solution)/shard_map/all_to_all | solution.py:52
  119.8 4.0 %all-to-all-start.2 = ((f32[4,32,1024]{2,1,0:T(8,128)}), f32[4,32,1024]{2,1,0:T(8,128)S(1)}, u32[]{:S(2)}, u32[]{:S(2)}) async-start(f32[4,32,1024]{2,1,0:T(8,128)} %bitcast.12), calls=%async_computation.2 | async-start | bytes 1048576 | tf_op jit(solution)/shard_map/all_to_all | solution.py:139
  123.8 6.9 %all-to-all-done.2 = f32[4,32,1024]{2,1,0:T(8,128)S(1)} async-done(((f32[4,32,1024]{2,1,0:T(8,128)}), f32[4,32,1024]{2,1,0:T(8,128)S(1)}, u32[]{:S(2)}, u32[]{:S(2)}) %all-to-all-start.2) | async-done | bytes 524320 | tf_op jit(solution)/shard_map/all_to_all | solution.py:139
  130.7 17.6 %all_to_all.45 = bf16[16,16,128]{2,1,0:T(8,128)(2,1)S(1)} all-to-all(bf16[16,16,128]{2,1,0:T(8,128)(2,1)S(1)} %broadcast_in_dim.35), channel_id=1, replica_groups=mesh['z'=16,'y'=4,'core'=2,'ch'=4] {'z'}, dimensions={0} | all-to-all | bytes 131072 | tf_op jit(solution)/shard_map/all_to_all | solution.py:55
  148.3 0.8 broadcast_in_dim.36
  149.2 7.8 %all-to-all-start.6 = ((bf16[8,16,16,128]{3,2,1,0:T(8,128)(2,1)}), bf16[8,16,16,128]{3,2,1,0:T(8,128)(2,1)S(1)}, u32[]{:S(2)}, u32[]{:S(2)}) async-start(bf16[8,16,16,128]{3,2,1,0:T(8,128)(2,1)} %broadcast_in_dim.36), calls=%async_computation.6 | async-start | bytes 1048576 | tf_op jit(solution)/shard_map/all_to_all | solution.py:57
  157.0 0.6 select_convert_fusion
  157.6 8.8 %all-to-all-done.6 = bf16[8,16,16,128]{3,2,1,0:T(8,128)(2,1)S(1)} async-done(((bf16[8,16,16,128]{3,2,1,0:T(8,128)(2,1)}), bf16[8,16,16,128]{3,2,1,0:T(8,128)(2,1)S(1)}, u32[]{:S(2)}, u32[]{:S(2)}) %all-to-all-start.6) | async-done | bytes 524320 | tf_op jit(solution)/shard_map/all_to_all | solution.py:57
  166.4 0.8 slice.35
  (22 shorter events, 0.2 us)
Async XLA Ops:
  0.6 4.1 %copy-start = (bf16[27,64,128]{2,1,0:T(8,128)(2,1)S(1)}, bf16[27,64,128]{2,1,0:T(8,128)(2,1)}, u32[]{:S(2)}) copy-start(bf16[27,64,128]{2,1,0:T(8,128)(2,1)} %param.10) | copy-start | bytes 1327108
  0.6 4.8 %copy-start.6 = (s32[4096]{0:T(1024)S(1)}, s32[4096]{0:T(1024)}, u32[]{:S(2)}) copy-start(s32[4096]{0:T(1024)} %param.12) | copy-start | bytes 49156
  0.7 4.8 %copy-start.3 = (bf16[1024,128]{1,0:T(8,128)(2,1)S(1)}, bf16[1024,128]{1,0:T(8,128)(2,1)}, u32[]{:S(2)}) copy-start(bf16[1024,128]{1,0:T(8,128)(2,1)} %param.9) | copy-start | bytes 786436
  8.5 1.0 copy-start.5
  9.5 39.3 %copy-start.7 = (s32[768]{0:T(1024)S(1)}, s32[768]{0:T(1024)}, u32[]{:S(2)}) copy-start(s32[768]{0:T(1024)} %param.16) | copy-start | bytes 9220
  11.1 38.9 %copy-start.4 = (bf16[64,512]{1,0:T(8,128)(2,1)S(1)}, bf16[64,512]{1,0:T(8,128)(2,1)}, u32[]{:S(2)}) copy-start(bf16[64,512]{1,0:T(8,128)(2,1)} %param.11) | copy-start | bytes 196612
  76.2 0.8 copy-start.1
  77.4 1.6 copy-start.2
  81.8 19.7 %all-to-all-start.3 = ((f32[8,16,16,128]{3,2,1,0:T(8,128)}), f32[8,16,16,128]{3,2,1,0:T(8,128)}, u32[]{:S(2)}, u32[]{:S(2)}) async-start(f32[8,16,16,128]{3,2,1,0:T(8,128)} %bitcast.70), calls=%async_computation.3 | async-start | bytes 2097152 | tf_op jit(solution)/shard_map/all_to_all | solution.py:51
  103.5 16.3 %all-to-all-start.4 = ((f32[16,16,128]{2,1,0:T(8,128)}), f32[16,16,128]{2,1,0:T(8,128)S(1)}, u32[]{:S(2)}, u32[]{:S(2)}) async-start(f32[16,16,128]{2,1,0:T(8,128)} %reduce_sum.41), calls=%async_computation.4 | async-start | bytes 262144 | tf_op jit(solution)/shard_map/all_to_all | solution.py:52
  119.8 10.9 %all-to-all-start.2 = ((f32[4,32,1024]{2,1,0:T(8,128)}), f32[4,32,1024]{2,1,0:T(8,128)S(1)}, u32[]{:S(2)}, u32[]{:S(2)}) async-start(f32[4,32,1024]{2,1,0:T(8,128)} %bitcast.12), calls=%async_computation.2 | async-start | bytes 1048576 | tf_op jit(solution)/shard_map/all_to_all | solution.py:139
  149.2 17.3 %all-to-all-start.6 = ((bf16[8,16,16,128]{3,2,1,0:T(8,128)(2,1)}), bf16[8,16,16,128]{3,2,1,0:T(8,128)(2,1)S(1)}, u32[]{:S(2)}, u32[]{:S(2)}) async-start(bf16[8,16,16,128]{3,2,1,0:T(8,128)(2,1)} %broadcast_in_dim.36), calls=%async_computation.6 | async-start | bytes 1048576 | tf_op jit(solution)/shard_map/all_to_all | solution.py:57

commit v10 on v9

--- a/solution.py
+++ b/solution.py
@@ -48,7 +48,8 @@
     width = weight_sum.shape[-1]
     chunk = weight_sum.size // (width * owners)
     part = weight_sum.reshape(near, sizes[0], chunk, width)
-    part = lax.all_to_all(part, VOX[1:], 0, 0, tiled=True).sum(axis=0)
+    part = lax.all_to_all(part.astype(jnp.bfloat16), VOX[1:], 0, 0, tiled=True)
+    part = part.astype(jnp.float32).sum(axis=0)
     part = lax.all_to_all(part, VOX[0], 0, 0, tiled=True).sum(axis=0)
     mine = (part * factor).astype(jnp.bfloat16)
     mine = jnp.broadcast_to(mine[None], (sizes[0], chunk, width))

time: 168 us -> 160 us (0.952)
  waiting for transfers between devices: 36.2 us -> 30.4 us
    all_to_all x1, waiting for transfers between devices: 13.6 us -> 7.81 us  [reduce_replicate(): part = lax.all_to_all(part.astype(jnp.bfloat16), VOX[1:], 0, 0, tiled=True)]
  transfers between devices with their start and end apart: 4 -> 4, of which waited for: 4 -> 4; matrix products, arithmetic and copies ran while one was open for 4% -> 5% of each run, Pallas kernels for 0% -> 0%
where the time goes in v10:
time: 160 us; the launch traced here: 159 us
  blocking collectives  77.4 us (48%)
  waiting for transfers between devices  30.4 us (19%)
  starting transfers between devices  19.9 us (12%)
  matrix products  17.1 us (11%)
  other arithmetic  6.62 us (4%)
  local copies, waits for them, and re-layouts  5.87 us (4%)
  between operations  1.6 us (1%)
    all_to_all x2, blocking collectives, flat_all_to_all(): return lax.all_to_all(x, VOX, 0, 0, tiled=True)  59.8 us
    all_to_all x1, blocking collectives, reduce_replicate(): mine = lax.all_to_all(mine, VOX[0], 0, 0, tiled=True)  17.6 us
    all_to_all x1, waiting for transfers between devices, reduce_replicate(): mine = lax.all_to_all(mine, VOX[1:], 0, 0, tiled=True)  8.82 us
    all_to_all x1, waiting for transfers between devices, reduce_replicate(): part = lax.all_to_all(part.astype(jnp.bfloat16), VOX[1:], 0, 0, tiled=True)  7.81 us
    all_to_all x1, starting transfers between devices, reduce_replicate(): mine = lax.all_to_all(mine, VOX[1:], 0, 0, tiled=True)  7.79 us
    all_to_all x1, waiting for transfers between devices, body(): fine_grad = lax.all_to_all(fine_parts, 'ch', 0, 0, tiled=True).sum(axis=0)  6.9 us
    all_to_all x1, waiting for transfers between devices, reduce_replicate(): part = lax.all_to_all(part, VOX[0], 0, 0, tiled=True).sum(axis=0)  6.89 us
    all_to_all x1, starting transfers between devices, reduce_replicate(): part = lax.all_to_all(part.astype(jnp.bfloat16), VOX[1:], 0, 0, tiled=True)  4.4 us
  transfers between devices with their start and end apart: 4, of which 4 were waited for; matrix products, arithmetic and copies ran while one was open for 5% of the time, Pallas kernels for 0%

profile of v10, /device:TPU:1, one launch (start us, length us, event | category | flops | bytes accessed | tf_op | source)
XLA Modules:
  0.0 159.0 jit_solution(9890690827672682089)
XLA Ops:
  0.6 0.0 copy-start
  1.4 0.7 compare_select_fusion
  2.1 0.8 copy.21
  2.8 0.2 fusion.41
  3.2 0.9 fusion.39
  4.1 0.7 multiply_add_fusion
  4.8 0.6 gather_fusion
  5.4 3.1 %fusion.6 = bf16[4096,128]{1,0:T(8,128)(2,1)S(1)} fusion(s32[4096]{0:T(1024)S(1)} %copy-done.6, bf16[1024,128]{1,0:T(8,128)(2,1)S(1)} %copy-done.3, pred[1024]{0:T(1024)(128)(4,1)S(1)} %iota_compare_fusion.30), kind=kOutput, calls=%fused_computation.9 | convolution fusion | flops 1078591488 | bytes 1328128 | tf_op jit(solution)/shard_map/dot_general | solution.py:89
  8.5 0.0 copy-start.5
  8.5 0.8 convolution_bitcast_fusion
  9.4 0.2 reduce-precision_convert_fusion.1
  9.5 0.0 copy-start.7
  9.5 1.5 fusion.5
  11.1 0.0 copy-start.4
  11.1 0.5 fusion.20
  11.5 0.2 copy.24
  11.7 0.2 all_to_all.27
  11.9 36.8 %all_to_all.43 = bf16[128,3,128]{2,1,0:T(4,128)(2,1)S(1)} all-to-all(bf16[128,3,128]{2,1,0:T(4,128)(2,1)S(1)} %all_to_all.27), channel_id=1, replica_groups=mesh['z'=16,'y'=4,'core'=2,'ch'=4] {'z','y','core'}, dimensions={0} | all-to-all | bytes 196608 | tf_op jit(solution)/shard_map/all_to_all | solution.py:33
  48.7 0.1 reshape.82
  48.8 1.2 fusion.52
  50.0 0.5 fusion.19
  50.5 0.2 copy.25
  50.7 0.2 all_to_all.29
  50.8 23.1 %all_to_all.44 = bf16[128,3,128]{2,1,0:T(4,128)(2,1)S(1)} all-to-all(bf16[128,3,128]{2,1,0:T(4,128)(2,1)S(1)} %all_to_all.29), channel_id=1, replica_groups=mesh['z'=16,'y'=4,'core'=2,'ch'=4] {'z','y','core'}, dimensions={0} | all-to-all | bytes 196608 | tf_op jit(solution)/shard_map/all_to_all | solution.py:33
  73.9 0.1 reshape.83
  74.0 2.1 %fusion.18 = bf16[8,32,8,128]{3,2,1,0:T(8,128)(2,1)S(1)} fusion(s32[4096]{0:T(1024)S(1)} %copy-done.5, bf16[768,64]{1,0:T(8,128)(2,1)S(1)} %reshape.83, s32[512]{0:T(512)S(1)} %bitcast.80), kind=kOutput, calls=%fused_computation.29 | convolution fusion | flops 321552384 | bytes 641024 | tf_op jit(solution)/shard_map/pt,to->po/dot_general | solution.py:120
  76.2 0.8 copy-done.1
  77.0 0.4 fusion.32
  77.4 0.0 copy-start.2
  77.4 1.5 fusion.34
  78.9 1.3 convolution_convert_fusion
  80.2 1.0 copy.29
  81.2 4.4 %all-to-all-start.3 = ((bf16[8,16,16,128]{3,2,1,0:T(8,128)(2,1)}), bf16[8,16,16,128]{3,2,1,0:T(8,128)(2,1)S(1)}, u32[]{:S(2)}, u32[]{:S(2)}) async-start(bf16[8,16,16,128]{3,2,1,0:T(8,128)(2,1)} %bitcast.70), calls=%async_computation.3 | async-start | bytes 1048576 | tf_op jit(solution)/shard_map/all_to_all | solution.py:51
  85.6 1.7 %reduce-precision_convert_fusion = (bf16[4096,128]{1,0:T(8,128)(2,1)}, bf16[4096,128]{1,0:T(8,128)(2,1)}) fusion(f32[32,128,128]{2,1,0:T(8,128)S(1)} %fusion.34), kind=kLoop, calls=%fused_computation.14 | loop fusion | flops 2097152 | bytes 4194304 | tf_op jit(solution)/shard_map/convert_element_type | solution.py:39
  87.3 7.8 %all-to-all-done.3 = bf16[8,16,16,128]{3,2,1,0:T(8,128)(2,1)S(1)} async-done(((bf16[8,16,16,128]{3,2,1,0:T(8,128)(2,1)}), bf16[8,16,16,128]{3,2,1,0:T(8,128)(2,1)S(1)}, u32[]{:S(2)}, u32[]{:S(2)}) %all-to-all-start.3) | async-done | bytes 524320 | tf_op jit(solution)/shard_map/all_to_all | solution.py:51
  95.1 0.7 convert_reduce_fusion
  95.8 3.7 %all-to-all-start.4 = ((f32[16,16,128]{2,1,0:T(8,128)}), f32[16,16,128]{2,1,0:T(8,128)S(1)}, u32[]{:S(2)}, u32[]{:S(2)}) async-start(f32[16,16,128]{2,1,0:T(8,128)} %convert_reduce_fusion), calls=%async_computation.4 | async-start | bytes 262144 | tf_op jit(solution)/shard_map/all_to_all | solution.py:53
  99.5 4.2 %fusion = f32[256,1024]{1,0:T(8,128)S(1)} fusion(s32[4096]{0:T(1024)S(1)} %copy-done.6, bf16[4096,128]{1,0:T(8,128)(2,1)} %get-tuple-element.4, bf16[4096,128]{1,0:T(8,128)(2,1)} %get-tuple-element.3), kind=kOutput, calls=%fused_computation.2 | convolution fusion | flops 2155872256 | bytes 3162112 | tf_op jit(solution)/shard_map/pc,pt->ct/dot_general | solution.py:40
  103.8 0.8 slice_add_fusion
  104.6 6.9 %all-to-all-done.4 = f32[16,16,128]{2,1,0:T(8,128)S(1)} async-done(((f32[16,16,128]{2,1,0:T(8,128)}), f32[16,16,128]{2,1,0:T(8,128)S(1)}, u32[]{:S(2)}, u32[]{:S(2)}) %all-to-all-start.4) | async-done | bytes 131104 | tf_op jit(solution)/shard_map/all_to_all | solution.py:53
  111.5 4.0 %all-to-all-start.2 = ((f32[4,32,1024]{2,1,0:T(8,128)}), f32[4,32,1024]{2,1,0:T(8,128)S(1)}, u32[]{:S(2)}, u32[]{:S(2)}) async-start(f32[4,32,1024]{2,1,0:T(8,128)} %bitcast.12), calls=%async_computation.2 | async-start | bytes 1048576 | tf_op jit(solution)/shard_map/all_to_all | solution.py:140
  115.6 6.9 %all-to-all-done.2 = f32[4,32,1024]{2,1,0:T(8,128)S(1)} async-done(((f32[4,32,1024]{2,1,0:T(8,128)}), f32[4,32,1024]{2,1,0:T(8,128)S(1)}, u32[]{:S(2)}, u32[]{:S(2)}) %all-to-all-start.2) | async-done | bytes 524320 | tf_op jit(solution)/shard_map/all_to_all | solution.py:140
  122.5 17.6 %all_to_all.45 = bf16[16,16,128]{2,1,0:T(8,128)(2,1)S(1)} all-to-all(bf16[16,16,128]{2,1,0:T(8,128)(2,1)S(1)} %broadcast_in_dim.35), channel_id=1, replica_groups=mesh['z'=16,'y'=4,'core'=2,'ch'=4] {'z'}, dimensions={0} | all-to-all | bytes 131072 | tf_op jit(solution)/shard_map/all_to_all | solution.py:56
  140.1 0.8 broadcast_in_dim.36
  140.9 7.8 %all-to-all-start.6 = ((bf16[8,16,16,128]{3,2,1,0:T(8,128)(2,1)}), bf16[8,16,16,128]{3,2,1,0:T(8,128)(2,1)S(1)}, u32[]{:S(2)}, u32[]{:S(2)}) async-start(bf16[8,16,16,128]{3,2,1,0:T(8,128)(2,1)} %broadcast_in_dim.36), calls=%async_computation.6 | async-start | bytes 1048576 | tf_op jit(solution)/shard_map/all_to_all | solution.py:58
  148.7 0.6 select_convert_fusion
  149.4 8.8 %all-to-all-done.6 = bf16[8,16,16,128]{3,2,1,0:T(8,128)(2,1)S(1)} async-done(((bf16[8,16,16,128]{3,2,1,0:T(8,128)(2,1)}), bf16[8,16,16,128]{3,2,1,0:T(8,128)(2,1)S(1)}, u32[]{:S(2)}, u32[]{:S(2)}) %all-to-all-start.6) | async-done | bytes 524320 | tf_op jit(solution)/shard_map/all_to_all | solution.py:58
  158.2 0.8 slice.35
  (22 shorter events, 0.2 us)
Async XLA Ops:
  0.6 4.1 %copy-start = (bf16[27,64,128]{2,1,0:T(8,128)(2,1)S(1)}, bf16[27,64,128]{2,1,0:T(8,128)(2,1)}, u32[]{:S(2)}) copy-start(bf16[27,64,128]{2,1,0:T(8,128)(2,1)} %param.10) | copy-start | bytes 1327108
  0.6 4.8 %copy-start.6 = (s32[4096]{0:T(1024)S(1)}, s32[4096]{0:T(1024)}, u32[]{:S(2)}) copy-start(s32[4096]{0:T(1024)} %param.12) | copy-start | bytes 49156
  0.7 4.8 %copy-start.3 = (bf16[1024,128]{1,0:T(8,128)(2,1)S(1)}, bf16[1024,128]{1,0:T(8,128)(2,1)}, u32[]{:S(2)}) copy-start(bf16[1024,128]{1,0:T(8,128)(2,1)} %param.9) | copy-start | bytes 786436
  8.5 1.0 copy-start.5
  9.5 39.3 %copy-start.7 = (s32[768]{0:T(1024)S(1)}, s32[768]{0:T(1024)}, u32[]{:S(2)}) copy-start(s32[768]{0:T(1024)} %param.16) | copy-start | bytes 9220
  11.1 38.9 %copy-start.4 = (bf16[64,512]{1,0:T(8,128)(2,1)S(1)}, bf16[64,512]{1,0:T(8,128)(2,1)}, u32[]{:S(2)}) copy-start(bf16[64,512]{1,0:T(8,128)(2,1)} %param.11) | copy-start | bytes 196612
  76.2 0.8 copy-start.1
  77.4 1.6 copy-start.2
  81.2 13.9 %all-to-all-start.3 = ((bf16[8,16,16,128]{3,2,1,0:T(8,128)(2,1)}), bf16[8,16,16,128]{3,2,1,0:T(8,128)(2,1)S(1)}, u32[]{:S(2)}, u32[]{:S(2)}) async-start(bf16[8,16,16,128]{3,2,1,0:T(8,128)(2,1)} %bitcast.70), calls=%async_computation.3 | async-start | bytes 1048576 | tf_op jit(solution)/shard_map/all_to_all | solution.py:51
  95.8 15.7 %all-to-all-start.4 = ((f32[16,16,128]{2,1,0:T(8,128)}), f32[16,16,128]{2,1,0:T(8,128)S(1)}, u32[]{:S(2)}, u32[]{:S(2)}) async-start(f32[16,16,128]{2,1,0:T(8,128)} %convert_reduce_fusion), calls=%async_computation.4 | async-start | bytes 262144 | tf_op jit(solution)/shard_map/all_to_all | solution.py:53
  111.5 10.9 %all-to-all-start.2 = ((f32[4,32,1024]{2,1,0:T(8,128)}), f32[4,32,1024]{2,1,0:T(8,128)S(1)}, u32[]{:S(2)}, u32[]{:S(2)}) async-start(f32[4,32,1024]{2,1,0:T(8,128)} %bitcast.12), calls=%async_computation.2 | async-start | bytes 1048576 | tf_op jit(solution)/shard_map/all_to_all | solution.py:140
  140.9 17.3 %all-to-all-start.6 = ((bf16[8,16,16,128]{3,2,1,0:T(8,128)(2,1)}), bf16[8,16,16,128]{3,2,1,0:T(8,128)(2,1)S(1)}, u32[]{:S(2)}, u32[]{:S(2)}) async-start(bf16[8,16,16,128]{3,2,1,0:T(8,128)(2,1)} %broadcast_in_dim.36), calls=%async_computation.6 | async-start | bytes 1048576 | tf_op jit(solution)/shard_map/all_to_all | solution.py:58

commit v11 on v10

--- a/solution.py
+++ b/solution.py
@@ -137,7 +137,8 @@
     )
     groups = lax.axis_size("ch")
     fine_parts = fine_sum.reshape(groups, width_in // groups, fine_total)
-    fine_grad = lax.all_to_all(fine_parts, "ch", 0, 0, tiled=True).sum(axis=0)
+    fine_parts = lax.all_to_all(fine_parts.astype(jnp.bfloat16), "ch", 0, 0, tiled=True)
+    fine_grad = fine_parts.astype(jnp.float32).sum(axis=0)
     grad_features = jnp.where(live_mask[None, :], fine_grad, jnp.zeros((), jnp.float32)).astype(
         jnp.bfloat16
     )

time: 160 us -> 158 us (0.988)
  no operation moved by 1% of the time
where the time goes in v11:
time: 158 us; the launch traced here: 157 us
  blocking collectives  76.8 us (49%)
  waiting for transfers between devices  29.1 us (18%)
  starting transfers between devices  20.2 us (13%)
  matrix products  17.1 us (11%)
  other arithmetic  6.56 us (4%)
  local copies, waits for them, and re-layouts  5.87 us (4%)
  between operations  1.6 us (1%)
    all_to_all x2, blocking collectives, flat_all_to_all(): return lax.all_to_all(x, VOX, 0, 0, tiled=True)  59.8 us
    all_to_all x1, blocking collectives, reduce_replicate(): mine = lax.all_to_all(mine, VOX[0], 0, 0, tiled=True)  16.9 us
    all_to_all x1, waiting for transfers between devices, reduce_replicate(): mine = lax.all_to_all(mine, VOX[1:], 0, 0, tiled=True)  8.81 us
    all_to_all x1, starting transfers between devices, reduce_replicate(): mine = lax.all_to_all(mine, VOX[1:], 0, 0, tiled=True)  8.07 us
    all_to_all x1, waiting for transfers between devices, reduce_replicate(): part = lax.all_to_all(part.astype(jnp.bfloat16), VOX[1:], 0, 0, tiled=True)  7.81 us
    all_to_all x1, waiting for transfers between devices, reduce_replicate(): part = lax.all_to_all(part, VOX[0], 0, 0, tiled=True).sum(axis=0)  6.97 us
    all_to_all x1, waiting for transfers between devices, body(): lax.all_to_all(fine_parts.astype(jnp.bfloat16), 'ch', 0, 0, tiled=True)  5.5 us
    all_to_all x1, starting transfers between devices, reduce_replicate(): part = lax.all_to_all(part.astype(jnp.bfloat16), VOX[1:], 0, 0, tiled=True)  4.4 us
  transfers between devices with their start and end apart: 4, of which 4 were waited for; matrix products, arithmetic and copies ran while one was open for 5% of the time, Pallas kernels for 0%

profile of v11, /device:TPU:1, one launch (start us, length us, event | category | flops | bytes accessed | tf_op | source)
XLA Modules:
  0.0 157.2 jit_solution(18303648737577568655)
XLA Ops:
  0.6 0.0 copy-start
  1.4 0.7 compare_select_fusion
  2.1 0.8 copy.21
  2.8 0.2 fusion.42
  3.2 0.9 fusion.40
  4.1 0.7 multiply_add_fusion
  4.8 0.6 gather_fusion
  5.4 3.1 %fusion.6 = bf16[4096,128]{1,0:T(8,128)(2,1)S(1)} fusion(s32[4096]{0:T(1024)S(1)} %copy-done.6, bf16[1024,128]{1,0:T(8,128)(2,1)S(1)} %copy-done.3, pred[1024]{0:T(1024)(128)(4,1)S(1)} %iota_compare_fusion.30), kind=kOutput, calls=%fused_computation.9 | convolution fusion | flops 1078591488 | bytes 1328128 | tf_op jit(solution)/shard_map/dot_general | solution.py:89
  8.5 0.0 copy-start.5
  8.5 0.8 convolution_bitcast_fusion
  9.4 0.2 reduce-precision_convert_fusion.1
  9.5 0.0 copy-start.7
  9.5 1.5 fusion.5
  11.1 0.0 copy-start.4
  11.1 0.5 fusion.20
  11.5 0.2 copy.24
  11.7 0.2 all_to_all.27
  11.9 36.8 %all_to_all.43 = bf16[128,3,128]{2,1,0:T(4,128)(2,1)S(1)} all-to-all(bf16[128,3,128]{2,1,0:T(4,128)(2,1)S(1)} %all_to_all.27), channel_id=1, replica_groups=mesh['z'=16,'y'=4,'core'=2,'ch'=4] {'z','y','core'}, dimensions={0} | all-to-all | bytes 196608 | tf_op jit(solution)/shard_map/all_to_all | solution.py:33
  48.7 0.1 reshape.81
  48.8 1.2 fusion.53
  50.0 0.5 fusion.19
  50.5 0.2 copy.25
  50.7 0.2 all_to_all.29
  50.8 23.1 %all_to_all.44 = bf16[128,3,128]{2,1,0:T(4,128)(2,1)S(1)} all-to-all(bf16[128,3,128]{2,1,0:T(4,128)(2,1)S(1)} %all_to_all.29), channel_id=1, replica_groups=mesh['z'=16,'y'=4,'core'=2,'ch'=4] {'z','y','core'}, dimensions={0} | all-to-all | bytes 196608 | tf_op jit(solution)/shard_map/all_to_all | solution.py:33
  73.9 0.1 reshape.82
  74.0 2.1 %fusion.18 = bf16[8,32,8,128]{3,2,1,0:T(8,128)(2,1)S(1)} fusion(s32[4096]{0:T(1024)S(1)} %copy-done.5, bf16[768,64]{1,0:T(8,128)(2,1)S(1)} %reshape.82, s32[512]{0:T(512)S(1)} %bitcast.80), kind=kOutput, calls=%fused_computation.29 | convolution fusion | flops 321552384 | bytes 641024 | tf_op jit(solution)/shard_map/pt,to->po/dot_general | solution.py:120
  76.2 0.8 copy-done.1
  77.0 0.4 fusion.32
  77.4 0.0 copy-start.2
  77.4 1.5 fusion.34
  78.9 1.3 convolution_convert_fusion
  80.2 1.0 copy.29
  81.2 4.4 %all-to-all-start.3 = ((bf16[8,16,16,128]{3,2,1,0:T(8,128)(2,1)}), bf16[8,16,16,128]{3,2,1,0:T(8,128)(2,1)S(1)}, u32[]{:S(2)}, u32[]{:S(2)}) async-start(bf16[8,16,16,128]{3,2,1,0:T(8,128)(2,1)} %bitcast.70), calls=%async_computation.3 | async-start | bytes 1048576 | tf_op jit(solution)/shard_map/all_to_all | solution.py:51
  85.6 1.7 %reduce-precision_convert_fusion = (bf16[4096,128]{1,0:T(8,128)(2,1)}, bf16[4096,128]{1,0:T(8,128)(2,1)}) fusion(f32[32,128,128]{2,1,0:T(8,128)S(1)} %fusion.34), kind=kLoop, calls=%fused_computation.14 | loop fusion | flops 2097152 | bytes 4194304 | tf_op jit(solution)/shard_map/convert_element_type | solution.py:39
  87.3 7.8 %all-to-all-done.3 = bf16[8,16,16,128]{3,2,1,0:T(8,128)(2,1)S(1)} async-done(((bf16[8,16,16,128]{3,2,1,0:T(8,128)(2,1)}), bf16[8,16,16,128]{3,2,1,0:T(8,128)(2,1)S(1)}, u32[]{:S(2)}, u32[]{:S(2)}) %all-to-all-start.3) | async-done | bytes 524320 | tf_op jit(solution)/shard_map/all_to_all | solution.py:51
  95.1 0.7 convert_reduce_fusion
  95.8 3.7 %all-to-all-start.4 = ((f32[16,16,128]{2,1,0:T(8,128)}), f32[16,16,128]{2,1,0:T(8,128)S(1)}, u32[]{:S(2)}, u32[]{:S(2)}) async-start(f32[16,16,128]{2,1,0:T(8,128)} %convert_reduce_fusion), calls=%async_computation.4 | async-start | bytes 262144 | tf_op jit(solution)/shard_map/all_to_all | solution.py:53
  99.6 4.2 %fusion = f32[256,1024]{1,0:T(8,128)S(1)} fusion(s32[4096]{0:T(1024)S(1)} %copy-done.6, bf16[4096,128]{1,0:T(8,128)(2,1)} %get-tuple-element.4, bf16[4096,128]{1,0:T(8,128)(2,1)} %get-tuple-element.3), kind=kOutput, calls=%fused_computation.2 | convolution fusion | flops 2155872256 | bytes 3162112 | tf_op jit(solution)/shard_map/pc,pt->ct/dot_general | solution.py:40
  103.8 0.8 fusion.36
  104.6 7.0 %all-to-all-done.4 = f32[16,16,128]{2,1,0:T(8,128)S(1)} async-done(((f32[16,16,128]{2,1,0:T(8,128)}), f32[16,16,128]{2,1,0:T(8,128)S(1)}, u32[]{:S(2)}, u32[]{:S(2)}) %all-to-all-start.4) | async-done | bytes 131104 | tf_op jit(solution)/shard_map/all_to_all | solution.py:53
  111.5 4.0 %all-to-all-start.2 = ((bf16[4,32,1024]{2,1,0:T(8,128)(2,1)}), bf16[4,32,1024]{2,1,0:T(8,128)(2,1)S(1)}, u32[]{:S(2)}, u32[]{:S(2)}) async-start(bf16[4,32,1024]{2,1,0:T(8,128)(2,1)} %bitcast.12), calls=%async_computation.2 | async-start | bytes 524288 | tf_op jit(solution)/shard_map/all_to_all | solution.py:140
  115.6 5.5 %all-to-all-done.2 = bf16[4,32,1024]{2,1,0:T(8,128)(2,1)S(1)} async-done(((bf16[4,32,1024]{2,1,0:T(8,128)(2,1)}), bf16[4,32,1024]{2,1,0:T(8,128)(2,1)S(1)}, u32[]{:S(2)}, u32[]{:S(2)}) %all-to-all-start.2) | async-done | bytes 262176 | tf_op jit(solution)/shard_map/all_to_all | solution.py:140
  121.1 16.9 %all_to_all.45 = bf16[16,16,128]{2,1,0:T(8,128)(2,1)S(1)} all-to-all(bf16[16,16,128]{2,1,0:T(8,128)(2,1)S(1)} %broadcast_in_dim.35), channel_id=1, replica_groups=mesh['z'=16,'y'=4,'core'=2,'ch'=4] {'z'}, dimensions={0} | all-to-all | bytes 131072 | tf_op jit(solution)/shard_map/all_to_all | solution.py:56
  138.0 0.8 broadcast_in_dim.36
  138.9 8.1 %all-to-all-start.6 = ((bf16[8,16,16,128]{3,2,1,0:T(8,128)(2,1)}), bf16[8,16,16,128]{3,2,1,0:T(8,128)(2,1)S(1)}, u32[]{:S(2)}, u32[]{:S(2)}) async-start(bf16[8,16,16,128]{3,2,1,0:T(8,128)(2,1)} %broadcast_in_dim.36), calls=%async_computation.6 | async-start | bytes 1048576 | tf_op jit(solution)/shard_map/all_to_all | solution.py:58
  147.0 0.6 select_convert_fusion
  147.6 8.8 %all-to-all-done.6 = bf16[8,16,16,128]{3,2,1,0:T(8,128)(2,1)S(1)} async-done(((bf16[8,16,16,128]{3,2,1,0:T(8,128)(2,1)}), bf16[8,16,16,128]{3,2,1,0:T(8,128)(2,1)S(1)}, u32[]{:S(2)}, u32[]{:S(2)}) %all-to-all-start.6) | async-done | bytes 524320 | tf_op jit(solution)/shard_map/all_to_all | solution.py:58
  156.4 0.8 slice.35
  (22 shorter events, 0.2 us)
Async XLA Ops:
  0.6 4.1 %copy-start = (bf16[27,64,128]{2,1,0:T(8,128)(2,1)S(1)}, bf16[27,64,128]{2,1,0:T(8,128)(2,1)}, u32[]{:S(2)}) copy-start(bf16[27,64,128]{2,1,0:T(8,128)(2,1)} %param.10) | copy-start | bytes 1327108
  0.6 4.8 %copy-start.6 = (s32[4096]{0:T(1024)S(1)}, s32[4096]{0:T(1024)}, u32[]{:S(2)}) copy-start(s32[4096]{0:T(1024)} %param.12) | copy-start | bytes 49156
  0.7 4.8 %copy-start.3 = (bf16[1024,128]{1,0:T(8,128)(2,1)S(1)}, bf16[1024,128]{1,0:T(8,128)(2,1)}, u32[]{:S(2)}) copy-start(bf16[1024,128]{1,0:T(8,128)(2,1)} %param.9) | copy-start | bytes 786436
  8.5 1.0 copy-start.5
  9.5 39.3 %copy-start.7 = (s32[768]{0:T(1024)S(1)}, s32[768]{0:T(1024)}, u32[]{:S(2)}) copy-start(s32[768]{0:T(1024)} %param.16) | copy-start | bytes 9220
  11.1 38.9 %copy-start.4 = (bf16[64,512]{1,0:T(8,128)(2,1)S(1)}, bf16[64,512]{1,0:T(8,128)(2,1)}, u32[]{:S(2)}) copy-start(bf16[64,512]{1,0:T(8,128)(2,1)} %param.11) | copy-start | bytes 196612
  76.2 0.8 copy-start.1
  77.4 1.6 copy-start.2
  81.2 13.9 %all-to-all-start.3 = ((bf16[8,16,16,128]{3,2,1,0:T(8,128)(2,1)}), bf16[8,16,16,128]{3,2,1,0:T(8,128)(2,1)S(1)}, u32[]{:S(2)}, u32[]{:S(2)}) async-start(bf16[8,16,16,128]{3,2,1,0:T(8,128)(2,1)} %bitcast.70), calls=%async_computation.3 | async-start | bytes 1048576 | tf_op jit(solution)/shard_map/all_to_all | solution.py:51
  95.8 15.7 %all-to-all-start.4 = ((f32[16,16,128]{2,1,0:T(8,128)}), f32[16,16,128]{2,1,0:T(8,128)S(1)}, u32[]{:S(2)}, u32[]{:S(2)}) async-start(f32[16,16,128]{2,1,0:T(8,128)} %convert_reduce_fusion), calls=%async_computation.4 | async-start | bytes 262144 | tf_op jit(solution)/shard_map/all_to_all | solution.py:53
  111.5 9.5 %all-to-all-start.2 = ((bf16[4,32,1024]{2,1,0:T(8,128)(2,1)}), bf16[4,32,1024]{2,1,0:T(8,128)(2,1)S(1)}, u32[]{:S(2)}, u32[]{:S(2)}) async-start(bf16[4,32,1024]{2,1,0:T(8,128)(2,1)} %bitcast.12), calls=%async_computation.2 | async-start | bytes 524288 | tf_op jit(solution)/shard_map/all_to_all | solution.py:140
  138.9 17.6 %all-to-all-start.6 = ((bf16[8,16,16,128]{3,2,1,0:T(8,128)(2,1)}), bf16[8,16,16,128]{3,2,1,0:T(8,128)(2,1)S(1)}, u32[]{:S(2)}, u32[]{:S(2)}) async-start(bf16[8,16,16,128]{3,2,1,0:T(8,128)(2,1)} %broadcast_in_dim.36), calls=%async_computation.6 | async-start | bytes 1048576 | tf_op jit(solution)/shard_map/all_to_all | solution.py:58

commit v12 on v10

--- a/solution.py
+++ b/solution.py
@@ -137,7 +137,12 @@
     )
     groups = lax.axis_size("ch")
     fine_parts = fine_sum.reshape(groups, width_in // groups, fine_total)
-    fine_grad = lax.all_to_all(fine_parts, "ch", 0, 0, tiled=True).sum(axis=0)
+    me = lax.axis_index("ch")
+    fine_grad = lax.dynamic_index_in_dim(fine_parts, me, 0, keepdims=False)
+    for shift in range(1, groups):
+        outgoing = lax.dynamic_index_in_dim(fine_parts, (me + shift) % groups, 0, keepdims=False)
+        pairs_of = [(i, (i + shift) % groups) for i in range(groups)]
+        fine_grad = fine_grad + lax.ppermute(outgoing, "ch", pairs_of)
     grad_features = jnp.where(live_mask[None, :], fine_grad, jnp.zeros((), jnp.float32)).astype(
         jnp.bfloat16
     )

time: 160 us -> 154 us (0.963)
  blocking collectives: 77.4 us -> 36.8 us
  starting transfers between devices: 19.9 us -> 37.4 us
  waiting for transfers between devices: 30.4 us -> 47.3 us
    all_to_all x2 -> x1, blocking collectives: 59.8 us -> 36.8 us  [flat_all_to_all(): return lax.all_to_all(x, VOX, 0, 0, tiled=True)]
    all_to_all x1 -> x2, waiting for transfers between devices: 6.9 us -> 27.5 us  [the longest x1 16 us: flat_all_to_all(): return lax.all_to_all(x, VOX, 0, 0, tiled=True)]
    all_to_all x1 -> x0, blocking collectives: 17.6 us -> none  [reduce_replicate(): mine = lax.all_to_all(mine, VOX[0], 0, 0, tiled=True)]
    ppermute x0 -> x3, starting transfers between devices: none -> 9.93 us  [body(): fine_grad = fine_grad + lax.ppermute(outgoing, 'ch', pairs_of)]
    all_to_all x1, waiting for transfers between devices: 8.82 us -> 0.01 us  [reduce_replicate(): mine = lax.all_to_all(mine, VOX[1:], 0, 0, tiled=True)]
    all_to_all x1 -> x2, starting transfers between devices: 4.01 us -> 12.4 us  [the longest x1 6.85 us: flat_all_to_all(): return lax.all_to_all(x, VOX, 0, 0, tiled=True)]
    ppermute x0 -> x3, waiting for transfers between devices: none -> 4.26 us  [body(): fine_grad = fine_grad + lax.ppermute(outgoing, 'ch', pairs_of)]
  transfers between devices with their start and end apart: 4 -> 8, of which waited for: 4 -> 5; matrix products, arithmetic and copies ran while one was open for 5% -> 4% of each run, Pallas kernels for 0% -> 0%
where the time goes in v12:
time: 154 us; the launch traced here: 153 us
  waiting for transfers between devices  47.3 us (31%)
  starting transfers between devices  37.4 us (24%)
  blocking collectives  36.8 us (24%)
  matrix products  17.1 us (11%)
  local copies, waits for them, and re-layouts  7.24 us (5%)
  other arithmetic  5.82 us (4%)
  between operations  1.7 us (1%)
    all_to_all x1, blocking collectives, flat_all_to_all(): return lax.all_to_all(x, VOX, 0, 0, tiled=True)  36.8 us
    all_to_all x1, waiting for transfers between devices, flat_all_to_all(): return lax.all_to_all(x, VOX, 0, 0, tiled=True)  16 us
    all_to_all x1, waiting for transfers between devices, reduce_replicate(): mine = lax.all_to_all(mine, VOX[0], 0, 0, tiled=True)  11.5 us
    ppermute x3, starting transfers between devices, body(): fine_grad = fine_grad + lax.ppermute(outgoing, 'ch', pairs_of)  9.93 us
    all_to_all x1, waiting for transfers between devices, reduce_replicate(): part = lax.all_to_all(part.astype(jnp.bfloat16), VOX[1:], 0, 0, tiled=True)  7.82 us
    all_to_all x1, waiting for transfers between devices, reduce_replicate(): part = lax.all_to_all(part, VOX[0], 0, 0, tiled=True).sum(axis=0)  7.73 us
    all_to_all x1, starting transfers between devices, flat_all_to_all(): return lax.all_to_all(x, VOX, 0, 0, tiled=True)  6.85 us
    all_to_all x1, starting transfers between devices, reduce_replicate(): mine = lax.all_to_all(mine, VOX[1:], 0, 0, tiled=True)  6.58 us
  transfers between devices with their start and end apart: 8, of which 5 were waited for; matrix products, arithmetic and copies ran while one was open for 4% of the time, Pallas kernels for 0%

profile of v12, /device:TPU:1, one launch (start us, length us, event | category | flops | bytes accessed | tf_op | source)
XLA Modules:
  0.0 153.4 jit_solution(3886444749184533632)
XLA Ops:
  0.6 0.0 copy-start
  1.4 0.7 compare_select_fusion
  2.1 0.8 copy.21
  2.8 0.2 fusion.41
  3.2 0.9 fusion.39
  4.1 0.7 multiply_add_fusion
  4.8 0.6 gather_fusion
  5.4 3.1 %fusion.6 = bf16[4096,128]{1,0:T(8,128)(2,1)S(1)} fusion(s32[4096]{0:T(1024)S(1)} %copy-done.6, bf16[1024,128]{1,0:T(8,128)(2,1)S(1)} %copy-done.3, pred[1024]{0:T(1024)(128)(4,1)S(1)} %iota_compare_fusion.30), kind=kOutput, calls=%fused_computation.9 | convolution fusion | flops 1078591488 | bytes 1328128 | tf_op jit(solution)/shard_map/dot_general | solution.py:89
  8.5 0.8 convolution_bitcast_fusion
  9.4 0.2 reduce-precision_convert_fusion.1
  9.5 1.5 fusion.5
  11.1 0.5 fusion.20
  11.5 0.2 copy.24
  11.7 0.2 all_to_all.24
  11.9 36.8 %all_to_all.38 = bf16[128,3,128]{2,1,0:T(4,128)(2,1)S(1)} all-to-all(bf16[128,3,128]{2,1,0:T(4,128)(2,1)S(1)} %all_to_all.24), channel_id=1, replica_groups=mesh['z'=16,'y'=4,'core'=2,'ch'=4] {'z','y','core'}, dimensions={0} | all-to-all | bytes 196608 | tf_op jit(solution)/shard_map/all_to_all | solution.py:33
  48.7 0.1 reshape.82
  48.8 1.2 fusion.56
  50.0 0.5 fusion.19
  50.5 0.2 copy.25
  50.7 0.8 all_to_all.26
  51.5 6.8 %all-to-all-start.1 = ((bf16[128,3,128]{2,1,0:T(4,128)(2,1)}), bf16[128,3,128]{2,1,0:T(4,128)(2,1)S(1)}, u32[]{:S(2)}, u32[]{:S(2)}) async-start(bf16[128,3,128]{2,1,0:T(4,128)(2,1)} %all_to_all.26), calls=%async_computation.1 | async-start | bytes 262144 | tf_op jit(solution)/shard_map/all_to_all | solution.py:33
  58.4 16.0 %all-to-all-done.1 = bf16[128,3,128]{2,1,0:T(4,128)(2,1)S(1)} async-done(((bf16[128,3,128]{2,1,0:T(4,128)(2,1)}), bf16[128,3,128]{2,1,0:T(4,128)(2,1)S(1)}, u32[]{:S(2)}, u32[]{:S(2)}) %all-to-all-start.1) | async-done | bytes 98336 | tf_op jit(solution)/shard_map/all_to_all | solution.py:33
  74.4 0.1 reshape.83
  74.5 2.1 %fusion.18 = bf16[8,32,8,128]{3,2,1,0:T(8,128)(2,1)S(1)} fusion(s32[4096]{0:T(1024)S(1)} %copy-done.5, bf16[768,64]{1,0:T(8,128)(2,1)S(1)} %reshape.83, s32[512]{0:T(512)S(1)} %bitcast.98), kind=kOutput, calls=%fused_computation.29 | convolution fusion | flops 321552384 | bytes 641024 | tf_op jit(solution)/shard_map/pt,to->po/dot_general | solution.py:120
  76.7 0.8 copy-done.1
  77.5 0.4 fusion.32
  77.9 1.5 %fusion.34 = f32[32,128,128]{2,1,0:T(8,128)S(1)} fusion(bf16[32,64,128]{2,1,0:T(8,128)(2,1)S(1)} %gather_fusion, bf16[8,32,8,128]{3,2,1,0:T(8,128)(2,1)} %copy-done.1), kind=kOutput, calls=%fused_computation.45 | convolution fusion | flops 67108864 | bytes 3145728 | tf_op jit(solution)/shard_map/bpo,boc->bpc/dot_general | solution.py:124
  79.4 1.3 convolution_convert_fusion
  80.7 1.0 copy.29
  81.7 4.8 %all-to-all-start.2 = ((bf16[8,16,16,128]{3,2,1,0:T(8,128)(2,1)}), bf16[8,16,16,128]{3,2,1,0:T(8,128)(2,1)S(1)}, u32[]{:S(2)}, u32[]{:S(2)}) async-start(bf16[8,16,16,128]{3,2,1,0:T(8,128)(2,1)} %bitcast.88), calls=%async_computation.2 | async-start | bytes 1048576 | tf_op jit(solution)/shard_map/all_to_all | solution.py:51
  86.5 1.7 %reduce-precision_convert_fusion = (bf16[4096,128]{1,0:T(8,128)(2,1)}, bf16[4096,128]{1,0:T(8,128)(2,1)}) fusion(f32[32,128,128]{2,1,0:T(8,128)S(1)} %fusion.34), kind=kLoop, calls=%fused_computation.14 | loop fusion | flops 2097152 | bytes 4194304 | tf_op jit(solution)/shard_map/convert_element_type | solution.py:39
  88.2 7.8 %all-to-all-done.2 = bf16[8,16,16,128]{3,2,1,0:T(8,128)(2,1)S(1)} async-done(((bf16[8,16,16,128]{3,2,1,0:T(8,128)(2,1)}), bf16[8,16,16,128]{3,2,1,0:T(8,128)(2,1)S(1)}, u32[]{:S(2)}, u32[]{:S(2)}) %all-to-all-start.2) | async-done | bytes 524320 | tf_op jit(solution)/shard_map/all_to_all | solution.py:51
  96.0 0.7 convert_reduce_fusion
  96.7 3.7 %all-to-all-start.3 = ((f32[16,16,128]{2,1,0:T(8,128)}), f32[16,16,128]{2,1,0:T(8,128)S(1)}, u32[]{:S(2)}, u32[]{:S(2)}) async-start(f32[16,16,128]{2,1,0:T(8,128)} %convert_reduce_fusion), calls=%async_computation.3 | async-start | bytes 262144 | tf_op jit(solution)/shard_map/all_to_all | solution.py:53
  100.4 4.2 %fusion = f32[256,1024]{1,0:T(8,128)S(1)} fusion(s32[4096]{0:T(1024)S(1)} %copy-done.6, bf16[4096,128]{1,0:T(8,128)(2,1)} %get-tuple-element.4, bf16[4096,128]{1,0:T(8,128)(2,1)} %get-tuple-element.3), kind=kOutput, calls=%fused_computation.2 | convolution fusion | flops 2155872256 | bytes 3162112 | tf_op jit(solution)/shard_map/pc,pt->ct/dot_general | solution.py:40
  104.7 7.7 %all-to-all-done.3 = f32[16,16,128]{2,1,0:T(8,128)S(1)} async-done(((f32[16,16,128]{2,1,0:T(8,128)}), f32[16,16,128]{2,1,0:T(8,128)S(1)}, u32[]{:S(2)}, u32[]{:S(2)}) %all-to-all-start.3) | async-done | bytes 131104 | tf_op jit(solution)/shard_map/all_to_all | solution.py:53
  112.4 0.6 broadcast_in_dim.35
  113.1 5.6 %all-to-all-start.4 = ((bf16[16,16,128]{2,1,0:T(8,128)(2,1)}), bf16[16,16,128]{2,1,0:T(8,128)(2,1)S(1)}, u32[]{:S(2)}, u32[]{:S(2)}) async-start(bf16[16,16,128]{2,1,0:T(8,128)(2,1)} %broadcast_in_dim.35), calls=%async_computation.4 | async-start | bytes 131072 | tf_op jit(solution)/shard_map/all_to_all | solution.py:56
  118.6 0.1 slice_add_fusion
  118.7 11.5 %all-to-all-done.4 = bf16[16,16,128]{2,1,0:T(8,128)(2,1)S(1)} async-done(((bf16[16,16,128]{2,1,0:T(8,128)(2,1)}), bf16[16,16,128]{2,1,0:T(8,128)(2,1)S(1)}, u32[]{:S(2)}, u32[]{:S(2)}) %all-to-all-start.4) | async-done | bytes 65568 | tf_op jit(solution)/shard_map/all_to_all | solution.py:56
  130.2 0.9 broadcast_in_dim.36
  131.1 6.6 %all-to-all-start.5 = ((bf16[8,16,16,128]{3,2,1,0:T(8,128)(2,1)}), bf16[8,16,16,128]{3,2,1,0:T(8,128)(2,1)S(1)}, u32[]{:S(2)}, u32[]{:S(2)}) async-start(bf16[8,16,16,128]{3,2,1,0:T(8,128)(2,1)} %broadcast_in_dim.36), calls=%async_computation.5 | async-start | bytes 1048576 | tf_op jit(solution)/shard_map/all_to_all | solution.py:58
  137.7 3.1 %collective-permute-start = (f32[32,1024]{1,0:T(8,128)S(1)}, f32[32,1024]{1,0:T(8,128)S(1)}, u32[]{:S(2)}, u32[]{:S(2)}) collective-permute-start(f32[32,1024]{1,0:T(8,128)S(1)} %get-tuple-element.7), channel_id=1, source_target_pairs={{0,1},{1,2},{2,3},{3,0},{4,5},{5,6},{6,7},{7,4},{8,9},{9,10},{10,1... | collective-permute-start | bytes 393224 | tf_op jit(solution)/shard_map/ppermute | solution.py:145
  140.8 3.4 %collective-permute-start.2 = (f32[32,1024]{1,0:T(8,128)S(1)}, f32[32,1024]{1,0:T(8,128)S(1)}, u32[]{:S(2)}, u32[]{:S(2)}) collective-permute-start(f32[32,1024]{1,0:T(8,128)S(1)} %get-tuple-element.8), channel_id=1, source_target_pairs={{0,3},{1,0},{2,1},{3,2},{4,7},{5,4},{6,5},{7,6},{8,11},{9,8},{10,9... | collective-permute-start | bytes 393224 | tf_op jit(solution)/shard_map/ppermute | solution.py:145
  144.2 3.4 %collective-permute-start.1 = (f32[32,1024]{1,0:T(8,128)S(1)}, f32[32,1024]{1,0:T(8,128)S(1)}, u32[]{:S(2)}, u32[]{:S(2)}) collective-permute-start(f32[32,1024]{1,0:T(8,128)S(1)} %get-tuple-element.9), channel_id=1, source_target_pairs={{0,2},{1,3},{2,0},{3,1},{4,6},{5,7},{6,4},{7,5},{8,10},{9,11},{10,... | collective-permute-start | bytes 393224 | tf_op jit(solution)/shard_map/ppermute | solution.py:145
  147.7 4.3 %collective-permute-done.1 = f32[32,1024]{1,0:T(8,128)S(1)} collective-permute-done((f32[32,1024]{1,0:T(8,128)S(1)}, f32[32,1024]{1,0:T(8,128)S(1)}, u32[]{:S(2)}, u32[]{:S(2)}) %collective-permute-start.1) | collective-permute-done | bytes 131104 | tf_op jit(solution)/shard_map/ppermute | solution.py:145
  151.9 0.7 fusion.48
  152.6 0.8 slice.35
  (28 shorter events, 0.2 us)
Async XLA Ops:
  0.6 4.1 %copy-start = (bf16[27,64,128]{2,1,0:T(8,128)(2,1)S(1)}, bf16[27,64,128]{2,1,0:T(8,128)(2,1)}, u32[]{:S(2)}) copy-start(bf16[27,64,128]{2,1,0:T(8,128)(2,1)} %param.10) | copy-start | bytes 1327108
  0.6 4.8 %copy-start.6 = (s32[4096]{0:T(1024)S(1)}, s32[4096]{0:T(1024)}, u32[]{:S(2)}) copy-start(s32[4096]{0:T(1024)} %param.12) | copy-start | bytes 49156
  0.7 4.8 %copy-start.3 = (bf16[1024,128]{1,0:T(8,128)(2,1)S(1)}, bf16[1024,128]{1,0:T(8,128)(2,1)}, u32[]{:S(2)}) copy-start(bf16[1024,128]{1,0:T(8,128)(2,1)} %param.9) | copy-start | bytes 786436
  8.5 1.0 copy-start.5
  9.5 39.3 %copy-start.7 = (s32[768]{0:T(1024)S(1)}, s32[768]{0:T(1024)}, u32[]{:S(2)}) copy-start(s32[768]{0:T(1024)} %param.16) | copy-start | bytes 9220
  11.1 38.9 %copy-start.4 = (bf16[64,512]{1,0:T(8,128)(2,1)S(1)}, bf16[64,512]{1,0:T(8,128)(2,1)}, u32[]{:S(2)}) copy-start(bf16[64,512]{1,0:T(8,128)(2,1)} %param.11) | copy-start | bytes 196612
  51.5 22.9 %all-to-all-start.1 = ((bf16[128,3,128]{2,1,0:T(4,128)(2,1)}), bf16[128,3,128]{2,1,0:T(4,128)(2,1)S(1)}, u32[]{:S(2)}, u32[]{:S(2)}) async-start(bf16[128,3,128]{2,1,0:T(4,128)(2,1)} %all_to_all.26), calls=%async_computation.1 | async-start | bytes 262144 | tf_op jit(solution)/shard_map/all_to_all | solution.py:33
  76.7 0.8 copy-start.1
  77.9 1.6 %copy-start.2 = (s32[32]{0:T(128)S(1)}, s32[32]{0:T(128)}, u32[]{:S(2)}) copy-start(s32[32]{0:T(128)} %param.14) | copy-start | bytes 388
  81.7 14.3 %all-to-all-start.2 = ((bf16[8,16,16,128]{3,2,1,0:T(8,128)(2,1)}), bf16[8,16,16,128]{3,2,1,0:T(8,128)(2,1)S(1)}, u32[]{:S(2)}, u32[]{:S(2)}) async-start(bf16[8,16,16,128]{3,2,1,0:T(8,128)(2,1)} %bitcast.88), calls=%async_computation.2 | async-start | bytes 1048576 | tf_op jit(solution)/shard_map/all_to_all | solution.py:51
  96.7 15.7 %all-to-all-start.3 = ((f32[16,16,128]{2,1,0:T(8,128)}), f32[16,16,128]{2,1,0:T(8,128)S(1)}, u32[]{:S(2)}, u32[]{:S(2)}) async-start(f32[16,16,128]{2,1,0:T(8,128)} %convert_reduce_fusion), calls=%async_computation.3 | async-start | bytes 262144 | tf_op jit(solution)/shard_map/all_to_all | solution.py:53
  113.1 17.1 %all-to-all-start.4 = ((bf16[16,16,128]{2,1,0:T(8,128)(2,1)}), bf16[16,16,128]{2,1,0:T(8,128)(2,1)S(1)}, u32[]{:S(2)}, u32[]{:S(2)}) async-start(bf16[16,16,128]{2,1,0:T(8,128)(2,1)} %broadcast_in_dim.35), calls=%async_computation.4 | async-start | bytes 131072 | tf_op jit(solution)/shard_map/all_to_all | solution.py:56
  131.1 21.5 %all-to-all-start.5 = ((bf16[8,16,16,128]{3,2,1,0:T(8,128)(2,1)}), bf16[8,16,16,128]{3,2,1,0:T(8,128)(2,1)S(1)}, u32[]{:S(2)}, u32[]{:S(2)}) async-start(bf16[8,16,16,128]{3,2,1,0:T(8,128)(2,1)} %broadcast_in_dim.36), calls=%async_computation.5 | async-start | bytes 1048576 | tf_op jit(solution)/shard_map/all_to_all | solution.py:58
  137.7 10.0 %collective-permute-start = (f32[32,1024]{1,0:T(8,128)S(1)}, f32[32,1024]{1,0:T(8,128)S(1)}, u32[]{:S(2)}, u32[]{:S(2)}) collective-permute-start(f32[32,1024]{1,0:T(8,128)S(1)} %get-tuple-element.7), channel_id=1, source_target_pairs={{0,1},{1,2},{2,3},{3,0},{4,5},{5,6},{6,7},{7,4},{8,9},{9,10},{10,1... | collective-permute-start | bytes 393224 | tf_op jit(solution)/shard_map/ppermute | solution.py:145
  140.8 6.9 %collective-permute-start.2 = (f32[32,1024]{1,0:T(8,128)S(1)}, f32[32,1024]{1,0:T(8,128)S(1)}, u32[]{:S(2)}, u32[]{:S(2)}) collective-permute-start(f32[32,1024]{1,0:T(8,128)S(1)} %get-tuple-element.8), channel_id=1, source_target_pairs={{0,3},{1,0},{2,1},{3,2},{4,7},{5,4},{6,5},{7,6},{8,11},{9,8},{10,9... | collective-permute-start | bytes 393224 | tf_op jit(solution)/shard_map/ppermute | solution.py:145
  144.2 7.7 %collective-permute-start.1 = (f32[32,1024]{1,0:T(8,128)S(1)}, f32[32,1024]{1,0:T(8,128)S(1)}, u32[]{:S(2)}, u32[]{:S(2)}) collective-permute-start(f32[32,1024]{1,0:T(8,128)S(1)} %get-tuple-element.9), channel_id=1, source_target_pairs={{0,2},{1,3},{2,0},{3,1},{4,6},{5,7},{6,4},{7,5},{8,10},{9,11},{10,... | collective-permute-start | bytes 393224 | tf_op jit(solution)/shard_map/ppermute | solution.py:145

commit v13 on v10

--- a/solution.py
+++ b/solution.py
@@ -137,7 +137,15 @@
     )
     groups = lax.axis_size("ch")
     fine_parts = fine_sum.reshape(groups, width_in // groups, fine_total)
-    fine_grad = lax.all_to_all(fine_parts, "ch", 0, 0, tiled=True).sum(axis=0)
+    me = lax.axis_index("ch")
+    high = jnp.bitwise_and(me, 2)
+    low = jnp.bitwise_and(me, 1)
+    kept = lax.dynamic_slice_in_dim(fine_parts, high, 2, axis=0)
+    sent = lax.dynamic_slice_in_dim(fine_parts, 2 - high, 2, axis=0)
+    kept = kept + lax.ppermute(sent, "ch", [(i, i ^ 2) for i in range(groups)])
+    fine_grad = lax.dynamic_index_in_dim(kept, low, 0, keepdims=False)
+    sent = lax.dynamic_index_in_dim(kept, 1 - low, 0, keepdims=False)
+    fine_grad = fine_grad + lax.ppermute(sent, "ch", [(i, i ^ 1) for i in range(groups)])
     grad_features = jnp.where(live_mask[None, :], fine_grad, jnp.zeros((), jnp.float32)).astype(
         jnp.bfloat16
     )

time: 160 us -> 152 us (0.950)
  blocking collectives: 77.4 us -> 36.8 us
  starting transfers between devices: 19.9 us -> 37.3 us
  waiting for transfers between devices: 30.4 us -> 45 us
    all_to_all x2 -> x1, blocking collectives: 59.8 us -> 36.8 us  [flat_all_to_all(): return lax.all_to_all(x, VOX, 0, 0, tiled=True)]
    all_to_all x1 -> x2, waiting for transfers between devices: 6.9 us -> 27.6 us  [the longest x1 16 us: flat_all_to_all(): return lax.all_to_all(x, VOX, 0, 0, tiled=True)]
    all_to_all x1 -> x0, blocking collectives: 17.6 us -> none  [reduce_replicate(): mine = lax.all_to_all(mine, VOX[0], 0, 0, tiled=True)]
    all_to_all x1 -> x2, starting transfers between devices: 4.01 us -> 15.3 us  [the longest x1 8.5 us: reduce_replicate(): mine = lax.all_to_all(mine, VOX[0], 0, 0, tiled=True)]
    ppermute x0 -> x2, starting transfers between devices: none -> 6.87 us  [the longest x1 4.65 us: body(): kept = kept + lax.ppermute(sent, 'ch', [(i, i ^ 2) for i in range(groups)])]
    all_to_all x1, waiting for transfers between devices: 8.82 us -> 1.98 us  [reduce_replicate(): mine = lax.all_to_all(mine, VOX[1:], 0, 0, tiled=True)]
    ppermute x0 -> x2, waiting for transfers between devices: none -> 4.63 us  [the longest x1 4.63 us: body(): lax.ppermute(sent, 'ch', [(i, i ^ 1) for i in range(groups)])]
    all_to_all x1, waiting for transfers between devices: 6.89 us -> 2.98 us  [reduce_replicate(): part = lax.all_to_all(part, VOX[0], 0, 0, tiled=True).sum(axis=0)]
  transfers between devices with their start and end apart: 4 -> 7, of which waited for: 4 -> 6; matrix products, arithmetic and copies ran while one was open for 5% -> 5% of each run, Pallas kernels for 0% -> 0%
where the time goes in v13:
time: 152 us; the launch traced here: 151 us
  waiting for transfers between devices  45 us (30%)
  starting transfers between devices  37.3 us (25%)
  blocking collectives  36.8 us (24%)
  matrix products  17.1 us (11%)
  local copies, waits for them, and re-layouts  7.27 us (5%)
  other arithmetic  5.84 us (4%)
  between operations  1.66 us (1%)
    all_to_all x1, blocking collectives, flat_all_to_all(): return lax.all_to_all(x, VOX, 0, 0, tiled=True)  36.8 us
    all_to_all x1, waiting for transfers between devices, flat_all_to_all(): return lax.all_to_all(x, VOX, 0, 0, tiled=True)  16 us
    all_to_all x1, waiting for transfers between devices, reduce_replicate(): mine = lax.all_to_all(mine, VOX[0], 0, 0, tiled=True)  11.5 us
    all_to_all x1, starting transfers between devices, reduce_replicate(): mine = lax.all_to_all(mine, VOX[0], 0, 0, tiled=True)  8.5 us
    all_to_all x1, waiting for transfers between devices, reduce_replicate(): part = lax.all_to_all(part.astype(jnp.bfloat16), VOX[1:], 0, 0, tiled=True)  7.81 us
    all_to_all x1, starting transfers between devices, flat_all_to_all(): return lax.all_to_all(x, VOX, 0, 0, tiled=True)  6.85 us
    all_to_all x1, starting transfers between devices, reduce_replicate(): mine = lax.all_to_all(mine, VOX[1:], 0, 0, tiled=True)  6.64 us
    all_to_all x1, starting transfers between devices, reduce_replicate(): part = lax.all_to_all(part.astype(jnp.bfloat16), VOX[1:], 0, 0, tiled=True)  4.77 us
  transfers between devices with their start and end apart: 7, of which 6 were waited for; matrix products, arithmetic and copies ran while one was open for 5% of the time, Pallas kernels for 0%

profile of v13, /device:TPU:1, one launch (start us, length us, event | category | flops | bytes accessed | tf_op | source)
XLA Modules:
  0.0 151.0 jit_solution(4414971656772768714)
XLA Ops:
  0.6 0.0 copy-start
  1.4 0.7 compare_select_fusion
  2.1 0.8 copy.21
  2.8 0.2 fusion.41
  3.2 0.9 fusion.39
  4.1 0.7 multiply_add_fusion
  4.8 0.6 gather_fusion
  5.4 3.1 %fusion.6 = bf16[4096,128]{1,0:T(8,128)(2,1)S(1)} fusion(s32[4096]{0:T(1024)S(1)} %copy-done.6, bf16[1024,128]{1,0:T(8,128)(2,1)S(1)} %copy-done.3, pred[1024]{0:T(1024)(128)(4,1)S(1)} %iota_compare_fusion.30), kind=kOutput, calls=%fused_computation.9 | convolution fusion | flops 1078591488 | bytes 1328128 | tf_op jit(solution)/shard_map/dot_general | solution.py:89
  8.5 0.8 convolution_bitcast_fusion
  9.4 0.2 reduce-precision_convert_fusion.1
  9.5 1.5 fusion.5
  11.1 0.5 fusion.20
  11.5 0.2 copy.24
  11.7 0.2 all_to_all.24
  11.9 36.8 %all_to_all.38 = bf16[128,3,128]{2,1,0:T(4,128)(2,1)S(1)} all-to-all(bf16[128,3,128]{2,1,0:T(4,128)(2,1)S(1)} %all_to_all.24), channel_id=1, replica_groups=mesh['z'=16,'y'=4,'core'=2,'ch'=4] {'z','y','core'}, dimensions={0} | all-to-all | bytes 196608 | tf_op jit(solution)/shard_map/all_to_all | solution.py:33
  48.7 0.1 reshape.82
  48.8 1.2 fusion.54
  50.0 0.5 fusion.19
  50.5 0.2 copy.25
  50.7 0.8 all_to_all.26
  51.5 6.8 %all-to-all-start.1 = ((bf16[128,3,128]{2,1,0:T(4,128)(2,1)}), bf16[128,3,128]{2,1,0:T(4,128)(2,1)S(1)}, u32[]{:S(2)}, u32[]{:S(2)}) async-start(bf16[128,3,128]{2,1,0:T(4,128)(2,1)} %all_to_all.26), calls=%async_computation.1 | async-start | bytes 262144 | tf_op jit(solution)/shard_map/all_to_all | solution.py:33
  58.4 16.0 %all-to-all-done.1 = bf16[128,3,128]{2,1,0:T(4,128)(2,1)S(1)} async-done(((bf16[128,3,128]{2,1,0:T(4,128)(2,1)}), bf16[128,3,128]{2,1,0:T(4,128)(2,1)S(1)}, u32[]{:S(2)}, u32[]{:S(2)}) %all-to-all-start.1) | async-done | bytes 98336 | tf_op jit(solution)/shard_map/all_to_all | solution.py:33
  74.4 0.1 reshape.83
  74.5 2.1 %fusion.18 = bf16[8,32,8,128]{3,2,1,0:T(8,128)(2,1)S(1)} fusion(s32[4096]{0:T(1024)S(1)} %copy-done.5, bf16[768,64]{1,0:T(8,128)(2,1)S(1)} %reshape.83, s32[512]{0:T(512)S(1)} %bitcast.90), kind=kOutput, calls=%fused_computation.29 | convolution fusion | flops 321552384 | bytes 641024 | tf_op jit(solution)/shard_map/pt,to->po/dot_general | solution.py:120
  76.7 0.8 copy-done.1
  77.5 0.4 fusion.32
  77.9 1.5 %fusion.34 = f32[32,128,128]{2,1,0:T(8,128)S(1)} fusion(bf16[32,64,128]{2,1,0:T(8,128)(2,1)S(1)} %gather_fusion, bf16[8,32,8,128]{3,2,1,0:T(8,128)(2,1)} %copy-done.1), kind=kOutput, calls=%fused_computation.45 | convolution fusion | flops 67108864 | bytes 3145728 | tf_op jit(solution)/shard_map/bpo,boc->bpc/dot_general | solution.py:124
  79.4 1.3 convolution_convert_fusion
  80.7 1.0 copy.29
  81.8 4.8 %all-to-all-start.2 = ((bf16[8,16,16,128]{3,2,1,0:T(8,128)(2,1)}), bf16[8,16,16,128]{3,2,1,0:T(8,128)(2,1)S(1)}, u32[]{:S(2)}, u32[]{:S(2)}) async-start(bf16[8,16,16,128]{3,2,1,0:T(8,128)(2,1)} %bitcast.80), calls=%async_computation.2 | async-start | bytes 1048576 | tf_op jit(solution)/shard_map/all_to_all | solution.py:51
  86.5 1.7 %reduce-precision_convert_fusion = (bf16[4096,128]{1,0:T(8,128)(2,1)}, bf16[4096,128]{1,0:T(8,128)(2,1)}) fusion(f32[32,128,128]{2,1,0:T(8,128)S(1)} %fusion.34), kind=kLoop, calls=%fused_computation.14 | loop fusion | flops 2097152 | bytes 4194304 | tf_op jit(solution)/shard_map/convert_element_type | solution.py:39
  88.2 7.8 %all-to-all-done.2 = bf16[8,16,16,128]{3,2,1,0:T(8,128)(2,1)S(1)} async-done(((bf16[8,16,16,128]{3,2,1,0:T(8,128)(2,1)}), bf16[8,16,16,128]{3,2,1,0:T(8,128)(2,1)S(1)}, u32[]{:S(2)}, u32[]{:S(2)}) %all-to-all-start.2) | async-done | bytes 524320 | tf_op jit(solution)/shard_map/all_to_all | solution.py:51
  96.0 0.7 convert_reduce_fusion
  96.7 3.7 %all-to-all-start.3 = ((f32[16,16,128]{2,1,0:T(8,128)}), f32[16,16,128]{2,1,0:T(8,128)S(1)}, u32[]{:S(2)}, u32[]{:S(2)}) async-start(f32[16,16,128]{2,1,0:T(8,128)} %convert_reduce_fusion), calls=%async_computation.3 | async-start | bytes 262144 | tf_op jit(solution)/shard_map/all_to_all | solution.py:53
  100.4 4.2 %fusion = f32[256,1024]{1,0:T(8,128)S(1)} fusion(s32[4096]{0:T(1024)S(1)} %copy-done.6, bf16[4096,128]{1,0:T(8,128)(2,1)} %get-tuple-element.4, bf16[4096,128]{1,0:T(8,128)(2,1)} %get-tuple-element.3), kind=kOutput, calls=%fused_computation.2 | convolution fusion | flops 2155872256 | bytes 3162112 | tf_op jit(solution)/shard_map/pc,pt->ct/dot_general | solution.py:40
  104.7 0.1 slice_add_fusion
  104.8 4.6 %collective-permute-start = (f32[2,32,1024]{2,1,0:T(8,128)S(1)}, f32[2,32,1024]{2,1,0:T(8,128)S(1)}, u32[]{:S(2)}, u32[]{:S(2)}) collective-permute-start(f32[2,32,1024]{2,1,0:T(8,128)S(1)} %constant_dynamic-slice_fusion), channel_id=1, source_target_pairs={{0,2},{1,3},{2,0},{3,1},{4,6},{5,7},{6,4},{7,5},{8,10},{9,11},{10,... | collective-permute-start | bytes 786440 | tf_op jit(solution)/shard_map/ppermute | solution.py:145
  109.4 3.0 %all-to-all-done.3 = f32[16,16,128]{2,1,0:T(8,128)S(1)} async-done(((f32[16,16,128]{2,1,0:T(8,128)}), f32[16,16,128]{2,1,0:T(8,128)S(1)}, u32[]{:S(2)}, u32[]{:S(2)}) %all-to-all-start.3) | async-done | bytes 131104 | tf_op jit(solution)/shard_map/all_to_all | solution.py:53
  112.4 0.6 broadcast_in_dim.35
  113.1 8.5 %all-to-all-start.4 = ((bf16[16,16,128]{2,1,0:T(8,128)(2,1)}), bf16[16,16,128]{2,1,0:T(8,128)(2,1)S(1)}, u32[]{:S(2)}, u32[]{:S(2)}) async-start(bf16[16,16,128]{2,1,0:T(8,128)(2,1)} %broadcast_in_dim.35), calls=%async_computation.4 | async-start | bytes 131072 | tf_op jit(solution)/shard_map/all_to_all | solution.py:56
  121.6 11.5 %all-to-all-done.4 = bf16[16,16,128]{2,1,0:T(8,128)(2,1)S(1)} async-done(((bf16[16,16,128]{2,1,0:T(8,128)(2,1)}), bf16[16,16,128]{2,1,0:T(8,128)(2,1)S(1)}, u32[]{:S(2)}, u32[]{:S(2)}) %all-to-all-start.4) | async-done | bytes 65568 | tf_op jit(solution)/shard_map/all_to_all | solution.py:56
  133.2 0.9 broadcast_in_dim.36
  134.0 6.6 %all-to-all-start.5 = ((bf16[8,16,16,128]{3,2,1,0:T(8,128)(2,1)}), bf16[8,16,16,128]{3,2,1,0:T(8,128)(2,1)S(1)}, u32[]{:S(2)}, u32[]{:S(2)}) async-start(bf16[8,16,16,128]{3,2,1,0:T(8,128)(2,1)} %broadcast_in_dim.36), calls=%async_computation.5 | async-start | bytes 1048576 | tf_op jit(solution)/shard_map/all_to_all | solution.py:58
  140.7 2.2 %collective-permute-start.1 = (f32[32,1024]{1,0:T(8,128)S(1)}, f32[32,1024]{1,0:T(8,128)S(1)}, u32[]{:S(2)}, u32[]{:S(2)}) collective-permute-start(f32[32,1024]{1,0:T(8,128)S(1)} %dynamic-slice_bitcast_fusion), channel_id=1, source_target_pairs={{0,1},{1,0},{2,3},{3,2},{4,5},{5,4},{6,7},{7,6},{8,9},{9,8},{10,11... | collective-permute-start | bytes 393224 | tf_op jit(solution)/shard_map/ppermute | solution.py:148
  142.9 4.6 %collective-permute-done.1 = f32[32,1024]{1,0:T(8,128)S(1)} collective-permute-done((f32[32,1024]{1,0:T(8,128)S(1)}, f32[32,1024]{1,0:T(8,128)S(1)}, u32[]{:S(2)}, u32[]{:S(2)}) %collective-permute-start.1) | collective-permute-done | bytes 131104 | tf_op jit(solution)/shard_map/ppermute | solution.py:148
  147.5 0.6 fusion.46
  148.2 2.0 %all-to-all-done.5 = bf16[8,16,16,128]{3,2,1,0:T(8,128)(2,1)S(1)} async-done(((bf16[8,16,16,128]{3,2,1,0:T(8,128)(2,1)}), bf16[8,16,16,128]{3,2,1,0:T(8,128)(2,1)S(1)}, u32[]{:S(2)}, u32[]{:S(2)}) %all-to-all-start.5) | async-done | bytes 524320 | tf_op jit(solution)/shard_map/all_to_all | solution.py:58
  150.2 0.8 slice.35
  (28 shorter events, 0.2 us)
Async XLA Ops:
  0.6 4.1 %copy-start = (bf16[27,64,128]{2,1,0:T(8,128)(2,1)S(1)}, bf16[27,64,128]{2,1,0:T(8,128)(2,1)}, u32[]{:S(2)}) copy-start(bf16[27,64,128]{2,1,0:T(8,128)(2,1)} %param.10) | copy-start | bytes 1327108
  0.6 4.8 %copy-start.6 = (s32[4096]{0:T(1024)S(1)}, s32[4096]{0:T(1024)}, u32[]{:S(2)}) copy-start(s32[4096]{0:T(1024)} %param.12) | copy-start | bytes 49156
  0.7 4.8 %copy-start.3 = (bf16[1024,128]{1,0:T(8,128)(2,1)S(1)}, bf16[1024,128]{1,0:T(8,128)(2,1)}, u32[]{:S(2)}) copy-start(bf16[1024,128]{1,0:T(8,128)(2,1)} %param.9) | copy-start | bytes 786436
  8.5 1.0 copy-start.5
  9.5 39.3 %copy-start.7 = (s32[768]{0:T(1024)S(1)}, s32[768]{0:T(1024)}, u32[]{:S(2)}) copy-start(s32[768]{0:T(1024)} %param.16) | copy-start | bytes 9220
  11.1 38.9 %copy-start.4 = (bf16[64,512]{1,0:T(8,128)(2,1)S(1)}, bf16[64,512]{1,0:T(8,128)(2,1)}, u32[]{:S(2)}) copy-start(bf16[64,512]{1,0:T(8,128)(2,1)} %param.11) | copy-start | bytes 196612
  51.5 22.9 %all-to-all-start.1 = ((bf16[128,3,128]{2,1,0:T(4,128)(2,1)}), bf16[128,3,128]{2,1,0:T(4,128)(2,1)S(1)}, u32[]{:S(2)}, u32[]{:S(2)}) async-start(bf16[128,3,128]{2,1,0:T(4,128)(2,1)} %all_to_all.26), calls=%async_computation.1 | async-start | bytes 262144 | tf_op jit(solution)/shard_map/all_to_all | solution.py:33
  76.7 0.8 copy-start.1
  77.9 1.6 %copy-start.2 = (s32[32]{0:T(128)S(1)}, s32[32]{0:T(128)}, u32[]{:S(2)}) copy-start(s32[32]{0:T(128)} %param.14) | copy-start | bytes 388
  81.8 14.3 %all-to-all-start.2 = ((bf16[8,16,16,128]{3,2,1,0:T(8,128)(2,1)}), bf16[8,16,16,128]{3,2,1,0:T(8,128)(2,1)S(1)}, u32[]{:S(2)}, u32[]{:S(2)}) async-start(bf16[8,16,16,128]{3,2,1,0:T(8,128)(2,1)} %bitcast.80), calls=%async_computation.2 | async-start | bytes 1048576 | tf_op jit(solution)/shard_map/all_to_all | solution.py:51
  96.7 15.7 %all-to-all-start.3 = ((f32[16,16,128]{2,1,0:T(8,128)}), f32[16,16,128]{2,1,0:T(8,128)S(1)}, u32[]{:S(2)}, u32[]{:S(2)}) async-start(f32[16,16,128]{2,1,0:T(8,128)} %convert_reduce_fusion), calls=%async_computation.3 | async-start | bytes 262144 | tf_op jit(solution)/shard_map/all_to_all | solution.py:53
  104.8 16.8 %collective-permute-start = (f32[2,32,1024]{2,1,0:T(8,128)S(1)}, f32[2,32,1024]{2,1,0:T(8,128)S(1)}, u32[]{:S(2)}, u32[]{:S(2)}) collective-permute-start(f32[2,32,1024]{2,1,0:T(8,128)S(1)} %constant_dynamic-slice_fusion), channel_id=1, source_target_pairs={{0,2},{1,3},{2,0},{3,1},{4,6},{5,7},{6,4},{7,5},{8,10},{9,11},{10,... | collective-permute-start | bytes 786440 | tf_op jit(solution)/shard_map/ppermute | solution.py:145
  113.1 20.1 %all-to-all-start.4 = ((bf16[16,16,128]{2,1,0:T(8,128)(2,1)}), bf16[16,16,128]{2,1,0:T(8,128)(2,1)S(1)}, u32[]{:S(2)}, u32[]{:S(2)}) async-start(bf16[16,16,128]{2,1,0:T(8,128)(2,1)} %broadcast_in_dim.35), calls=%async_computation.4 | async-start | bytes 131072 | tf_op jit(solution)/shard_map/all_to_all | solution.py:56
  134.0 16.1 %all-to-all-start.5 = ((bf16[8,16,16,128]{3,2,1,0:T(8,128)(2,1)}), bf16[8,16,16,128]{3,2,1,0:T(8,128)(2,1)S(1)}, u32[]{:S(2)}, u32[]{:S(2)}) async-start(bf16[8,16,16,128]{3,2,1,0:T(8,128)(2,1)} %broadcast_in_dim.36), calls=%async_computation.5 | async-start | bytes 1048576 | tf_op jit(solution)/shard_map/all_to_all | solution.py:58
  140.7 6.9 %collective-permute-start.1 = (f32[32,1024]{1,0:T(8,128)S(1)}, f32[32,1024]{1,0:T(8,128)S(1)}, u32[]{:S(2)}, u32[]{:S(2)}) collective-permute-start(f32[32,1024]{1,0:T(8,128)S(1)} %dynamic-slice_bitcast_fusion), channel_id=1, source_target_pairs={{0,1},{1,0},{2,3},{3,2},{4,5},{5,4},{6,7},{7,6},{8,9},{9,8},{10,11... | collective-permute-start | bytes 393224 | tf_op jit(solution)/shard_map/ppermute | solution.py:148

commit v14 on v13

--- a/solution.py
+++ b/solution.py
@@ -131,10 +131,12 @@
     rows_all = offsets_all * width_out
     step = owners * 8
     padded = -(-rows_all // step) * step // width_out
-    offset_hot = one_hot(block_offset, padded).astype(jnp.float32)
-    weight_sum = jnp.einsum(
-        "bk,boc->koc", offset_hot, grad_weight, precision=lax.Precision.HIGHEST
-    )
+    offset_hot = (
+        jnp.arange(padded, dtype=jnp.int32)[:, None] == block_offset[None, :]
+    ).astype(jnp.float32)
+    weight_sum = jnp.dot(
+        offset_hot, grad_weight.reshape(blocks, -1), precision=lax.Precision.HIGHEST
+    ).reshape(padded, width_out, width_in)
     groups = lax.axis_size("ch")
     fine_parts = fine_sum.reshape(groups, width_in // groups, fine_total)
     me = lax.axis_index("ch")

time: 152 us -> 152 us (level)
  no operation moved by 1% of the time
where the time goes in v14:
time: 152 us; the launch traced here: 151 us
  waiting for transfers between devices  45 us (30%)
  starting transfers between devices  37.3 us (25%)
  blocking collectives  36.8 us (24%)
  matrix products  17.1 us (11%)
  local copies, waits for them, and re-layouts  7.31 us (5%)
  other arithmetic  5.84 us (4%)
  between operations  1.66 us (1%)
    all_to_all x1, blocking collectives, flat_all_to_all(): return lax.all_to_all(x, VOX, 0, 0, tiled=True)  36.8 us
    all_to_all x1, waiting for transfers between devices, flat_all_to_all(): return lax.all_to_all(x, VOX, 0, 0, tiled=True)  16 us
    all_to_all x1, waiting for transfers between devices, reduce_replicate(): mine = lax.all_to_all(mine, VOX[0], 0, 0, tiled=True)  11.5 us
    all_to_all x1, starting transfers between devices, reduce_replicate(): mine = lax.all_to_all(mine, VOX[0], 0, 0, tiled=True)  8.5 us
    all_to_all x1, waiting for transfers between devices, reduce_replicate(): part = lax.all_to_all(part.astype(jnp.bfloat16), VOX[1:], 0, 0, tiled=True)  7.81 us
    all_to_all x1, starting transfers between devices, flat_all_to_all(): return lax.all_to_all(x, VOX, 0, 0, tiled=True)  6.85 us
    all_to_all x1, starting transfers between devices, reduce_replicate(): mine = lax.all_to_all(mine, VOX[1:], 0, 0, tiled=True)  6.63 us
    all_to_all x1, starting transfers between devices, reduce_replicate(): part = lax.all_to_all(part.astype(jnp.bfloat16), VOX[1:], 0, 0, tiled=True)  4.77 us
  transfers between devices with their start and end apart: 7, of which 6 were waited for; matrix products, arithmetic and copies ran while one was open for 5% of the time, Pallas kernels for 0%

profile of v14, /device:TPU:1, one launch (start us, length us, event | category | flops | bytes accessed | tf_op | source)
XLA Modules:
  0.0 151.0 jit_solution(13856919897281316151)
XLA Ops:
  0.6 0.0 copy-start
  1.4 0.7 compare_select_fusion
  2.1 0.8 copy.22
  2.8 0.2 fusion.42
  3.2 0.9 fusion.40
  4.1 0.7 multiply_add_fusion
  4.8 0.6 gather_fusion
  5.4 3.1 %fusion.6 = bf16[4096,128]{1,0:T(8,128)(2,1)S(1)} fusion(s32[4096]{0:T(1024)S(1)} %copy-done.6, bf16[1024,128]{1,0:T(8,128)(2,1)S(1)} %copy-done.3, pred[1024]{0:T(1024)(128)(4,1)S(1)} %iota_compare_fusion.31), kind=kOutput, calls=%fused_computation.10 | convolution fusion | flops 1078591488 | bytes 1328128 | tf_op jit(solution)/shard_map/dot_general | solution.py:89
  8.5 0.8 convolution_bitcast_fusion
  9.4 0.2 reduce-precision_convert_fusion.1
  9.5 1.5 fusion.5
  11.1 0.5 fusion.20
  11.5 0.2 copy.25
  11.7 0.2 all_to_all.24
  11.9 36.8 %all_to_all.38 = bf16[128,3,128]{2,1,0:T(4,128)(2,1)S(1)} all-to-all(bf16[128,3,128]{2,1,0:T(4,128)(2,1)S(1)} %all_to_all.24), channel_id=1, replica_groups=mesh['z'=16,'y'=4,'core'=2,'ch'=4] {'z','y','core'}, dimensions={0} | all-to-all | bytes 196608 | tf_op jit(solution)/shard_map/all_to_all | solution.py:33
  48.7 0.1 reshape.84
  48.8 1.2 fusion.55
  50.0 0.5 fusion.19
  50.5 0.2 copy.26
  50.7 0.8 all_to_all.26
  51.5 6.8 %all-to-all-start.1 = ((bf16[128,3,128]{2,1,0:T(4,128)(2,1)}), bf16[128,3,128]{2,1,0:T(4,128)(2,1)S(1)}, u32[]{:S(2)}, u32[]{:S(2)}) async-start(bf16[128,3,128]{2,1,0:T(4,128)(2,1)} %all_to_all.26), calls=%async_computation.1 | async-start | bytes 262144 | tf_op jit(solution)/shard_map/all_to_all | solution.py:33
  58.4 16.0 %all-to-all-done.1 = bf16[128,3,128]{2,1,0:T(4,128)(2,1)S(1)} async-done(((bf16[128,3,128]{2,1,0:T(4,128)(2,1)}), bf16[128,3,128]{2,1,0:T(4,128)(2,1)S(1)}, u32[]{:S(2)}, u32[]{:S(2)}) %all-to-all-start.1) | async-done | bytes 98336 | tf_op jit(solution)/shard_map/all_to_all | solution.py:33
  74.4 0.1 reshape.85
  74.5 2.1 %fusion.18 = bf16[8,32,8,128]{3,2,1,0:T(8,128)(2,1)S(1)} fusion(s32[4096]{0:T(1024)S(1)} %copy-done.5, bf16[768,64]{1,0:T(8,128)(2,1)S(1)} %reshape.85, s32[512]{0:T(512)S(1)} %bitcast.90), kind=kOutput, calls=%fused_computation.29 | convolution fusion | flops 321552384 | bytes 641024 | tf_op jit(solution)/shard_map/pt,to->po/dot_general | solution.py:120
  76.7 0.8 copy-done.1
  77.5 0.4 fusion.33
  77.9 1.5 %fusion.35 = f32[32,128,128]{2,1,0:T(8,128)S(1)} fusion(bf16[32,64,128]{2,1,0:T(8,128)(2,1)S(1)} %gather_fusion, bf16[8,32,8,128]{3,2,1,0:T(8,128)(2,1)} %copy-done.1), kind=kOutput, calls=%fused_computation.46 | convolution fusion | flops 67108864 | bytes 3145728 | tf_op jit(solution)/shard_map/bpo,boc->bpc/dot_general | solution.py:124
  79.4 1.3 convolution_convert_fusion
  80.7 1.1 convert_element_type.85
  81.8 4.8 %all-to-all-start.2 = ((bf16[8,16,16,128]{3,2,1,0:T(8,128)(2,1)}), bf16[8,16,16,128]{3,2,1,0:T(8,128)(2,1)S(1)}, u32[]{:S(2)}, u32[]{:S(2)}) async-start(bf16[8,16,16,128]{3,2,1,0:T(8,128)(2,1)} %convert_element_type.85), calls=%async_computation.2 | async-start | bytes 1048576 | tf_op jit(solution)/shard_map/all_to_all | solution.py:51
  86.6 1.7 %reduce-precision_convert_fusion = (bf16[4096,128]{1,0:T(8,128)(2,1)}, bf16[4096,128]{1,0:T(8,128)(2,1)}) fusion(f32[32,128,128]{2,1,0:T(8,128)S(1)} %fusion.35), kind=kLoop, calls=%fused_computation.15 | loop fusion | flops 2097152 | bytes 4194304 | tf_op jit(solution)/shard_map/convert_element_type | solution.py:39
  88.2 7.8 %all-to-all-done.2 = bf16[8,16,16,128]{3,2,1,0:T(8,128)(2,1)S(1)} async-done(((bf16[8,16,16,128]{3,2,1,0:T(8,128)(2,1)}), bf16[8,16,16,128]{3,2,1,0:T(8,128)(2,1)S(1)}, u32[]{:S(2)}, u32[]{:S(2)}) %all-to-all-start.2) | async-done | bytes 524320 | tf_op jit(solution)/shard_map/all_to_all | solution.py:51
  96.0 0.7 convert_reduce_fusion
  96.8 3.7 %all-to-all-start.3 = ((f32[16,16,128]{2,1,0:T(8,128)}), f32[16,16,128]{2,1,0:T(8,128)S(1)}, u32[]{:S(2)}, u32[]{:S(2)}) async-start(f32[16,16,128]{2,1,0:T(8,128)} %convert_reduce_fusion), calls=%async_computation.3 | async-start | bytes 262144 | tf_op jit(solution)/shard_map/all_to_all | solution.py:53
  100.5 4.2 %fusion = f32[256,1024]{1,0:T(8,128)S(1)} fusion(s32[4096]{0:T(1024)S(1)} %copy-done.6, bf16[4096,128]{1,0:T(8,128)(2,1)} %get-tuple-element.4, bf16[4096,128]{1,0:T(8,128)(2,1)} %get-tuple-element.3), kind=kOutput, calls=%fused_computation.2 | convolution fusion | flops 2155872256 | bytes 3162112 | tf_op jit(solution)/shard_map/pc,pt->ct/dot_general | solution.py:40
  104.7 0.1 slice_add_fusion
  104.8 4.6 %collective-permute-start = (f32[2,32,1024]{2,1,0:T(8,128)S(1)}, f32[2,32,1024]{2,1,0:T(8,128)S(1)}, u32[]{:S(2)}, u32[]{:S(2)}) collective-permute-start(f32[2,32,1024]{2,1,0:T(8,128)S(1)} %constant_dynamic-slice_fusion), channel_id=1, source_target_pairs={{0,2},{1,3},{2,0},{3,1},{4,6},{5,7},{6,4},{7,5},{8,10},{9,11},{10,... | collective-permute-start | bytes 786440 | tf_op jit(solution)/shard_map/ppermute | solution.py:147
  109.5 3.0 %all-to-all-done.3 = f32[16,16,128]{2,1,0:T(8,128)S(1)} async-done(((f32[16,16,128]{2,1,0:T(8,128)}), f32[16,16,128]{2,1,0:T(8,128)S(1)}, u32[]{:S(2)}, u32[]{:S(2)}) %all-to-all-start.3) | async-done | bytes 131104 | tf_op jit(solution)/shard_map/all_to_all | solution.py:53
  112.5 0.6 broadcast_in_dim.35
  113.1 8.5 %all-to-all-start.4 = ((bf16[16,16,128]{2,1,0:T(8,128)(2,1)}), bf16[16,16,128]{2,1,0:T(8,128)(2,1)S(1)}, u32[]{:S(2)}, u32[]{:S(2)}) async-start(bf16[16,16,128]{2,1,0:T(8,128)(2,1)} %broadcast_in_dim.35), calls=%async_computation.4 | async-start | bytes 131072 | tf_op jit(solution)/shard_map/all_to_all | solution.py:56
  121.7 11.5 %all-to-all-done.4 = bf16[16,16,128]{2,1,0:T(8,128)(2,1)S(1)} async-done(((bf16[16,16,128]{2,1,0:T(8,128)(2,1)}), bf16[16,16,128]{2,1,0:T(8,128)(2,1)S(1)}, u32[]{:S(2)}, u32[]{:S(2)}) %all-to-all-start.4) | async-done | bytes 65568 | tf_op jit(solution)/shard_map/all_to_all | solution.py:56
  133.2 0.9 broadcast_in_dim.36
  134.1 6.6 %all-to-all-start.5 = ((bf16[8,16,16,128]{3,2,1,0:T(8,128)(2,1)}), bf16[8,16,16,128]{3,2,1,0:T(8,128)(2,1)S(1)}, u32[]{:S(2)}, u32[]{:S(2)}) async-start(bf16[8,16,16,128]{3,2,1,0:T(8,128)(2,1)} %broadcast_in_dim.36), calls=%async_computation.5 | async-start | bytes 1048576 | tf_op jit(solution)/shard_map/all_to_all | solution.py:58
  140.7 2.2 %collective-permute-start.1 = (f32[32,1024]{1,0:T(8,128)S(1)}, f32[32,1024]{1,0:T(8,128)S(1)}, u32[]{:S(2)}, u32[]{:S(2)}) collective-permute-start(f32[32,1024]{1,0:T(8,128)S(1)} %dynamic-slice_bitcast_fusion), channel_id=1, source_target_pairs={{0,1},{1,0},{2,3},{3,2},{4,5},{5,4},{6,7},{7,6},{8,9},{9,8},{10,11... | collective-permute-start | bytes 393224 | tf_op jit(solution)/shard_map/ppermute | solution.py:150
  142.9 4.6 %collective-permute-done.1 = f32[32,1024]{1,0:T(8,128)S(1)} collective-permute-done((f32[32,1024]{1,0:T(8,128)S(1)}, f32[32,1024]{1,0:T(8,128)S(1)}, u32[]{:S(2)}, u32[]{:S(2)}) %collective-permute-start.1) | collective-permute-done | bytes 131104 | tf_op jit(solution)/shard_map/ppermute | solution.py:150
  147.6 0.6 fusion.47
  148.2 2.0 %all-to-all-done.5 = bf16[8,16,16,128]{3,2,1,0:T(8,128)(2,1)S(1)} async-done(((bf16[8,16,16,128]{3,2,1,0:T(8,128)(2,1)}), bf16[8,16,16,128]{3,2,1,0:T(8,128)(2,1)S(1)}, u32[]{:S(2)}, u32[]{:S(2)}) %all-to-all-start.5) | async-done | bytes 524320 | tf_op jit(solution)/shard_map/all_to_all | solution.py:58
  150.2 0.8 slice.35
  (28 shorter events, 0.2 us)
Async XLA Ops:
  0.6 4.1 %copy-start = (bf16[27,64,128]{2,1,0:T(8,128)(2,1)S(1)}, bf16[27,64,128]{2,1,0:T(8,128)(2,1)}, u32[]{:S(2)}) copy-start(bf16[27,64,128]{2,1,0:T(8,128)(2,1)} %param.10) | copy-start | bytes 1327108
  0.6 4.8 %copy-start.6 = (s32[4096]{0:T(1024)S(1)}, s32[4096]{0:T(1024)}, u32[]{:S(2)}) copy-start(s32[4096]{0:T(1024)} %param.12) | copy-start | bytes 49156
  0.7 4.8 %copy-start.3 = (bf16[1024,128]{1,0:T(8,128)(2,1)S(1)}, bf16[1024,128]{1,0:T(8,128)(2,1)}, u32[]{:S(2)}) copy-start(bf16[1024,128]{1,0:T(8,128)(2,1)} %param.9) | copy-start | bytes 786436
  8.5 1.0 copy-start.5
  9.5 39.3 %copy-start.7 = (s32[768]{0:T(1024)S(1)}, s32[768]{0:T(1024)}, u32[]{:S(2)}) copy-start(s32[768]{0:T(1024)} %param.16) | copy-start | bytes 9220
  11.1 38.9 %copy-start.4 = (bf16[64,512]{1,0:T(8,128)(2,1)S(1)}, bf16[64,512]{1,0:T(8,128)(2,1)}, u32[]{:S(2)}) copy-start(bf16[64,512]{1,0:T(8,128)(2,1)} %param.11) | copy-start | bytes 196612
  51.5 22.9 %all-to-all-start.1 = ((bf16[128,3,128]{2,1,0:T(4,128)(2,1)}), bf16[128,3,128]{2,1,0:T(4,128)(2,1)S(1)}, u32[]{:S(2)}, u32[]{:S(2)}) async-start(bf16[128,3,128]{2,1,0:T(4,128)(2,1)} %all_to_all.26), calls=%async_computation.1 | async-start | bytes 262144 | tf_op jit(solution)/shard_map/all_to_all | solution.py:33
  76.7 0.8 copy-start.1
  77.9 1.6 %copy-start.2 = (s32[32]{0:T(128)S(1)}, s32[32]{0:T(128)}, u32[]{:S(2)}) copy-start(s32[32]{0:T(128)} %param.14) | copy-start | bytes 388
  81.8 14.3 %all-to-all-start.2 = ((bf16[8,16,16,128]{3,2,1,0:T(8,128)(2,1)}), bf16[8,16,16,128]{3,2,1,0:T(8,128)(2,1)S(1)}, u32[]{:S(2)}, u32[]{:S(2)}) async-start(bf16[8,16,16,128]{3,2,1,0:T(8,128)(2,1)} %convert_element_type.85), calls=%async_computation.2 | async-start | bytes 1048576 | tf_op jit(solution)/shard_map/all_to_all | solution.py:51
  96.8 15.7 %all-to-all-start.3 = ((f32[16,16,128]{2,1,0:T(8,128)}), f32[16,16,128]{2,1,0:T(8,128)S(1)}, u32[]{:S(2)}, u32[]{:S(2)}) async-start(f32[16,16,128]{2,1,0:T(8,128)} %convert_reduce_fusion), calls=%async_computation.3 | async-start | bytes 262144 | tf_op jit(solution)/shard_map/all_to_all | solution.py:53
  104.8 16.8 %collective-permute-start = (f32[2,32,1024]{2,1,0:T(8,128)S(1)}, f32[2,32,1024]{2,1,0:T(8,128)S(1)}, u32[]{:S(2)}, u32[]{:S(2)}) collective-permute-start(f32[2,32,1024]{2,1,0:T(8,128)S(1)} %constant_dynamic-slice_fusion), channel_id=1, source_target_pairs={{0,2},{1,3},{2,0},{3,1},{4,6},{5,7},{6,4},{7,5},{8,10},{9,11},{10,... | collective-permute-start | bytes 786440 | tf_op jit(solution)/shard_map/ppermute | solution.py:147
  113.1 20.1 %all-to-all-start.4 = ((bf16[16,16,128]{2,1,0:T(8,128)(2,1)}), bf16[16,16,128]{2,1,0:T(8,128)(2,1)S(1)}, u32[]{:S(2)}, u32[]{:S(2)}) async-start(bf16[16,16,128]{2,1,0:T(8,128)(2,1)} %broadcast_in_dim.35), calls=%async_computation.4 | async-start | bytes 131072 | tf_op jit(solution)/shard_map/all_to_all | solution.py:56
  134.1 16.1 %all-to-all-start.5 = ((bf16[8,16,16,128]{3,2,1,0:T(8,128)(2,1)}), bf16[8,16,16,128]{3,2,1,0:T(8,128)(2,1)S(1)}, u32[]{:S(2)}, u32[]{:S(2)}) async-start(bf16[8,16,16,128]{3,2,1,0:T(8,128)(2,1)} %broadcast_in_dim.36), calls=%async_computation.5 | async-start | bytes 1048576 | tf_op jit(solution)/shard_map/all_to_all | solution.py:58
  140.7 6.9 %collective-permute-start.1 = (f32[32,1024]{1,0:T(8,128)S(1)}, f32[32,1024]{1,0:T(8,128)S(1)}, u32[]{:S(2)}, u32[]{:S(2)}) collective-permute-start(f32[32,1024]{1,0:T(8,128)S(1)} %dynamic-slice_bitcast_fusion), channel_id=1, source_target_pairs={{0,1},{1,0},{2,3},{3,2},{4,5},{5,4},{6,7},{7,6},{8,9},{9,8},{10,11... | collective-permute-start | bytes 393224 | tf_op jit(solution)/shard_map/ppermute | solution.py:150

commit v15 on v14

--- a/solution.py
+++ b/solution.py
@@ -8,9 +8,11 @@
 
 def owner_slots(owner_of, owners):
     labels = jnp.arange(owners, dtype=jnp.int32)
-    onehot = (owner_of[:, None] == labels[None, :]).astype(jnp.int32)
-    before = jnp.cumsum(onehot, axis=0) - onehot
-    return jnp.sum(before * onehot, axis=1)
+    onehot = (owner_of[:, None] == labels[None, :]).astype(jnp.bfloat16)
+    rows = jnp.arange(owner_of.shape[0], dtype=jnp.int32)
+    earlier = (rows[None, :] < rows[:, None]).astype(jnp.bfloat16)
+    before = jnp.dot(earlier, onehot, preferred_element_type=jnp.float32)
+    return jnp.sum(before * onehot.astype(jnp.float32), axis=1).astype(jnp.int32)
 
 
 def one_hot(index, size):

time: 152 us -> 152 us (level)
  matrix products: 17.1 us -> 19.1 us
where the time goes in v15:
time: 152 us; the launch traced here: 151 us
  waiting for transfers between devices  45 us (30%)
  starting transfers between devices  37.3 us (25%)
  blocking collectives  36.8 us (24%)
  matrix products  19.1 us (13%)
  local copies, waits for them, and re-layouts  6.46 us (4%)
  other arithmetic  4.66 us (3%)
  between operations  1.62 us (1%)
    all_to_all x1, blocking collectives, flat_all_to_all(): return lax.all_to_all(x, VOX, 0, 0, tiled=True)  36.8 us
    all_to_all x1, waiting for transfers between devices, flat_all_to_all(): return lax.all_to_all(x, VOX, 0, 0, tiled=True)  16 us
    all_to_all x1, waiting for transfers between devices, reduce_replicate(): mine = lax.all_to_all(mine, VOX[0], 0, 0, tiled=True)  11.5 us
    all_to_all x1, starting transfers between devices, reduce_replicate(): mine = lax.all_to_all(mine, VOX[0], 0, 0, tiled=True)  8.52 us
    all_to_all x1, waiting for transfers between devices, reduce_replicate(): part = lax.all_to_all(part.astype(jnp.bfloat16), VOX[1:], 0, 0, tiled=True)  7.83 us
    all_to_all x1, starting transfers between devices, flat_all_to_all(): return lax.all_to_all(x, VOX, 0, 0, tiled=True)  6.85 us
    all_to_all x1, starting transfers between devices, reduce_replicate(): mine = lax.all_to_all(mine, VOX[1:], 0, 0, tiled=True)  6.63 us
    all_to_all x1, starting transfers between devices, reduce_replicate(): part = lax.all_to_all(part.astype(jnp.bfloat16), VOX[1:], 0, 0, tiled=True)  4.78 us
  transfers between devices with their start and end apart: 7, of which 6 were waited for; matrix products, arithmetic and copies ran while one was open for 5% of the time, Pallas kernels for 0%

profile of v15, /device:TPU:1, one launch (start us, length us, event | category | flops | bytes accessed | tf_op | source)
XLA Modules:
  0.0 150.9 jit_solution(17805173261234845371)
XLA Ops:
  0.6 0.0 copy-start
  1.4 0.7 compare_select_fusion
  2.0 1.1 fusion.21
  3.1 0.7 multiply_add_fusion
  3.8 0.6 gather_fusion
  4.5 4.1 %fusion.6 = bf16[4096,128]{1,0:T(8,128)(2,1)S(1)} fusion(s32[4096]{0:T(1024)} %param.12, bf16[1024,128]{1,0:T(8,128)(2,1)} %param.9, pred[1024]{0:T(1024)(128)(4,1)S(1)} %iota_compare_fusion.32), kind=kOutput, calls=%fused_computation.10 | convolution fusion | flops 1078591488 | bytes 1328128 | tf_op jit(solution)/shard_map/dot_general | solution.py:91
  8.5 0.0 copy-start.4
  8.5 0.8 convolution_bitcast_fusion
  9.3 0.2 reduce-precision_convert_fusion.1
  9.5 0.0 copy-start.6
  9.5 1.5 fusion.5
  11.1 0.5 fusion.20
  11.5 0.2 copy.20
  11.7 0.2 all_to_all.24
  11.9 36.8 %all_to_all.38 = bf16[128,3,128]{2,1,0:T(4,128)(2,1)S(1)} all-to-all(bf16[128,3,128]{2,1,0:T(4,128)(2,1)S(1)} %all_to_all.24), channel_id=1, replica_groups=mesh['z'=16,'y'=4,'core'=2,'ch'=4] {'z','y','core'}, dimensions={0} | all-to-all | bytes 196608 | tf_op jit(solution)/shard_map/all_to_all | solution.py:35
  48.6 0.1 reshape.74
  48.8 1.2 fusion.53
  50.0 0.5 fusion.19
  50.5 0.2 copy.21
  50.6 0.8 all_to_all.26
  51.5 6.8 %all-to-all-start.1 = ((bf16[128,3,128]{2,1,0:T(4,128)(2,1)}), bf16[128,3,128]{2,1,0:T(4,128)(2,1)S(1)}, u32[]{:S(2)}, u32[]{:S(2)}) async-start(bf16[128,3,128]{2,1,0:T(4,128)(2,1)} %all_to_all.26), calls=%async_computation.1 | async-start | bytes 262144 | tf_op jit(solution)/shard_map/all_to_all | solution.py:35
  58.3 16.0 %all-to-all-done.1 = bf16[128,3,128]{2,1,0:T(4,128)(2,1)S(1)} async-done(((bf16[128,3,128]{2,1,0:T(4,128)(2,1)}), bf16[128,3,128]{2,1,0:T(4,128)(2,1)S(1)}, u32[]{:S(2)}, u32[]{:S(2)}) %all-to-all-start.1) | async-done | bytes 98336 | tf_op jit(solution)/shard_map/all_to_all | solution.py:35
  74.4 0.1 reshape.75
  74.5 2.1 %fusion.18 = bf16[8,32,8,128]{3,2,1,0:T(8,128)(2,1)S(1)} fusion(s32[4096]{0:T(1024)S(1)} %copy-done.4, bf16[768,64]{1,0:T(8,128)(2,1)S(1)} %reshape.75, s32[512]{0:T(512)S(1)} %bitcast.72), kind=kOutput, calls=%fused_computation.29 | convolution fusion | flops 321552384 | bytes 641024 | tf_op jit(solution)/shard_map/pt,to->po/dot_general | solution.py:122
  76.7 0.8 copy-done.1
  77.5 0.4 fusion.34
  77.9 1.5 %fusion.36 = f32[32,128,128]{2,1,0:T(8,128)S(1)} fusion(bf16[32,64,128]{2,1,0:T(8,128)(2,1)S(1)} %gather_fusion, bf16[8,32,8,128]{3,2,1,0:T(8,128)(2,1)} %copy-done.1), kind=kOutput, calls=%fused_computation.49 | convolution fusion | flops 67108864 | bytes 3145728 | tf_op jit(solution)/shard_map/bpo,boc->bpc/dot_general | solution.py:126
  79.4 1.3 convolution_convert_fusion
  80.7 1.0 convert_element_type.100
  81.7 4.8 %all-to-all-start.2 = ((bf16[8,16,16,128]{3,2,1,0:T(8,128)(2,1)}), bf16[8,16,16,128]{3,2,1,0:T(8,128)(2,1)S(1)}, u32[]{:S(2)}, u32[]{:S(2)}) async-start(bf16[8,16,16,128]{3,2,1,0:T(8,128)(2,1)} %convert_element_type.100), calls=%async_computation.2 | async-start | bytes 1048576 | tf_op jit(solution)/shard_map/all_to_all | solution.py:53
  86.5 1.7 %reduce-precision_convert_fusion = (bf16[4096,128]{1,0:T(8,128)(2,1)}, bf16[4096,128]{1,0:T(8,128)(2,1)}) fusion(f32[32,128,128]{2,1,0:T(8,128)S(1)} %fusion.36), kind=kLoop, calls=%fused_computation.15 | loop fusion | flops 2097152 | bytes 4194304 | tf_op jit(solution)/shard_map/convert_element_type | solution.py:41
  88.2 7.8 %all-to-all-done.2 = bf16[8,16,16,128]{3,2,1,0:T(8,128)(2,1)S(1)} async-done(((bf16[8,16,16,128]{3,2,1,0:T(8,128)(2,1)}), bf16[8,16,16,128]{3,2,1,0:T(8,128)(2,1)S(1)}, u32[]{:S(2)}, u32[]{:S(2)}) %all-to-all-start.2) | async-done | bytes 524320 | tf_op jit(solution)/shard_map/all_to_all | solution.py:53
  96.0 0.7 convert_reduce_fusion
  96.7 3.7 %all-to-all-start.3 = ((f32[16,16,128]{2,1,0:T(8,128)}), f32[16,16,128]{2,1,0:T(8,128)S(1)}, u32[]{:S(2)}, u32[]{:S(2)}) async-start(f32[16,16,128]{2,1,0:T(8,128)} %convert_reduce_fusion), calls=%async_computation.3 | async-start | bytes 262144 | tf_op jit(solution)/shard_map/all_to_all | solution.py:55
  100.4 4.2 %fusion = f32[256,1024]{1,0:T(8,128)S(1)} fusion(s32[4096]{0:T(1024)S(1)} %copy-done.5, bf16[4096,128]{1,0:T(8,128)(2,1)} %get-tuple-element.4, bf16[4096,128]{1,0:T(8,128)(2,1)} %get-tuple-element.3), kind=kOutput, calls=%fused_computation.2 | convolution fusion | flops 2155872256 | bytes 3162112 | tf_op jit(solution)/shard_map/pc,pt->ct/dot_general | solution.py:42
  104.7 0.1 slice_add_fusion
  104.8 4.7 %collective-permute-start = (f32[2,32,1024]{2,1,0:T(8,128)S(1)}, f32[2,32,1024]{2,1,0:T(8,128)S(1)}, u32[]{:S(2)}, u32[]{:S(2)}) collective-permute-start(f32[2,32,1024]{2,1,0:T(8,128)S(1)} %constant_dynamic-slice_fusion), channel_id=1, source_target_pairs={{0,2},{1,3},{2,0},{3,1},{4,6},{5,7},{6,4},{7,5},{8,10},{9,11},{10,... | collective-permute-start | bytes 786440 | tf_op jit(solution)/shard_map/ppermute | solution.py:149
  109.4 3.0 %all-to-all-done.3 = f32[16,16,128]{2,1,0:T(8,128)S(1)} async-done(((f32[16,16,128]{2,1,0:T(8,128)}), f32[16,16,128]{2,1,0:T(8,128)S(1)}, u32[]{:S(2)}, u32[]{:S(2)}) %all-to-all-start.3) | async-done | bytes 131104 | tf_op jit(solution)/shard_map/all_to_all | solution.py:55
  112.4 0.6 broadcast_in_dim.35
  113.1 8.5 %all-to-all-start.4 = ((bf16[16,16,128]{2,1,0:T(8,128)(2,1)}), bf16[16,16,128]{2,1,0:T(8,128)(2,1)S(1)}, u32[]{:S(2)}, u32[]{:S(2)}) async-start(bf16[16,16,128]{2,1,0:T(8,128)(2,1)} %broadcast_in_dim.35), calls=%async_computation.4 | async-start | bytes 131072 | tf_op jit(solution)/shard_map/all_to_all | solution.py:58
  121.6 11.5 %all-to-all-done.4 = bf16[16,16,128]{2,1,0:T(8,128)(2,1)S(1)} async-done(((bf16[16,16,128]{2,1,0:T(8,128)(2,1)}), bf16[16,16,128]{2,1,0:T(8,128)(2,1)S(1)}, u32[]{:S(2)}, u32[]{:S(2)}) %all-to-all-start.4) | async-done | bytes 65568 | tf_op jit(solution)/shard_map/all_to_all | solution.py:58
  133.2 0.9 broadcast_in_dim.36
  134.0 6.6 %all-to-all-start.5 = ((bf16[8,16,16,128]{3,2,1,0:T(8,128)(2,1)}), bf16[8,16,16,128]{3,2,1,0:T(8,128)(2,1)S(1)}, u32[]{:S(2)}, u32[]{:S(2)}) async-start(bf16[8,16,16,128]{3,2,1,0:T(8,128)(2,1)} %broadcast_in_dim.36), calls=%async_computation.5 | async-start | bytes 1048576 | tf_op jit(solution)/shard_map/all_to_all | solution.py:60
  140.7 2.2 %collective-permute-start.1 = (f32[32,1024]{1,0:T(8,128)S(1)}, f32[32,1024]{1,0:T(8,128)S(1)}, u32[]{:S(2)}, u32[]{:S(2)}) collective-permute-start(f32[32,1024]{1,0:T(8,128)S(1)} %dynamic-slice_bitcast_fusion), channel_id=1, source_target_pairs={{0,1},{1,0},{2,3},{3,2},{4,5},{5,4},{6,7},{7,6},{8,9},{9,8},{10,11... | collective-permute-start | bytes 393224 | tf_op jit(solution)/shard_map/ppermute | solution.py:152
  142.9 4.6 %collective-permute-done.1 = f32[32,1024]{1,0:T(8,128)S(1)} collective-permute-done((f32[32,1024]{1,0:T(8,128)S(1)}, f32[32,1024]{1,0:T(8,128)S(1)}, u32[]{:S(2)}, u32[]{:S(2)}) %collective-permute-start.1) | collective-permute-done | bytes 131104 | tf_op jit(solution)/shard_map/ppermute | solution.py:152
  147.5 0.6 fusion.45
  148.2 2.0 %all-to-all-done.5 = bf16[8,16,16,128]{3,2,1,0:T(8,128)(2,1)S(1)} async-done(((bf16[8,16,16,128]{3,2,1,0:T(8,128)(2,1)}), bf16[8,16,16,128]{3,2,1,0:T(8,128)(2,1)S(1)}, u32[]{:S(2)}, u32[]{:S(2)}) %all-to-all-start.5) | async-done | bytes 524320 | tf_op jit(solution)/shard_map/all_to_all | solution.py:60
  150.2 0.8 slice.26
  (19 shorter events, 0.1 us)
Async XLA Ops:
  0.6 3.2 %copy-start = (bf16[27,64,128]{2,1,0:T(8,128)(2,1)S(1)}, bf16[27,64,128]{2,1,0:T(8,128)(2,1)}, u32[]{:S(2)}) copy-start(bf16[27,64,128]{2,1,0:T(8,128)(2,1)} %param.10) | copy-start | bytes 1327108
  8.5 1.0 copy-start.4
  9.5 39.3 %copy-start.6 = (s32[768]{0:T(1024)S(1)}, s32[768]{0:T(1024)}, u32[]{:S(2)}) copy-start(s32[768]{0:T(1024)} %param.16) | copy-start | bytes 9220
  11.0 38.9 %copy-start.3 = (bf16[64,512]{1,0:T(8,128)(2,1)S(1)}, bf16[64,512]{1,0:T(8,128)(2,1)}, u32[]{:S(2)}) copy-start(bf16[64,512]{1,0:T(8,128)(2,1)} %param.11) | copy-start | bytes 196612
  51.5 22.9 %all-to-all-start.1 = ((bf16[128,3,128]{2,1,0:T(4,128)(2,1)}), bf16[128,3,128]{2,1,0:T(4,128)(2,1)S(1)}, u32[]{:S(2)}, u32[]{:S(2)}) async-start(bf16[128,3,128]{2,1,0:T(4,128)(2,1)} %all_to_all.26), calls=%async_computation.1 | async-start | bytes 262144 | tf_op jit(solution)/shard_map/all_to_all | solution.py:35
  76.7 0.8 copy-start.1
  77.9 1.6 %copy-start.2 = (s32[32]{0:T(128)S(1)}, s32[32]{0:T(128)}, u32[]{:S(2)}) copy-start(s32[32]{0:T(128)} %param.14) | copy-start | bytes 388
  81.7 14.3 %all-to-all-start.2 = ((bf16[8,16,16,128]{3,2,1,0:T(8,128)(2,1)}), bf16[8,16,16,128]{3,2,1,0:T(8,128)(2,1)S(1)}, u32[]{:S(2)}, u32[]{:S(2)}) async-start(bf16[8,16,16,128]{3,2,1,0:T(8,128)(2,1)} %convert_element_type.100), calls=%async_computation.2 | async-start | bytes 1048576 | tf_op jit(solution)/shard_map/all_to_all | solution.py:53
  86.5 13.9 %copy-start.5 = (s32[4096]{0:T(1024)S(1)}, s32[4096]{0:T(1024)}, u32[]{:S(2)}) copy-start(s32[4096]{0:T(1024)} %param.12) | copy-start | bytes 49156
  96.7 15.7 %all-to-all-start.3 = ((f32[16,16,128]{2,1,0:T(8,128)}), f32[16,16,128]{2,1,0:T(8,128)S(1)}, u32[]{:S(2)}, u32[]{:S(2)}) async-start(f32[16,16,128]{2,1,0:T(8,128)} %convert_reduce_fusion), calls=%async_computation.3 | async-start | bytes 262144 | tf_op jit(solution)/shard_map/all_to_all | solution.py:55
  104.8 16.8 %collective-permute-start = (f32[2,32,1024]{2,1,0:T(8,128)S(1)}, f32[2,32,1024]{2,1,0:T(8,128)S(1)}, u32[]{:S(2)}, u32[]{:S(2)}) collective-permute-start(f32[2,32,1024]{2,1,0:T(8,128)S(1)} %constant_dynamic-slice_fusion), channel_id=1, source_target_pairs={{0,2},{1,3},{2,0},{3,1},{4,6},{5,7},{6,4},{7,5},{8,10},{9,11},{10,... | collective-permute-start | bytes 786440 | tf_op jit(solution)/shard_map/ppermute | solution.py:149
  113.1 20.1 %all-to-all-start.4 = ((bf16[16,16,128]{2,1,0:T(8,128)(2,1)}), bf16[16,16,128]{2,1,0:T(8,128)(2,1)S(1)}, u32[]{:S(2)}, u32[]{:S(2)}) async-start(bf16[16,16,128]{2,1,0:T(8,128)(2,1)} %broadcast_in_dim.35), calls=%async_computation.4 | async-start | bytes 131072 | tf_op jit(solution)/shard_map/all_to_all | solution.py:58
  134.0 16.1 %all-to-all-start.5 = ((bf16[8,16,16,128]{3,2,1,0:T(8,128)(2,1)}), bf16[8,16,16,128]{3,2,1,0:T(8,128)(2,1)S(1)}, u32[]{:S(2)}, u32[]{:S(2)}) async-start(bf16[8,16,16,128]{3,2,1,0:T(8,128)(2,1)} %broadcast_in_dim.36), calls=%async_computation.5 | async-start | bytes 1048576 | tf_op jit(solution)/shard_map/all_to_all | solution.py:60
  140.7 6.9 %collective-permute-start.1 = (f32[32,1024]{1,0:T(8,128)S(1)}, f32[32,1024]{1,0:T(8,128)S(1)}, u32[]{:S(2)}, u32[]{:S(2)}) collective-permute-start(f32[32,1024]{1,0:T(8,128)S(1)} %dynamic-slice_bitcast_fusion), channel_id=1, source_target_pairs={{0,1},{1,0},{2,3},{3,2},{4,5},{5,4},{6,7},{7,6},{8,9},{9,8},{10,11... | collective-permute-start | bytes 393224 | tf_op jit(solution)/shard_map/ppermute | solution.py:152
